TPU v7x, 128 devices: a whole 4x4x4 slice. The times are simulated.
128 devices in a mesh: rows: 32 (over x, z, core), cols: 4 (over y).
Axes of the slice: x: 4, y: 4, z: 4, core: 2. Of those that a mesh axis runs over, the one named last changes fastest.
Arguments:
- land_jac: float32 [16, 3, 262144], P(None, None, ('rows', 'cols')), may hold values from -6 to 6, as said below
- pose_jac: float32 [16, 6, 262144], P(None, None, ('rows', 'cols')), may hold values from -2 to 2
- segment: int32 [8, 262144], P(None, ('rows', 'cols')), may hold values from 0 to 4
- knot_frac: float32 [8, 262144], P(None, ('rows', 'cols')), may hold values from 0 to 1
- track_len: int32 [262144], P(('rows', 'cols')), may hold values from 2 to 8
- block_base: int32 [2048], P(('rows', 'cols')), may hold values from 0 to 504, as said below
- damping: float32 [3072], P('cols'), may hold values from 0.15 to 1.5
Outputs:
- factors: float32 [3072, 768], P('cols')
Inputs may be any that keep to these rules, and one draw needn't show every extreme that they name: `land_jac`: observation j's rows 2j and 2j+1 are s [1, 0, a] and s [0, 1, b] with s positive; a is below -0.5 at observation 0 and above 0.5 at observation 1. A block's window of 8 knots lies inside one group: block_base mod 128 is at most 120.
All inputs are finite; a program needn't handle non-finite values.
Results may differ from a plain program's by a relative error of at most 0.0003.
Values sent between devices are 32-bit elements; how exact they have to be, the bound alone decides.
No kernel may reach another device: no remote copies, remote signals or barrier semaphores. Data moves between devices by JAX's collectives and lax.ppermute only.
A program may use at most 320 MiB of HBM per device.

v0:
```python
import jax
import jax.numpy as jnp
from jax import lax
from jax.sharding import PartitionSpec as P

KDOF = 6
WIN_KNOTS = 8


def basis_weights(knot_frac):
    u_square = knot_frac * knot_frac
    u_cubed = u_square * knot_frac
    return (
        (1.0 - knot_frac) ** 3 / 6.0,
        (3.0 * u_cubed - 6.0 * u_square + 4.0) / 6.0,
        (-3.0 * u_cubed + 3.0 * u_square + 3.0 * knot_frac + 1.0) / 6.0,
        u_cubed / 6.0,
    )


def reduce_rows(land_jac, pose_jac, segment, knot_frac, track_len):
    num_obs = segment.shape[0]
    landmarks = segment.shape[1]
    observed = (
        lax.broadcasted_iota(jnp.int32, (num_obs, landmarks), 0) < track_len[None, :]
    ).astype(jnp.float32)
    row_mask = jnp.repeat(observed, 2, axis=0)
    landmark = land_jac * row_mask[:, None, :]
    pose_rows = (pose_jac * row_mask[:, None, :]).reshape(num_obs, 2, 1, KDOF, landmarks)
    weights = basis_weights(knot_frac)
    knot_index = lax.broadcasted_iota(jnp.int32, (1, WIN_KNOTS, 1), 1)
    knot_weight = jnp.zeros((num_obs, WIN_KNOTS, landmarks), jnp.float32)
    for k in range(4):
        knot_weight = knot_weight + weights[k][:, None, :] * (
            segment[:, None, :] + k == knot_index
        ).astype(jnp.float32)
    knot_jac = (knot_weight[:, None, :, None, :] * pose_rows).reshape(
        2 * num_obs, WIN_KNOTS * KDOF, landmarks
    )
    for k in range(3):
        column = landmark[k:, k, :]
        length = jnp.sqrt(jnp.sum(column * column, axis=0))
        signum = jnp.where(column[0] >= 0.0, 1.0, -1.0)
        leading = column[0] + signum * length
        vector = jnp.concatenate([leading[None, :], column[1:]], axis=0)
        reflect_scale = 2.0 / jnp.sum(vector * vector, axis=0)

        def reflect(matrix):
            lower_rows = matrix[k:]
            projection = jnp.sum(vector[:, None, :] * lower_rows, axis=0)
            updated = lower_rows - (reflect_scale * vector)[:, None, :] * projection[None, :, :]
            return jnp.concatenate([matrix[:k], updated], axis=0)

        landmark = reflect(landmark)
        knot_jac = reflect(knot_jac)
    return knot_jac[3:]


def block_grams(reduced, num_blocks):
    red_rows, win_width, landmarks = reduced.shape
    shaped = reduced.reshape(red_rows, win_width, num_blocks, landmarks // num_blocks)
    return jnp.einsum("rcbl,rdbl->bcd", shaped, shaped, precision=lax.Precision.HIGHEST)


def place_blocks(gram_sum, block_gram, block_start, group_cols):
    win_width = block_gram.shape[1]
    group_knots = group_cols // KDOF

    def add_block(position, running):
        base_knot = block_start[position]
        group_id = base_knot // group_knots
        offset = base_knot % group_knots * KDOF
        row_start = group_id * group_cols + offset
        keep = jnp.float32(1.0)
        current = lax.dynamic_slice(running, (row_start, offset), (win_width, win_width))
        return lax.dynamic_update_slice(
            running, current + keep * block_gram[position], (row_start, offset)
        )

    return lax.fori_loop(0, block_gram.shape[0], add_block, gram_sum)


def local(land_jac, pose_jac, segment, knot_frac, track_len, block_base, damping):
    num_blocks = block_base.shape[0]
    reduced = reduce_rows(land_jac, pose_jac, segment, knot_frac, track_len)
    grams = block_grams(reduced, num_blocks)
    group_cols = damping.shape[0]
    num_groups = lax.axis_size("cols")
    local_gram = place_blocks(
        jnp.zeros((group_cols * num_groups, group_cols), jnp.float32), grams, block_base, group_cols
    )
    group_gram = lax.psum_scatter(local_gram, "cols", scatter_dimension=0, tiled=True)
    gram_whole = lax.psum(group_gram, "rows")
    factors = jnp.linalg.cholesky(gram_whole + jnp.diag(damping)).T
    return factors


def solution(mesh):
    return jax.shard_map(
        local,
        mesh=mesh,
        in_specs=(
            P(None, None, ("rows", "cols")),
            P(None, None, ("rows", "cols")),
            P(None, ("rows", "cols")),
            P(None, ("rows", "cols")),
            P(("rows", "cols")),
            P(("rows", "cols")),
            P("cols"),
        ),
        out_specs=P("cols", None),
        check_vma=False,
    )
```

profile of v0, /device:TPU:1, one launch (start us, length us, event | category | flops | bytes accessed | tf_op | source)
XLA Modules:
  0.0 537.3 jit_solution(5043726960606032738)
XLA Ops:
  7.4 1.0 broadcast_multiply_fusion.2
  10.9 6.8 %broadcast_multiply_fusion = (f32[8,2,8,6,2048]{4,1,0,3,2:T(2,128)}, f32[8,6,2048]{2,1,0:T(8,128)S(1)}) fusion(f32[8,2,6,2048]{3,1,0,2:T(2,128)S(1)} %mul.348, f32[8,8,2048]{2,0,1:T(8,128)S(1)} %select_add_fusion.1, f32[8,2,2048]{2,1,0:T(2,128)S(1)} %mul.361), kind=kLoop, calls=%fused_computation.9 | loop fusion | flops 4620288 | bytes 8126464 | tf_op jit(solution)/shard_map/mul | solution.py:37
  17.6 8.6 %mul.351 = f32[16,48,2048]{2,0,1:T(8,128)} reshape(f32[8,2,8,6,2048]{4,1,0,3,2:T(2,128)} %get-tuple-element.137) | data formatting | bytes 12582912 | tf_op jit(solution)/shard_map/mul | solution.py:37
  26.3 5.1 multiply_reduce_fusion.1
  31.4 2.7 multiply_reduce_fusion
  34.1 4.0 slice_subtract_fusion
  38.1 7.2 %reshape.310 = f32[13,48,16,128]{3,2,0,1:T(8,128)} reshape(f32[13,48,2048]{2,0,1:T(8,128)} %slice_subtract_fusion) | data formatting | bytes 10223616 | tf_op jit(solution)/shard_map/reshape | solution.py:61
  45.2 12.0 %fusion.3 = f32[16,48,48]{2,1,0:T(8,128)S(1)} fusion(f32[13,48,16,128]{3,2,0,1:T(8,128)} %reshape.310), kind=kOutput, calls=%fused_computation.17 | convolution fusion | flops 736100352 | bytes 5259264 | tf_op jit(solution)/shard_map/rcbl,rdbl->bcd/dot_general | solution.py:62
  57.2 4.8 broadcast_in_dim.34.clone
  62.0 114.2 %while.15 = (s32[]{:T(128)}, f32[3072,768]{0,1:T(8,128)}, s32[16]{0:T(128)S(1)}, f32[16,48,48]{2,1,0:T(8,128)S(1)}, s32[]{:T(128)}, /*index=5*/s32[]{:T(128)}, s...) while((s32[]{:T(128)}, f32[3072,768]{0,1:T(8,128)}, ...), condition=%wide.region_12.13_spmd, body=%wide.region_11.12_spmd.sunk | while | flops 2334 | bytes 101824 | solution.py:80
  65.2 0.9 dynamic_slice.36
  66.3 2.9 dynamic_update_slice.11
  72.4 0.9 dynamic_slice.36
  73.4 2.9 dynamic_update_slice.11
  79.5 0.9 dynamic_slice.36
  80.6 2.9 dynamic_update_slice.11
  86.7 0.9 dynamic_slice.36
  87.8 2.9 dynamic_update_slice.11
  94.9 2.9 dynamic_update_slice.11
  101.0 0.9 dynamic_slice.36
  102.1 2.9 dynamic_update_slice.11
  108.1 0.9 dynamic_slice.36
  109.2 2.9 dynamic_update_slice.11
  115.3 0.9 dynamic_slice.36
  116.3 2.9 dynamic_update_slice.11
  122.4 0.9 dynamic_slice.36
  123.5 2.9 dynamic_update_slice.11
  129.5 0.9 dynamic_slice.36
  130.6 2.9 dynamic_update_slice.11
  136.7 0.9 dynamic_slice.36
  137.8 2.7 dynamic_update_slice.11
  144.8 2.9 dynamic_update_slice.11
  150.8 0.9 dynamic_slice.36
  151.9 2.9 dynamic_update_slice.11
  158.0 0.9 dynamic_slice.36
  159.0 2.9 dynamic_update_slice.11
  165.1 0.9 dynamic_slice.36
  166.2 2.9 dynamic_update_slice.11
  172.2 0.9 dynamic_slice.36
  173.3 2.9 dynamic_update_slice.11
  176.3 92.4 %reduce-scatter.2.cloned.1.call-done = f32[768,768]{0,1:T(8,128)} async-done(((f32[3072,768]{0,1:T(8,128)}), f32[768,768]{0,1:T(8,128)}) %reduce-scatter.2.cloned.1.call-update) | async-done | bytes 2359312 | tf_op jit(solution)/shard_map/reduce_scatter | solution.py:92
  268.7 110.7 %all-reduce.3.cloned.1.call-done = f32[768,768]{0,1:T(8,128)} async-done(((f32[768,768]{0,1:T(8,128)}), f32[768,768]{0,1:T(8,128)}) %all-reduce.3.cloned.1.call-update) | async-done | bytes 2359312 | tf_op jit(solution)/shard_map/psum | solution.py:93
  379.4 3.2 select_add_fusion
  382.7 2.4 copy.26
  385.1 2.0 fusion.2
  387.1 1.4 copy-done
  388.5 11.7 %cholesky.164 = f32[128,128]{1,0:T(8,128)S(1)} custom-call(f32[128,128]{1,0:T(8,128)S(1)} %cholesky.421), custom_call_target="Cholesky" | custom-call | tf_op jit(solution)/shard_map/jit(cholesky)/cholesky | solution.py:94
  400.3 9.8 %custom-call.43 = f32[1,128,128]{1,2,0:T(8,128)S(1)} custom-call(f32[1,128,128]{2,1,0:T(8,128)S(1)} %get-tuple-element.148), custom_call_target="InvertDiagBlocksLowerTriangular" | custom-call | tf_op jit(solution)/shard_map/jit(cholesky)/cholesky | solution.py:94
  410.2 1.4 fusion.10
  411.5 1.4 convolution_subtract_fusion
  413.1 11.7 %cholesky.187 = f32[128,128]{1,0:T(8,128)S(1)} custom-call(f32[128,128]{1,0:T(8,128)S(1)} %cholesky.425), custom_call_target="Cholesky" | custom-call | tf_op jit(solution)/shard_map/jit(cholesky)/cholesky | solution.py:94
  425.0 10.0 %custom-call.44 = f32[1,128,128]{1,2,0:T(8,128)S(1)} custom-call(f32[1,128,128]{2,1,0:T(8,128)S(1)} %get-tuple-element.146), custom_call_target="InvertDiagBlocksLowerTriangular" | custom-call | tf_op jit(solution)/shard_map/jit(cholesky)/cholesky | solution.py:94
  435.6 1.9 convolution_subtract_fusion.1
  437.5 11.7 %cholesky.352 = f32[128,128]{1,0:T(8,128)S(1)} custom-call(f32[128,128]{1,0:T(8,128)S(1)} %cholesky.430), custom_call_target="Cholesky" | custom-call | tf_op jit(solution)/shard_map/jit(cholesky)/cholesky | solution.py:94
  449.4 9.8 %custom-call.45 = f32[1,128,128]{1,2,0:T(8,128)S(1)} custom-call(f32[1,128,128]{2,1,0:T(8,128)S(1)} %get-tuple-element.144), custom_call_target="InvertDiagBlocksLowerTriangular" | custom-call | tf_op jit(solution)/shard_map/jit(cholesky)/cholesky | solution.py:94
  459.6 2.1 convolution_subtract_fusion.2
  461.7 11.9 %cholesky.371 = f32[128,128]{1,0:T(8,128)S(1)} custom-call(f32[128,128]{1,0:T(8,128)S(1)} %cholesky.435), custom_call_target="Cholesky" | custom-call | tf_op jit(solution)/shard_map/jit(cholesky)/cholesky | solution.py:94
  473.8 9.8 %custom-call.46 = f32[1,128,128]{1,2,0:T(8,128)S(1)} custom-call(f32[1,128,128]{2,1,0:T(8,128)S(1)} %get-tuple-element.142), custom_call_target="InvertDiagBlocksLowerTriangular" | custom-call | tf_op jit(solution)/shard_map/jit(cholesky)/cholesky | solution.py:94
  483.9 1.9 convolution_subtract_fusion.3
  485.8 11.7 %cholesky.390 = f32[128,128]{1,0:T(8,128)S(1)} custom-call(f32[128,128]{1,0:T(8,128)S(1)} %cholesky.440), custom_call_target="Cholesky" | custom-call | tf_op jit(solution)/shard_map/jit(cholesky)/cholesky | solution.py:94
  497.7 9.8 %custom-call.47 = f32[1,128,128]{1,2,0:T(8,128)S(1)} custom-call(f32[1,128,128]{2,1,0:T(8,128)S(1)} %get-tuple-element.140), custom_call_target="InvertDiagBlocksLowerTriangular" | custom-call | tf_op jit(solution)/shard_map/jit(cholesky)/cholesky | solution.py:94
  507.8 1.8 convolution_subtract_fusion.4
  509.6 11.7 %cholesky.408 = f32[128,128]{1,0:T(8,128)S(1)} custom-call(f32[128,128]{1,0:T(8,128)S(1)} %convolution_subtract_fusion.4), custom_call_target="Cholesky" | custom-call | tf_op jit(solution)/shard_map/jit(cholesky)/cholesky | solution.py:94
  528.6 1.6 select_bitcast_fusion
  (158 shorter events, 23.6 us)
Async XLA Ops:
  6.5 2.1 copy-start.1
  6.5 262.2 %reduce-scatter.2.cloned.1.call-start = ((), (), s32[]{:S(2)}) async-start(), calls=%async_computation.1 | async-start | bytes 11796480 | tf_op jit(solution)/shard_map/reduce_scatter | solution.py:92
  8.8 0.8 copy-start.3
  8.9 0.8 copy-start.4
  9.0 1.2 copy-start.2
  57.2 4.8 copy-start.6
  176.2 203.2 %copy-start.5 = (f32[768]{0:T(1024)S(1)}, f32[768]{0:T(1024)}, u32[]{:S(2)}) copy-start(f32[768]{0:T(1024)} %param.15) | copy-start | bytes 9220
  176.2 203.2 %all-reduce.3.cloned.1.call-start = ((), (), s32[]{:S(2)}) async-start(), calls=%async_computation.2 | async-start | bytes 4718592 | tf_op jit(solution)/shard_map/psum | solution.py:93
  387.1 1.4 copy-start
Sparse Core Ops, SparseCore 0:
  176.3 92.3 reduce-scatter.1
  272.0 107.3 all-reduce.2
where the time goes:
time: 548 us; the launch traced here: 537 us
  waiting for transfers between devices  203 us (37%)
  other arithmetic  152 us (28%)
  local copies, waits for them, and re-layouts  99.8 us (18%)
  loops' own time  40.8 us (7%)
  matrix products  23.9 us (4%)
  between operations  18 us (3%)
    another operation x22, other arithmetic, local(): factors = jnp.linalg.cholesky(gram_whole + jnp.diag(damping)).T  123 us
    psum x1, waiting for transfers between devices, local(): gram_whole = lax.psum(group_gram, 'rows')  111 us
    reduce_scatter x1, waiting for transfers between devices, local(): lax.psum_scatter(local_gram, 'cols', scatter_dimension=0, tiled=True)  92.4 us
    dynamic_update_slice x32, local copies, waits for them, and re-layouts, add_block(): lax.dynamic_update_slice(running, current + keep * block_gram[position],...  47.4 us
    another operation x1, loops' own time, place_blocks(): return lax.fori_loop(0, block_gram.shape[0], add_block, gram_sum)  40.8 us
    dynamic_slice x32, local copies, waits for them, and re-layouts, add_block(): lax.dynamic_slice(running, (row_start, offset), (win_width, win_width))  15.7 us
    dot_general x1, matrix products, block_grams(): jnp.einsum('rcbl,rdbl->bcd', shaped, shaped, precision=lax.Precision.HIGH...  12 us
    another operation x10, matrix products, local(): factors = jnp.linalg.cholesky(gram_whole + jnp.diag(damping)).T  11.9 us
  transfers between devices with their start and end apart: 2, of which 2 were waited for; matrix products, arithmetic and copies ran while one was open for 0% of the time, Pallas kernels for 0%

commit v1 on v0

--- a/solution.py
+++ b/solution.py
@@ -62,22 +62,37 @@
     return jnp.einsum("rcbl,rdbl->bcd", shaped, shaped, precision=lax.Precision.HIGHEST)
 
 
-def place_blocks(gram_sum, block_gram, block_start, group_cols):
-    win_width = block_gram.shape[1]
+def skew_blocks(grams):
+    num_blocks = grams.shape[0]
+    g5 = grams.reshape(num_blocks, WIN_KNOTS, KDOF, WIN_KNOTS, KDOF)
+    k1 = lax.broadcasted_iota(jnp.int32, (WIN_KNOTS, WIN_KNOTS, WIN_KNOTS), 0)
+    k2 = lax.broadcasted_iota(jnp.int32, (WIN_KNOTS, WIN_KNOTS, WIN_KNOTS), 1)
+    d = lax.broadcasted_iota(jnp.int32, (WIN_KNOTS, WIN_KNOTS, WIN_KNOTS), 2)
+    pick = (k2 == k1 + d).astype(jnp.float32)
+    return jnp.einsum("bienf,ind->bidef", g5, pick, precision=lax.Precision.HIGHEST)
+
+
+def place_band(skewed, block_start, group_cols, num_groups):
+    num_blocks = skewed.shape[0]
     group_knots = group_cols // KDOF
+    rows = num_groups * group_knots
+    target = (block_start // group_knots) * group_knots + block_start % group_knots
+    target = target[:, None] + jnp.arange(WIN_KNOTS, dtype=jnp.int32)[None, :]
+    row_id = lax.broadcasted_iota(jnp.int32, (rows, num_blocks, WIN_KNOTS), 0)
+    onehot = (row_id == target[None]).astype(jnp.float32).reshape(rows, num_blocks * WIN_KNOTS)
+    flat = skewed.reshape(num_blocks * WIN_KNOTS, WIN_KNOTS * KDOF * KDOF)
+    return jnp.dot(onehot, flat, precision=lax.Precision.HIGHEST)
 
-    def add_block(position, running):
-        base_knot = block_start[position]
-        group_id = base_knot // group_knots
-        offset = base_knot % group_knots * KDOF
-        row_start = group_id * group_cols + offset
-        keep = jnp.float32(1.0)
-        current = lax.dynamic_slice(running, (row_start, offset), (win_width, win_width))
-        return lax.dynamic_update_slice(
-            running, current + keep * block_gram[position], (row_start, offset)
-        )
 
-    return lax.fori_loop(0, block_gram.shape[0], add_block, gram_sum)
+def band_to_lower(band, group_cols):
+    group_knots = group_cols // KDOF
+    band4 = band.reshape(group_knots, WIN_KNOTS, KDOF, KDOF)
+    k = lax.broadcasted_iota(jnp.int32, (group_knots, WIN_KNOTS, group_knots), 0)
+    d = lax.broadcasted_iota(jnp.int32, (group_knots, WIN_KNOTS, group_knots), 1)
+    m = lax.broadcasted_iota(jnp.int32, (group_knots, WIN_KNOTS, group_knots), 2)
+    spread = (m == k + d).astype(jnp.float32)
+    lower = jnp.einsum("kdef,kdm->mfke", band4, spread, precision=lax.Precision.HIGHEST)
+    return lower.reshape(group_cols, group_cols)
 
 
 def local(land_jac, pose_jac, segment, knot_frac, track_len, block_base, damping):
@@ -86,12 +101,11 @@
     grams = block_grams(reduced, num_blocks)
     group_cols = damping.shape[0]
     num_groups = lax.axis_size("cols")
-    local_gram = place_blocks(
-        jnp.zeros((group_cols * num_groups, group_cols), jnp.float32), grams, block_base, group_cols
-    )
-    group_gram = lax.psum_scatter(local_gram, "cols", scatter_dimension=0, tiled=True)
-    gram_whole = lax.psum(group_gram, "rows")
-    factors = jnp.linalg.cholesky(gram_whole + jnp.diag(damping)).T
+    band = place_band(skew_blocks(grams), block_base, group_cols, num_groups)
+    group_band = lax.psum_scatter(band, "cols", scatter_dimension=0, tiled=True)
+    band_whole = lax.psum(group_band, "rows")
+    lower = band_to_lower(band_whole, group_cols) + jnp.diag(damping)
+    factors = lax.linalg.cholesky(lower, symmetrize_input=False).T
     return factors
 
 

time: 548 us -> 426 us (0.78)
  waiting for transfers between devices: 203 us -> 135 us
  loops' own time: 40.8 us -> 0 us
  local copies, waits for them, and re-layouts: 99.8 us -> 91.3 us
    reduce_scatter x1, waiting for transfers between devices: 92.4 us -> 23.3 us  [local(): group_band = lax.psum_scatter(band, 'cols', scatter_dimension=0, tiled=True)]
    dynamic_update_slice x32 -> x0, local copies, waits for them, and re-layouts: 47.4 us -> none  [add_block(): lax.dynamic_update_slice(running, current + keep * block_gram[position],...]
    reshape x0 -> x6, local copies, waits for them, and re-layouts: none -> 44.5 us  [the longest x1 35.5 us: band_to_lower(): return lower.reshape(group_cols, group_cols)]
    another operation x1 -> x0, loops' own time: 40.8 us -> none  [place_blocks(): return lax.fori_loop(0, block_gram.shape[0], add_block, gram_sum)]
    transpose x0 -> x3, local copies, waits for them, and re-layouts: none -> 28.2 us  [the longest x1 24 us: band_to_lower(): jnp.einsum('kdef,kdm->mfke', band4, spread, precision=lax.Precision.HIGHEST)]
    dynamic_slice x48 -> x0, local copies, waits for them, and re-layouts: 25.8 us -> none  [the longest x32 15.7 us: add_block(): lax.dynamic_slice(running, (row_start, offset), (win_width, win_width))]
    dot_general x0 -> x3, matrix products: none -> 6.88 us  [the longest x1 3.67 us: band_to_lower(): jnp.einsum('kdef,kdm->mfke', band4, spread, precision=lax.Precision.HIGHEST)]
where the time goes in v1:
time: 426 us; the launch traced here: 420 us
  other arithmetic  147 us (35%)
  waiting for transfers between devices  135 us (32%)
  local copies, waits for them, and re-layouts  91.3 us (21%)
  matrix products  28.6 us (7%)
  between operations  18 us (4%)
    another operation x22, other arithmetic, local(): factors = lax.linalg.cholesky(lower, symmetrize_input=False).T  124 us
    psum x1, waiting for transfers between devices, local(): band_whole = lax.psum(group_band, 'rows')  111 us
    reshape x1, local copies, waits for them, and re-layouts, band_to_lower(): return lower.reshape(group_cols, group_cols)  35.5 us
    transpose x1, local copies, waits for them, and re-layouts, band_to_lower(): jnp.einsum('kdef,kdm->mfke', band4, spread, precision=lax.Precision.HIGHEST)  24 us
    reduce_scatter x1, waiting for transfers between devices, local(): group_band = lax.psum_scatter(band, 'cols', scatter_dimension=0, tiled=True)  23.3 us
    dot_general x1, matrix products, block_grams(): jnp.einsum('rcbl,rdbl->bcd', shaped, shaped, precision=lax.Precision.HIGH...  11.9 us
    another operation x10, matrix products, local(): factors = lax.linalg.cholesky(lower, symmetrize_input=False).T  9.81 us
    mul x2, local copies, waits for them, and re-layouts, reduce_rows(): knot_weight[:, None, :, None, :] * pose_rows  9.06 us
  transfers between devices with their start and end apart: 2, of which 2 were waited for; matrix products, arithmetic and copies ran while one was open for 0% of the time, Pallas kernels for 0%

profile of v1, /device:TPU:1, one launch (start us, length us, event | category | flops | bytes accessed | tf_op | source)
XLA Modules:
  0.0 419.7 jit_solution(93566701999656274)
XLA Ops:
  6.5 0.8 fusion.41
  7.3 0.1 mul.329
  7.4 1.0 broadcast_multiply_fusion.2
  8.6 0.1 multiply_reduce_fusion.4
  8.7 0.1 mul.345
  9.2 0.1 multiply_reduce_fusion.3
  9.4 0.1 multiply_subtract_fusion
  9.5 0.1 iota_add_fusion
  9.6 0.1 copy-done.3
  10.0 0.2 copy-done.2
  10.1 0.1 broadcast_multiply_fusion.1
  10.2 0.5 mul.332
  10.7 0.2 select_add_fusion.1
  10.9 6.8 %broadcast_multiply_fusion = (f32[8,2,8,6,2048]{4,1,0,3,2:T(2,128)}, f32[8,6,2048]{2,1,0:T(8,128)S(1)}) fusion(f32[8,2,6,2048]{3,1,0,2:T(2,128)S(1)} %mul.332, f32[8,8,2048]{2,0,1:T(8,128)S(1)} %select_add_fusion.1, f32[8,2,2048]{2,1,0:T(2,128)S(1)} %mul.345), kind=kLoop, calls=%fused_computation.8 | loop fusion | flops 4620288 | bytes 8126464 | tf_op jit(solution)/shard_map/mul | solution.py:37
  17.6 8.6 %mul.335 = f32[16,48,2048]{2,0,1:T(8,128)} reshape(f32[8,2,8,6,2048]{4,1,0,3,2:T(2,128)} %get-tuple-element.15) | data formatting | bytes 12582912 | tf_op jit(solution)/shard_map/mul | solution.py:37
  26.3 5.1 %multiply_reduce_fusion.1 = (f32[48,2048]{1,0:T(8,128)S(1)}, f32[15,48,2048]{2,0,1:T(8,128)S(1)}) fusion(f32[15,2048]{1,0:T(8,128)S(1)} %get-tuple-element.10, f32[48,2048]{1,0:T(8,128)S(1)} %mul.348, f32[15,2048]{1,0:T(8,128)S(1)} %slice.171, f32[16,48,2048]{2,0,1:T(8,128)} %mul.335), kind=kLoop, calls=%fused_computation.4 | loop fusion | flops 5799936 | bytes 12828672 | tf_op jit(solution)/shard_map/reduce_sum | solution.py:50
  31.4 2.7 multiply_reduce_fusion
  34.1 4.0 slice_subtract_fusion
  38.1 7.4 %reshape.374 = f32[13,48,16,128]{3,2,0,1:T(8,128)} reshape(f32[13,48,2048]{2,0,1:T(8,128)} %slice_subtract_fusion) | data formatting | bytes 10223616 | tf_op jit(solution)/shard_map/reshape | solution.py:61
  45.5 11.9 %fusion.2 = f32[16,48,48]{2,1,0:T(8,128)S(1)} fusion(f32[13,48,16,128]{3,2,0,1:T(8,128)} %reshape.374), kind=kOutput, calls=%fused_computation.16 | convolution fusion | flops 736100352 | bytes 5259264 | tf_op jit(solution)/shard_map/rcbl,rdbl->bcd/dot_general | solution.py:62
  57.4 0.9 reshape.375
  58.3 3.7 copy.17
  62.0 1.9 convolution_bitcast_fusion.1
  63.9 1.1 copy.18
  65.0 1.2 reshape.366
  66.2 1.3 fusion.16
  67.5 23.3 %reduce-scatter.2.cloned.1.call-done = f32[128,288]{0,1:T(8,128)} async-done(((f32[512,288]{0,1:T(8,128)}), f32[128,288]{0,1:T(8,128)}) %reduce-scatter.2.cloned.1.call-update) | async-done | bytes 147472 | tf_op jit(solution)/shard_map/reduce_scatter | solution.py:105
  90.9 0.9 reshape.367
  91.8 2.2 copy.19
  94.1 111.5 %all-reduce.3.cloned.1.call-done = f32[128,8,6,6]{1,3,2,0:T(8,128)} async-done(((f32[128,8,6,6]{1,3,2,0:T(8,128)}), f32[128,8,6,6]{1,3,2,0:T(8,128)}) %all-reduce.3.cloned.1.call-update) | async-done | bytes 147472 | tf_op jit(solution)/shard_map/psum | solution.py:106
  205.5 3.7 convolution_bitcast_fusion
  209.2 24.0 %copy.20 = f32[128,6,128,6]{3,2,1,0:T(8,128)} copy(f32[128,6,128,6]{0,1,3,2:T(8,128)S(1)} %convolution_bitcast_fusion) | data formatting | bytes 4718592 | tf_op jit(solution)/shard_map/kdef,kdm->mfke/transpose | solution.py:94
  233.3 35.5 %reshape.368 = f32[768,768]{1,0:T(8,128)S(1)} reshape(f32[128,6,128,6]{3,2,1,0:T(8,128)} %copy.20) | data formatting | bytes 4718592 | tf_op jit(solution)/shard_map/reshape | solution.py:95
  268.8 0.2 select_add_fusion
  269.1 1.4 copy-done
  270.5 11.7 %cholesky.164 = f32[128,128]{1,0:T(8,128)S(1)} custom-call(f32[128,128]{1,0:T(8,128)S(1)} %cholesky.421), custom_call_target="Cholesky" | custom-call | tf_op jit(solution)/shard_map/cholesky | solution.py:108
  282.2 9.8 %custom-call.32 = f32[1,128,128]{1,2,0:T(8,128)S(1)} custom-call(f32[1,128,128]{2,1,0:T(8,128)S(1)} %get-tuple-element.32), custom_call_target="InvertDiagBlocksLowerTriangular" | custom-call | tf_op jit(solution)/shard_map/cholesky | solution.py:108
  292.0 0.2 cholesky.338
  292.2 1.4 constant_dynamic-update-slice_fusion.5
  293.6 1.4 convolution_subtract_fusion
  295.0 11.7 %cholesky.187 = f32[128,128]{1,0:T(8,128)S(1)} custom-call(f32[128,128]{1,0:T(8,128)S(1)} %cholesky.425), custom_call_target="Cholesky" | custom-call | tf_op jit(solution)/shard_map/cholesky | solution.py:108
  306.8 10.2 %custom-call.33 = f32[1,128,128]{1,2,0:T(8,128)S(1)} custom-call(f32[1,128,128]{2,1,0:T(8,128)S(1)} %get-tuple-element.29), custom_call_target="InvertDiagBlocksLowerTriangular" | custom-call | tf_op jit(solution)/shard_map/cholesky | solution.py:108
  317.0 0.4 convolution_dynamic-update-slice_fusion
  317.3 1.5 convolution_subtract_fusion.1
  318.9 11.7 %cholesky.352 = f32[128,128]{1,0:T(8,128)S(1)} custom-call(f32[128,128]{1,0:T(8,128)S(1)} %cholesky.430), custom_call_target="Cholesky" | custom-call | tf_op jit(solution)/shard_map/cholesky | solution.py:108
  330.6 0.7 compare_reduce_fusion.3
  331.4 9.8 %custom-call.34 = f32[1,128,128]{1,2,0:T(8,128)S(1)} custom-call(f32[1,128,128]{2,1,0:T(8,128)S(1)} %get-tuple-element.26), custom_call_target="InvertDiagBlocksLowerTriangular" | custom-call | tf_op jit(solution)/shard_map/cholesky | solution.py:108
  341.2 0.3 convolution_dynamic-update-slice_fusion.1
  341.5 1.6 convolution_subtract_fusion.2
  343.1 11.9 %cholesky.371 = f32[128,128]{1,0:T(8,128)S(1)} custom-call(f32[128,128]{1,0:T(8,128)S(1)} %cholesky.435), custom_call_target="Cholesky" | custom-call | tf_op jit(solution)/shard_map/cholesky | solution.py:108
  355.0 0.6 compare_reduce_fusion.2
  355.6 9.8 %custom-call.35 = f32[1,128,128]{1,2,0:T(8,128)S(1)} custom-call(f32[1,128,128]{2,1,0:T(8,128)S(1)} %get-tuple-element.23), custom_call_target="InvertDiagBlocksLowerTriangular" | custom-call | tf_op jit(solution)/shard_map/cholesky | solution.py:108
  365.4 0.3 convolution_dynamic-update-slice_fusion.2
  365.7 1.5 convolution_subtract_fusion.3
  367.2 11.7 %cholesky.390 = f32[128,128]{1,0:T(8,128)S(1)} custom-call(f32[128,128]{1,0:T(8,128)S(1)} %cholesky.440), custom_call_target="Cholesky" | custom-call | tf_op jit(solution)/shard_map/cholesky | solution.py:108
  378.9 0.7 compare_reduce_fusion.1
  379.6 9.8 %custom-call.36 = f32[1,128,128]{1,2,0:T(8,128)S(1)} custom-call(f32[1,128,128]{2,1,0:T(8,128)S(1)} %get-tuple-element.20), custom_call_target="InvertDiagBlocksLowerTriangular" | custom-call | tf_op jit(solution)/shard_map/cholesky | solution.py:108
  389.4 0.2 convolution_dynamic-update-slice_fusion.3
  389.6 1.3 convolution_subtract_fusion.4
  390.9 11.9 %cholesky.408 = f32[128,128]{1,0:T(8,128)S(1)} custom-call(f32[128,128]{1,0:T(8,128)S(1)} %convolution_subtract_fusion.4), custom_call_target="Cholesky" | custom-call | tf_op jit(solution)/shard_map/cholesky | solution.py:108
  402.9 0.7 compare_reduce_fusion
  403.6 0.7 compare_reduce_fusion.4
  408.0 1.6 select_bitcast_fusion
  409.6 3.0 copy.21
  (59 shorter events, 1.2 us)
Async XLA Ops:
  6.5 2.1 copy-start.1
  6.5 84.3 %reduce-scatter.2.cloned.1.call-start = ((), (), s32[]{:S(2)}) async-start(), calls=%async_computation.1 | async-start | bytes 737280 | tf_op jit(solution)/shard_map/reduce_scatter | solution.py:105
  8.8 0.7 copy-start.6
  8.9 0.8 copy-start.3
  8.9 0.8 copy-start.4
  9.0 1.2 copy-start.2
  67.5 138.0 %all-reduce.3.cloned.1.call-start = ((), (), s32[]{:S(2)}) async-start(), calls=%async_computation.2 | async-start | bytes 6291456 | tf_op jit(solution)/shard_map/psum | solution.py:106
  233.3 35.6 %copy-start.5 = (f32[768]{0:T(1024)S(1)}, f32[768]{0:T(1024)}, u32[]{:S(2)}) copy-start(f32[768]{0:T(1024)} %param.13) | copy-start | bytes 9220
  269.1 1.4 copy-start
Sparse Core Ops, SparseCore 0:
  67.6 23.2 reduce-scatter.1
  94.2 111.2 all-reduce.2

commit v2 on v1

--- a/solution.py
+++ b/solution.py
@@ -95,6 +95,31 @@
     return lower.reshape(group_cols, group_cols)
 
 
+def halve_over(band, axis):
+    n = lax.axis_size(axis)
+    c = lax.axis_index(axis)
+    size = band.shape[0]
+    s = n // 2
+    while s >= 1:
+        half = size // 2
+        bit = (c // s) % 2
+        keep = lax.dynamic_slice_in_dim(band, bit * half, half, 0)
+        send = lax.dynamic_slice_in_dim(band, (1 - bit) * half, half, 0)
+        band = keep + lax.ppermute(send, axis, [(i, i ^ s) for i in range(n)])
+        size = half
+        s //= 2
+    return band
+
+
+def butterfly_sum(band, axis):
+    n = lax.axis_size(axis)
+    s = 1
+    while s < n:
+        band = band + lax.ppermute(band, axis, [(i, i ^ s) for i in range(n)])
+        s *= 2
+    return band
+
+
 def local(land_jac, pose_jac, segment, knot_frac, track_len, block_base, damping):
     num_blocks = block_base.shape[0]
     reduced = reduce_rows(land_jac, pose_jac, segment, knot_frac, track_len)
@@ -102,8 +127,7 @@
     group_cols = damping.shape[0]
     num_groups = lax.axis_size("cols")
     band = place_band(skew_blocks(grams), block_base, group_cols, num_groups)
-    group_band = lax.psum_scatter(band, "cols", scatter_dimension=0, tiled=True)
-    band_whole = lax.psum(group_band, "rows")
+    band_whole = butterfly_sum(halve_over(band, "cols"), "rows")
     lower = band_to_lower(band_whole, group_cols) + jnp.diag(damping)
     factors = lax.linalg.cholesky(lower, symmetrize_input=False).T
     return factors

time: 426 us -> 320 us (0.75)
  the two profiles are of different devices: /device:TPU:1 before, /device:TPU:38 now
where the time goes in v2:
time: 320 us; the launch traced here: 313 us
  other arithmetic  147 us (46%)
  local copies, waits for them, and re-layouts  91.1 us (28%)
  waiting for transfers between devices  33 us (10%)
  matrix products  27.8 us (9%)
  starting transfers between devices  9.64 us (3%)
  between operations  4.62 us (1%)
    another operation x22, other arithmetic, local(): factors = lax.linalg.cholesky(lower, symmetrize_input=False).T  124 us
    reshape x1, local copies, waits for them, and re-layouts, band_to_lower(): return lower.reshape(group_cols, group_cols)  35.7 us
    transpose x1, local copies, waits for them, and re-layouts, band_to_lower(): jnp.einsum('kdef,kdm->mfke', band4, spread, precision=lax.Precision.HIGHEST)  24 us
    ppermute x5, waiting for transfers between devices, butterfly_sum(): band = band + lax.ppermute(band, axis, [(i, i ^ s) for i in range(n)])  22.4 us
    dot_general x1, matrix products, block_grams(): jnp.einsum('rcbl,rdbl->bcd', shaped, shaped, precision=lax.Precision.HIGH...  11.9 us
    ppermute x2, waiting for transfers between devices, halve_over(): band = keep + lax.ppermute(send, axis, [(i, i ^ s) for i in range(n)])  10.6 us
    another operation x10, matrix products, local(): factors = lax.linalg.cholesky(lower, symmetrize_input=False).T  9.82 us
    mul x2, local copies, waits for them, and re-layouts, reduce_rows(): knot_weight[:, None, :, None, :] * pose_rows  9.17 us
  transfers between devices with their start and end apart: 7, of which 7 were waited for; matrix products, arithmetic and copies ran while one was open for 0% of the time, Pallas kernels for 0%

profile of v2, /device:TPU:38, one launch (start us, length us, event | category | flops | bytes accessed | tf_op | source)
XLA Modules:
  0.0 313.2 jit_solution(10601694257756762667)
XLA Ops:
  0.0 0.8 fusion.41
  0.9 1.0 broadcast_multiply_fusion.2
  3.7 0.5 mul.344
  4.1 0.2 select_add_fusion.1
  4.3 6.8 %broadcast_multiply_fusion = (f32[8,2,8,6,2048]{4,1,0,3,2:T(2,128)}, f32[8,6,2048]{2,1,0:T(8,128)S(1)}) fusion(f32[8,2,6,2048]{3,1,0,2:T(2,128)S(1)} %mul.344, f32[8,8,2048]{2,0,1:T(8,128)S(1)} %select_add_fusion.1, f32[8,2,2048]{2,1,0:T(2,128)S(1)} %mul.357), kind=kLoop, calls=%fused_computation.8 | loop fusion | flops 4620288 | bytes 8126464 | tf_op jit(solution)/shard_map/mul | solution.py:37
  11.1 8.7 %mul.347 = f32[16,48,2048]{2,0,1:T(8,128)} reshape(f32[8,2,8,6,2048]{4,1,0,3,2:T(2,128)} %get-tuple-element.15) | data formatting | bytes 12582912 | tf_op jit(solution)/shard_map/mul | solution.py:37
  19.9 5.1 %multiply_reduce_fusion.1 = (f32[48,2048]{1,0:T(8,128)S(1)}, f32[15,48,2048]{2,0,1:T(8,128)S(1)}) fusion(f32[15,2048]{1,0:T(8,128)S(1)} %get-tuple-element.10, f32[48,2048]{1,0:T(8,128)S(1)} %mul.360, f32[15,2048]{1,0:T(8,128)S(1)} %slice.171, f32[16,48,2048]{2,0,1:T(8,128)} %mul.347), kind=kLoop, calls=%fused_computation.4 | loop fusion | flops 5799936 | bytes 12828672 | tf_op jit(solution)/shard_map/reduce_sum | solution.py:50
  25.0 2.7 multiply_reduce_fusion
  27.7 4.0 %slice_subtract_fusion = f32[13,48,2048]{2,0,1:T(8,128)} fusion(f32[14,48,2048]{2,0,1:T(8,128)S(1)} %get-tuple-element.8, f32[48,2048]{1,0:T(8,128)S(1)} %get-tuple-element.7, f32[13,2048]{1,0:T(8,128)S(1)} %slice.182), kind=kLoop, calls=%fused_computation | loop fusion | flops 2555904 | bytes 10723328 | tf_op jit(solution)/shard_map/sub | solution.py:51
  31.7 7.3 %reshape.374 = f32[13,48,16,128]{3,2,0,1:T(8,128)} reshape(f32[13,48,2048]{2,0,1:T(8,128)} %slice_subtract_fusion) | data formatting | bytes 10223616 | tf_op jit(solution)/shard_map/reshape | solution.py:61
  39.0 11.9 %fusion.2 = f32[16,48,48]{2,1,0:T(8,128)S(1)} fusion(f32[13,48,16,128]{3,2,0,1:T(8,128)} %reshape.374), kind=kOutput, calls=%fused_computation.16 | convolution fusion | flops 736100352 | bytes 5259264 | tf_op jit(solution)/shard_map/rcbl,rdbl->bcd/dot_general | solution.py:62
  50.9 0.9 reshape.375
  51.8 3.7 %copy.17 = f32[16,8,6,8,6]{0,3,4,2,1:T(8,128)} copy(f32[16,8,6,8,6]{4,3,2,1,0:T(8,128)S(1)} %reshape.375) | data formatting | bytes 294912 | tf_op jit(solution)/shard_map/reshape | solution.py:67
  55.5 1.9 convolution_bitcast_fusion.1
  57.4 1.5 copy.18
  58.9 1.2 reshape.366
  60.1 0.5 fusion.16
  60.6 3.3 %collective-permute-start = (f32[256,288]{0,1:T(8,128)S(1)}, f32[256,288]{0,1:T(8,128)S(1)}, u32[]{:S(2)}, u32[]{:S(2)}) collective-permute-start(f32[256,288]{0,1:T(8,128)S(1)} %constant_dynamic-slice_fusion.1), channel_id=1, source_target_pairs={{0,2},{1,3},{2,0},{3,1},{4,6},{5,7},{6,4},{7,5},{8,10},{9,11},{10,... | collective-permute-start | bytes 884744 | tf_op jit(solution)/shard_map/ppermute | solution.py:108
  63.9 7.1 %collective-permute-done = f32[256,288]{0,1:T(8,128)S(1)} collective-permute-done((f32[256,288]{0,1:T(8,128)S(1)}, f32[256,288]{0,1:T(8,128)S(1)}, u32[]{:S(2)}, u32[]{:S(2)}) %collective-permute-start) | collective-permute-done | bytes 294944 | tf_op jit(solution)/shard_map/ppermute | solution.py:108
  71.0 1.7 collective-permute-start.1
  72.7 3.6 %collective-permute-done.1 = f32[128,288]{0,1:T(8,128)S(1)} collective-permute-done((f32[128,288]{0,1:T(8,128)S(1)}, f32[128,288]{0,1:T(8,128)S(1)}, u32[]{:S(2)}, u32[]{:S(2)}) %collective-permute-start.1) | collective-permute-done | bytes 147488 | tf_op jit(solution)/shard_map/ppermute | solution.py:108
  76.4 1.4 collective-permute-done.2
  77.7 0.2 collective-permute-start.3
  77.9 5.8 %collective-permute-done.3 = f32[128,288]{0,1:T(8,128)S(1)} collective-permute-done((f32[128,288]{0,1:T(8,128)S(1)}, f32[128,288]{0,1:T(8,128)S(1)}, u32[]{:S(2)}, u32[]{:S(2)}) %collective-permute-start.3) | collective-permute-done | bytes 147488 | tf_op jit(solution)/shard_map/ppermute | solution.py:118
  83.7 3.1 collective-permute-start.4
  86.8 3.7 %collective-permute-done.4 = f32[128,288]{0,1:T(8,128)S(1)} collective-permute-done((f32[128,288]{0,1:T(8,128)S(1)}, f32[128,288]{0,1:T(8,128)S(1)}, u32[]{:S(2)}, u32[]{:S(2)}) %collective-permute-start.4) | collective-permute-done | bytes 147488 | tf_op jit(solution)/shard_map/ppermute | solution.py:118
  90.5 0.9 collective-permute-start.5
  91.4 5.3 %collective-permute-done.5 = f32[128,288]{0,1:T(8,128)S(1)} collective-permute-done((f32[128,288]{0,1:T(8,128)S(1)}, f32[128,288]{0,1:T(8,128)S(1)}, u32[]{:S(2)}, u32[]{:S(2)}) %collective-permute-start.5) | collective-permute-done | bytes 147488 | tf_op jit(solution)/shard_map/ppermute | solution.py:118
  96.7 0.5 collective-permute-start.6
  97.2 6.2 %collective-permute-done.6 = f32[128,288]{0,1:T(8,128)S(1)} collective-permute-done((f32[128,288]{0,1:T(8,128)S(1)}, f32[128,288]{0,1:T(8,128)S(1)}, u32[]{:S(2)}, u32[]{:S(2)}) %collective-permute-start.6) | collective-permute-done | bytes 147488 | tf_op jit(solution)/shard_map/ppermute | solution.py:118
  103.5 2.2 copy.19
  105.7 3.7 %convolution_bitcast_fusion = f32[128,6,128,6]{0,1,3,2:T(8,128)S(1)} fusion(f32[128,8,6,6]{1,3,2,0:T(8,128)} %copy.19), kind=kOutput, calls=%fused_computation.13 | convolution fusion | flops 56885248 | bytes 2506752 | tf_op jit(solution)/shard_map/kdef,kdm->mfke/dot_general | solution.py:94
  109.4 24.0 %copy.20 = f32[128,6,128,6]{3,2,1,0:T(8,128)} copy(f32[128,6,128,6]{0,1,3,2:T(8,128)S(1)} %convolution_bitcast_fusion) | data formatting | bytes 4718592 | tf_op jit(solution)/shard_map/kdef,kdm->mfke/transpose | solution.py:94
  133.5 35.7 %reshape.368 = f32[768,768]{1,0:T(8,128)S(1)} reshape(f32[128,6,128,6]{3,2,1,0:T(8,128)} %copy.20) | data formatting | bytes 4718592 | tf_op jit(solution)/shard_map/reshape | solution.py:95
  169.2 0.2 select_add_fusion
  169.4 1.4 copy-done
  170.9 11.7 %cholesky.164 = f32[128,128]{1,0:T(8,128)S(1)} custom-call(f32[128,128]{1,0:T(8,128)S(1)} %cholesky.421), custom_call_target="Cholesky" | custom-call | tf_op jit(solution)/shard_map/cholesky | solution.py:132
  182.6 9.8 %custom-call.32 = f32[1,128,128]{1,2,0:T(8,128)S(1)} custom-call(f32[1,128,128]{2,1,0:T(8,128)S(1)} %get-tuple-element.32), custom_call_target="InvertDiagBlocksLowerTriangular" | custom-call | tf_op jit(solution)/shard_map/cholesky | solution.py:132
  192.6 1.4 constant_dynamic-update-slice_fusion
  194.0 1.4 convolution_subtract_fusion
  195.4 11.7 %cholesky.187 = f32[128,128]{1,0:T(8,128)S(1)} custom-call(f32[128,128]{1,0:T(8,128)S(1)} %cholesky.425), custom_call_target="Cholesky" | custom-call | tf_op jit(solution)/shard_map/cholesky | solution.py:132
  207.1 10.0 %custom-call.33 = f32[1,128,128]{1,2,0:T(8,128)S(1)} custom-call(f32[1,128,128]{2,1,0:T(8,128)S(1)} %get-tuple-element.29), custom_call_target="InvertDiagBlocksLowerTriangular" | custom-call | tf_op jit(solution)/shard_map/cholesky | solution.py:132
  217.1 0.4 convolution_dynamic-update-slice_fusion
  217.5 1.5 convolution_subtract_fusion.1
  219.1 11.7 %cholesky.352 = f32[128,128]{1,0:T(8,128)S(1)} custom-call(f32[128,128]{1,0:T(8,128)S(1)} %cholesky.430), custom_call_target="Cholesky" | custom-call | tf_op jit(solution)/shard_map/cholesky | solution.py:132
  230.8 0.7 compare_reduce_fusion.3
  231.5 9.8 %custom-call.34 = f32[1,128,128]{1,2,0:T(8,128)S(1)} custom-call(f32[1,128,128]{2,1,0:T(8,128)S(1)} %get-tuple-element.26), custom_call_target="InvertDiagBlocksLowerTriangular" | custom-call | tf_op jit(solution)/shard_map/cholesky | solution.py:132
  241.3 0.3 convolution_dynamic-update-slice_fusion.1
  241.7 1.6 convolution_subtract_fusion.2
  243.2 12.1 %cholesky.371 = f32[128,128]{1,0:T(8,128)S(1)} custom-call(f32[128,128]{1,0:T(8,128)S(1)} %cholesky.435), custom_call_target="Cholesky" | custom-call | tf_op jit(solution)/shard_map/cholesky | solution.py:132
  255.4 0.6 compare_reduce_fusion.2
  256.0 9.8 %custom-call.35 = f32[1,128,128]{1,2,0:T(8,128)S(1)} custom-call(f32[1,128,128]{2,1,0:T(8,128)S(1)} %get-tuple-element.23), custom_call_target="InvertDiagBlocksLowerTriangular" | custom-call | tf_op jit(solution)/shard_map/cholesky | solution.py:132
  265.8 0.3 convolution_dynamic-update-slice_fusion.2
  266.1 1.5 convolution_subtract_fusion.3
  267.6 11.7 %cholesky.390 = f32[128,128]{1,0:T(8,128)S(1)} custom-call(f32[128,128]{1,0:T(8,128)S(1)} %cholesky.440), custom_call_target="Cholesky" | custom-call | tf_op jit(solution)/shard_map/cholesky | solution.py:132
  279.3 0.7 compare_reduce_fusion.1
  280.0 9.8 %custom-call.36 = f32[1,128,128]{1,2,0:T(8,128)S(1)} custom-call(f32[1,128,128]{2,1,0:T(8,128)S(1)} %get-tuple-element.20), custom_call_target="InvertDiagBlocksLowerTriangular" | custom-call | tf_op jit(solution)/shard_map/cholesky | solution.py:132
  289.8 0.2 convolution_dynamic-update-slice_fusion.3
  290.0 1.3 convolution_subtract_fusion.4
  291.3 11.9 %cholesky.408 = f32[128,128]{1,0:T(8,128)S(1)} custom-call(f32[128,128]{1,0:T(8,128)S(1)} %convolution_subtract_fusion.4), custom_call_target="Cholesky" | custom-call | tf_op jit(solution)/shard_map/cholesky | solution.py:132
  303.3 0.7 compare_reduce_fusion
  304.0 0.7 compare_reduce_fusion.4
  308.4 1.6 select_bitcast_fusion
  310.0 3.0 copy.21
  (76 shorter events, 2.3 us)
Async XLA Ops:
  0.0 2.1 copy-start.1
  2.3 0.7 copy-start.6
  2.4 0.8 copy-start.3
  2.4 0.9 copy-start.4
  2.5 1.2 copy-start.2
  60.6 10.3 %collective-permute-start = (f32[256,288]{0,1:T(8,128)S(1)}, f32[256,288]{0,1:T(8,128)S(1)}, u32[]{:S(2)}, u32[]{:S(2)}) collective-permute-start(f32[256,288]{0,1:T(8,128)S(1)} %constant_dynamic-slice_fusion.1), channel_id=1, source_target_pairs={{0,2},{1,3},{2,0},{3,1},{4,6},{5,7},{6,4},{7,5},{8,10},{9,11},{10,... | collective-permute-start | bytes 884744 | tf_op jit(solution)/shard_map/ppermute | solution.py:108
  71.0 5.2 %collective-permute-start.1 = (f32[128,288]{0,1:T(8,128)S(1)}, f32[128,288]{0,1:T(8,128)S(1)}, u32[]{:S(2)}, u32[]{:S(2)}) collective-permute-start(f32[128,288]{0,1:T(8,128)S(1)} %constant_dynamic-slice_fusion), channel_id=1, source_target_pairs={{0,1},{1,0},{2,3},{3,2},{4,5},{5,4},{6,7},{7,6},{8,9},{9,8},{10,11... | collective-permute-start | bytes 442376 | tf_op jit(solution)/shard_map/ppermute | solution.py:108
  76.3 1.5 collective-permute-start.2
  77.7 6.0 %collective-permute-start.3 = (f32[128,288]{0,1:T(8,128)S(1)}, f32[128,288]{0,1:T(8,128)S(1)}, u32[]{:S(2)}, u32[]{:S(2)}) collective-permute-start(f32[128,288]{0,1:T(8,128)S(1)} %add.250), channel_id=1, source_target_pairs={{0,8},{4,12},{8,0},{12,4},{16,24},{20,28},{24,16},{28,20},{32,40},... | collective-permute-start | bytes 442376 | tf_op jit(solution)/shard_map/ppermute | solution.py:118
  83.7 6.7 %collective-permute-start.4 = (f32[128,288]{0,1:T(8,128)S(1)}, f32[128,288]{0,1:T(8,128)S(1)}, u32[]{:S(2)}, u32[]{:S(2)}) collective-permute-start(f32[128,288]{0,1:T(8,128)S(1)} %add.251), channel_id=1, source_target_pairs={{0,16},{4,20},{8,24},{12,28},{16,0},{20,4},{24,8},{28,12},{32,48},... | collective-permute-start | bytes 442376 | tf_op jit(solution)/shard_map/ppermute | solution.py:118
  90.5 6.2 %collective-permute-start.5 = (f32[128,288]{0,1:T(8,128)S(1)}, f32[128,288]{0,1:T(8,128)S(1)}, u32[]{:S(2)}, u32[]{:S(2)}) collective-permute-start(f32[128,288]{0,1:T(8,128)S(1)} %add.252), channel_id=1, source_target_pairs={{0,32},{4,36},{8,40},{12,44},{16,48},{20,52},{24,56},{28,60},{32,0... | collective-permute-start | bytes 442376 | tf_op jit(solution)/shard_map/ppermute | solution.py:118
  96.7 6.7 %collective-permute-start.6 = (f32[128,288]{0,1:T(8,128)S(1)}, f32[128,288]{0,1:T(8,128)S(1)}, u32[]{:S(2)}, u32[]{:S(2)}) collective-permute-start(f32[128,288]{0,1:T(8,128)S(1)} %add.253), channel_id=1, source_target_pairs={{0,64},{4,68},{8,72},{12,76},{16,80},{20,84},{24,88},{28,92},{32,9... | collective-permute-start | bytes 442376 | tf_op jit(solution)/shard_map/ppermute | solution.py:118
  133.5 35.7 %copy-start.5 = (f32[768]{0:T(1024)S(1)}, f32[768]{0:T(1024)}, u32[]{:S(2)}) copy-start(f32[768]{0:T(1024)} %param.13) | copy-start | bytes 9220
  169.4 1.4 copy-start

commit v3 on v2

--- a/solution.py
+++ b/solution.py
@@ -2,9 +2,14 @@
 import jax.numpy as jnp
 from jax import lax
 from jax.sharding import PartitionSpec as P
+from jax.experimental import pallas as pl
+from jax.experimental.pallas import tpu as pltpu
+import functools
 
 KDOF = 6
 WIN_KNOTS = 8
+PANEL = 8
+WIDTH = 256
 
 
 def basis_weights(knot_frac):
@@ -95,6 +100,74 @@
     return lower.reshape(group_cols, group_cols)
 
 
+def band_chol_kernel(n, band_w, yt_ref, out_ref, w_ref, r_ref, u_ref):
+    w_ref[...] = jnp.zeros_like(w_ref)
+    r_ref[...] = jnp.zeros_like(r_ref)
+    lanes = lax.broadcasted_iota(jnp.int32, (band_w, WIDTH), 1)
+    for k in range(n // KDOF):
+        lo = KDOF * k
+        tile = (lo // 128) * 128
+        blk = yt_ref[:, tile:tile + WIDTH]
+        keep = (lanes >= lo - tile) & (lanes < lo - tile + KDOF)
+        w_ref[lo:lo + band_w, tile:tile + WIDTH] += jnp.where(keep, blk, 0.0)
+    tiles = n // 128
+    ri = lax.broadcasted_iota(jnp.int32, (128, 128), 0)
+    ci = lax.broadcasted_iota(jnp.int32, (128, 128), 1)
+    for a in range(tiles):
+        for b in (a, a + 1):
+            if b >= tiles:
+                continue
+            low = w_ref[128 * a:128 * a + 128, 128 * b:128 * b + 128]
+            mirror = w_ref[128 * b:128 * b + 128, 128 * a:128 * a + 128].T
+            upper = (ci + 128 * b) // KDOF > (ri + 128 * a) // KDOF
+            w_ref[128 * a:128 * a + 128, 128 * b:128 * b + 128] = jnp.where(upper, mirror, low)
+
+    lane = lax.broadcasted_iota(jnp.int32, (PANEL, WIDTH), 1)
+    row = lax.broadcasted_iota(jnp.int32, (PANEL, 1), 0)
+
+    def panel(p, carry):
+        j0 = pl.multiple_of(p * PANEL, PANEL)
+        base = pl.multiple_of((p // (128 // PANEL)) * 128, 128)
+        off = j0 - base
+        blk = w_ref[pl.ds(j0, PANEL), pl.ds(base, WIDTH)]
+        out_rows = []
+        for t in range(PANEL):
+            jt = off + t
+            col = jnp.sum(jnp.where(lane == jt, blk, 0.0), axis=1, keepdims=True)
+            inv = lax.rsqrt(col[t:t + 1, :])
+            rrow = jnp.where(lane[0:1, :] >= jt, blk[t:t + 1, :] * inv, 0.0)
+            out_rows.append(rrow)
+            mult = jnp.where(row > t, col * inv, 0.0)
+            blk = blk - mult * rrow
+        rp = jnp.concatenate(out_rows, axis=0)
+        r_ref[pl.ds(j0, PANEL), pl.ds(base, WIDTH)] = rp
+        u_ref[...] = jnp.dot(rp.T, rp, precision=lax.Precision.HIGHEST, preferred_element_type=jnp.float32)
+        start = pl.multiple_of(j0 + PANEL, PANEL)
+        trail = w_ref[pl.ds(start, band_w), pl.ds(base, WIDTH)]
+        w_ref[pl.ds(start, band_w), pl.ds(base, WIDTH)] = trail - u_ref[pl.ds(off + PANEL, band_w), :]
+        return carry
+
+    lax.fori_loop(0, n // PANEL, panel, 0)
+    out_ref[...] = r_ref[0:n, 0:n]
+
+
+def band_cholesky(yt, n):
+    band_w = yt.shape[0]
+    padded = n + 128
+    yt = jnp.pad(yt, ((0, 0), (0, padded - n)))
+    return pl.pallas_call(
+        functools.partial(band_chol_kernel, n, band_w),
+        out_shape=jax.ShapeDtypeStruct((n, n), jnp.float32),
+        in_specs=[pl.BlockSpec(memory_space=pltpu.VMEM)],
+        out_specs=pl.BlockSpec(memory_space=pltpu.VMEM),
+        scratch_shapes=[
+            pltpu.VMEM((n + 64, padded), jnp.float32),
+            pltpu.VMEM((n, padded), jnp.float32),
+            pltpu.VMEM((WIDTH, WIDTH), jnp.float32),
+        ],
+    )(yt)
+
+
 def halve_over(band, axis):
     n = lax.axis_size(axis)
     c = lax.axis_index(axis)
@@ -128,9 +201,13 @@
     num_groups = lax.axis_size("cols")
     band = place_band(skew_blocks(grams), block_base, group_cols, num_groups)
     band_whole = butterfly_sum(halve_over(band, "cols"), "rows")
-    lower = band_to_lower(band_whole, group_cols) + jnp.diag(damping)
-    factors = lax.linalg.cholesky(lower, symmetrize_input=False).T
-    return factors
+    group_knots = group_cols // KDOF
+    yt = band_whole.reshape(group_knots, WIN_KNOTS, KDOF, KDOF).transpose(1, 3, 0, 2)
+    yt = yt.reshape(WIN_KNOTS * KDOF, group_cols)
+    t = lax.broadcasted_iota(jnp.int32, yt.shape, 0)
+    i = lax.broadcasted_iota(jnp.int32, yt.shape, 1)
+    yt = yt + jnp.where(t == i % KDOF, damping[None, :], 0.0)
+    return band_cholesky(yt, group_cols)
 
 
 def solution(mesh):

time: 320 us -> 220 us (0.69); the launches traced: 313 us -> 219 us
  other arithmetic: 147 us -> 23.7 us
  Pallas kernels: 0 us -> 111 us
  local copies, waits for them, and re-layouts: 91.1 us -> 27.1 us
  matrix products: 27.8 us -> 14.3 us
  between operations: 4.62 us -> 0.5 us
    another operation x22 -> x0, other arithmetic: 124 us -> none  [local(): factors = lax.linalg.cholesky(lower, symmetrize_input=False).T]
    pallas_call x0 -> x1, Pallas kernels: none -> 111 us  [band_cholesky(): pl.pallas_call(functools.partial(band_chol_kernel, n, band_w), out_shape=...]
    reshape x3 -> x2, local copies, waits for them, and re-layouts: 38 us -> 2.14 us  [the longest x1 2.12 us: local(): yt = yt.reshape(WIN_KNOTS * KDOF, group_cols)]
    transpose x2 -> x1, local copies, waits for them, and re-layouts: 27.1 us -> 1.05 us  [local(): band_whole.reshape(group_knots, WIN_KNOTS, KDOF, KDOF).transpose(1, 3, 0, 2)]
    another operation x10 -> x0, matrix products: 9.82 us -> none  [local(): factors = lax.linalg.cholesky(lower, symmetrize_input=False).T]
    dot_general x1 -> x0, matrix products: 3.67 us -> none  [band_to_lower(): jnp.einsum('kdef,kdm->mfke', band4, spread, precision=lax.Precision.HIGHEST)]
where the time goes in v3:
time: 220 us; the launch traced here: 219 us
  Pallas kernels  111 us (50%)
  waiting for transfers between devices  33 us (15%)
  local copies, waits for them, and re-layouts  27.1 us (12%)
  other arithmetic  23.7 us (11%)
  matrix products  14.3 us (6%)
  starting transfers between devices  9.64 us (4%)
    pallas_call x1, Pallas kernels, band_cholesky(): pl.pallas_call(functools.partial(band_chol_kernel, n, band_w), out_shape=...  111 us
    ppermute x5, waiting for transfers between devices, butterfly_sum(): band = band + lax.ppermute(band, axis, [(i, i ^ s) for i in range(n)])  22.4 us
    dot_general x1, matrix products, block_grams(): jnp.einsum('rcbl,rdbl->bcd', shaped, shaped, precision=lax.Precision.HIGH...  11.9 us
    ppermute x2, waiting for transfers between devices, halve_over(): band = keep + lax.ppermute(send, axis, [(i, i ^ s) for i in range(n)])  10.6 us
    reduce_sum x4, other arithmetic, reflect(): projection = jnp.sum(vector[:, None, :] * lower_rows, axis=0)  8.98 us
    mul x2, local copies, waits for them, and re-layouts, reduce_rows(): knot_weight[:, None, :, None, :] * pose_rows  8.9 us
    reshape x1, local copies, waits for them, and re-layouts, block_grams(): reduced.reshape(red_rows, win_width, num_blocks, landmarks // num_blocks)  6.97 us
    mul x1, other arithmetic, reduce_rows(): knot_weight[:, None, :, None, :] * pose_rows  6.76 us
  transfers between devices with their start and end apart: 7, of which 7 were waited for; matrix products, arithmetic and copies ran while one was open for 0% of the time, Pallas kernels for 0%

profile of v3, /device:TPU:38, one launch (start us, length us, event | category | flops | bytes accessed | tf_op | source)
XLA Modules:
  0.0 219.5 jit_solution(16075074512397953485)
XLA Ops:
  0.0 0.0 copy-start.4
  0.0 0.0 copy-start.1
  0.0 0.0 copy-start.2
  0.0 0.0 copy-start
  0.0 0.8 fusion.20
  0.9 0.1 mul.341
  1.0 1.0 broadcast_multiply_fusion.2
  2.2 1.1 multiply_reduce_fusion.4
  3.2 0.1 mul.357
  3.4 1.1 multiply_subtract_fusion.1
  4.7 0.1 multiply_reduce_fusion.3
  4.8 0.1 multiply_subtract_fusion
  5.0 0.0 copy-done.4
  5.0 0.1 iota_add_fusion
  5.1 0.0 copy-done.1
  5.1 0.0 copy-done.2
  5.4 0.0 copy-done
  5.4 0.1 broadcast_multiply_fusion.1
  5.4 0.5 mul.344
  5.9 0.2 select_add_fusion
  6.1 6.8 %broadcast_multiply_fusion = (f32[8,2,8,6,2048]{4,1,0,3,2:T(2,128)}, f32[8,6,2048]{2,1,0:T(8,128)S(1)}) fusion(f32[8,2,6,2048]{3,1,0,2:T(2,128)S(1)} %mul.344, f32[8,8,2048]{2,0,1:T(8,128)S(1)} %select_add_fusion, f32[8,2,2048]{2,1,0:T(2,128)S(1)} %mul.357), kind=kLoop, calls=%fused_computation.8 | loop fusion | flops 4620288 | bytes 8126464 | tf_op jit(solution)/shard_map/mul | solution.py:42
  12.9 8.4 %mul.347 = f32[16,48,2048]{2,0,1:T(8,128)} reshape(f32[8,2,8,6,2048]{4,1,0,3,2:T(2,128)} %get-tuple-element.15) | data formatting | bytes 12582912 | tf_op jit(solution)/shard_map/mul | solution.py:42
  21.3 0.1 mul.360
  21.4 5.1 %multiply_reduce_fusion.1 = (f32[48,2048]{1,0:T(8,128)S(1)}, f32[15,48,2048]{2,0,1:T(8,128)S(1)}) fusion(f32[15,2048]{1,0:T(8,128)S(1)} %get-tuple-element.10, f32[48,2048]{1,0:T(8,128)S(1)} %mul.360, f32[15,2048]{1,0:T(8,128)S(1)} %slice.79, f32[16,48,2048]{2,0,1:T(8,128)} %mul.347), kind=kLoop, calls=%fused_computation.4 | loop fusion | flops 5799936 | bytes 12828672 | tf_op jit(solution)/shard_map/reduce_sum | solution.py:55
  26.5 2.7 %multiply_reduce_fusion = (f32[48,2048]{1,0:T(8,128)S(1)}, f32[14,48,2048]{2,0,1:T(8,128)S(1)}) fusion(f32[14,2048]{1,0:T(8,128)S(1)} %get-tuple-element.6, f32[48,2048]{1,0:T(8,128)S(1)} %get-tuple-element.11, f32[14,2048]{1,0:T(8,128)S(1)} %slice.84, f32[15,48,2048]{2,0,1:T(8,128)S(1)} %get-tuple-element.12), kind=kLoop, calls=%fused_computation.3 | loop fusion | flops 5406720 | bytes 12025856 | tf_op jit(solution)/shard_map/reduce_sum | solution.py:55
  29.2 4.0 %slice_subtract_fusion = f32[13,48,2048]{2,0,1:T(8,128)} fusion(f32[14,48,2048]{2,0,1:T(8,128)S(1)} %get-tuple-element.8, f32[48,2048]{1,0:T(8,128)S(1)} %get-tuple-element.7, f32[13,2048]{1,0:T(8,128)S(1)} %slice.90), kind=kLoop, calls=%fused_computation | loop fusion | flops 2555904 | bytes 10723328 | tf_op jit(solution)/shard_map/sub | solution.py:56
  33.2 7.0 %reshape.338 = f32[13,48,16,128]{3,2,0,1:T(8,128)} reshape(f32[13,48,2048]{2,0,1:T(8,128)} %slice_subtract_fusion) | data formatting | bytes 10223616 | tf_op jit(solution)/shard_map/reshape | solution.py:66
  40.1 11.9 %fusion.2 = f32[16,48,48]{2,1,0:T(8,128)S(1)} fusion(f32[13,48,16,128]{3,2,0,1:T(8,128)} %reshape.338), kind=kOutput, calls=%fused_computation.10 | convolution fusion | flops 736100352 | bytes 5259264 | tf_op jit(solution)/shard_map/rcbl,rdbl->bcd/dot_general | solution.py:67
  52.1 0.9 reshape.339
  53.0 3.7 %copy.15 = f32[16,8,6,8,6]{0,3,4,2,1:T(8,128)} copy(f32[16,8,6,8,6]{4,3,2,1,0:T(8,128)S(1)} %reshape.339) | data formatting | bytes 294912 | tf_op jit(solution)/shard_map/reshape | solution.py:72
  56.7 1.9 convolution_bitcast_fusion
  58.6 1.2 copy.16
  59.8 1.2 reshape.333
  61.0 0.0 copy-start.3
  61.0 0.5 fusion.6
  61.5 3.3 %collective-permute-start = (f32[256,288]{0,1:T(8,128)S(1)}, f32[256,288]{0,1:T(8,128)S(1)}, u32[]{:S(2)}, u32[]{:S(2)}) collective-permute-start(f32[256,288]{0,1:T(8,128)S(1)} %constant_dynamic-slice_fusion.1), channel_id=1, source_target_pairs={{0,2},{1,3},{2,0},{3,1},{4,6},{5,7},{6,4},{7,5},{8,10},{9,11},{10,... | collective-permute-start | bytes 884744 | tf_op jit(solution)/shard_map/ppermute | solution.py:181
  64.8 7.1 %collective-permute-done = f32[256,288]{0,1:T(8,128)S(1)} collective-permute-done((f32[256,288]{0,1:T(8,128)S(1)}, f32[256,288]{0,1:T(8,128)S(1)}, u32[]{:S(2)}, u32[]{:S(2)}) %collective-permute-start) | collective-permute-done | bytes 294944 | tf_op jit(solution)/shard_map/ppermute | solution.py:181
  71.9 1.7 collective-permute-start.1
  73.6 3.6 %collective-permute-done.1 = f32[128,288]{0,1:T(8,128)S(1)} collective-permute-done((f32[128,288]{0,1:T(8,128)S(1)}, f32[128,288]{0,1:T(8,128)S(1)}, u32[]{:S(2)}, u32[]{:S(2)}) %collective-permute-start.1) | collective-permute-done | bytes 147488 | tf_op jit(solution)/shard_map/ppermute | solution.py:181
  77.1 0.1 collective-permute-start.2
  77.2 1.4 collective-permute-done.2
  78.6 0.2 collective-permute-start.3
  78.8 5.8 %collective-permute-done.3 = f32[128,288]{0,1:T(8,128)S(1)} collective-permute-done((f32[128,288]{0,1:T(8,128)S(1)}, f32[128,288]{0,1:T(8,128)S(1)}, u32[]{:S(2)}, u32[]{:S(2)}) %collective-permute-start.3) | collective-permute-done | bytes 147488 | tf_op jit(solution)/shard_map/ppermute | solution.py:191
  84.6 3.1 %collective-permute-start.4 = (f32[128,288]{0,1:T(8,128)S(1)}, f32[128,288]{0,1:T(8,128)S(1)}, u32[]{:S(2)}, u32[]{:S(2)}) collective-permute-start(f32[128,288]{0,1:T(8,128)S(1)} %add.215), channel_id=1, source_target_pairs={{0,16},{4,20},{8,24},{12,28},{16,0},{20,4},{24,8},{28,12},{32,48},... | collective-permute-start | bytes 442376 | tf_op jit(solution)/shard_map/ppermute | solution.py:191
  87.7 3.7 %collective-permute-done.4 = f32[128,288]{0,1:T(8,128)S(1)} collective-permute-done((f32[128,288]{0,1:T(8,128)S(1)}, f32[128,288]{0,1:T(8,128)S(1)}, u32[]{:S(2)}, u32[]{:S(2)}) %collective-permute-start.4) | collective-permute-done | bytes 147488 | tf_op jit(solution)/shard_map/ppermute | solution.py:191
  91.4 0.9 collective-permute-start.5
  92.3 5.3 %collective-permute-done.5 = f32[128,288]{0,1:T(8,128)S(1)} collective-permute-done((f32[128,288]{0,1:T(8,128)S(1)}, f32[128,288]{0,1:T(8,128)S(1)}, u32[]{:S(2)}, u32[]{:S(2)}) %collective-permute-start.5) | collective-permute-done | bytes 147488 | tf_op jit(solution)/shard_map/ppermute | solution.py:191
  97.6 0.5 collective-permute-start.6
  98.1 6.2 %collective-permute-done.6 = f32[128,288]{0,1:T(8,128)S(1)} collective-permute-done((f32[128,288]{0,1:T(8,128)S(1)}, f32[128,288]{0,1:T(8,128)S(1)}, u32[]{:S(2)}, u32[]{:S(2)}) %collective-permute-start.6) | collective-permute-done | bytes 147488 | tf_op jit(solution)/shard_map/ppermute | solution.py:191
  104.4 1.1 copy.17
  105.5 2.1 reshape.335
  107.6 0.0 copy-done.3
  107.6 0.7 pad.4.yt_ref
  108.3 111.2 %shard_map.73 = f32[768,768]{1,0:T(8,128)} custom-call(f32[48,896]{1,0:T(8,128)} %pad.4.yt_ref), custom_call_target="tpu_custom_call" | custom-call | tf_op jit(solution)/shard_map/pallas_call | solution.py:158
  (44 shorter events, 0.9 us)
Async XLA Ops:
  0.0 5.0 %copy-start.4 = (s32[16]{0:T(128)S(1)}, s32[16]{0:T(128)}, u32[]{:S(2)}) copy-start(s32[16]{0:T(128)} %param.12) | copy-start | bytes 196
  0.0 5.1 %copy-start.1 = (s32[8,2048]{1,0:T(8,128)S(1)}, s32[8,2048]{1,0:T(8,128)}, u32[]{:S(2)}) copy-start(s32[8,2048]{1,0:T(8,128)} %param.9) | copy-start | bytes 196612
  0.0 5.1 %copy-start.2 = (f32[8,2048]{1,0:T(8,128)S(1)}, f32[8,2048]{1,0:T(8,128)}, u32[]{:S(2)}) copy-start(f32[8,2048]{1,0:T(8,128)} %param.10) | copy-start | bytes 196612
  0.0 5.4 %copy-start = (f32[16,6,2048]{2,0,1:T(8,128)S(1)}, f32[16,6,2048]{2,0,1:T(8,128)}, u32[]{:S(2)}) copy-start(f32[16,6,2048]{2,0,1:T(8,128)} %param.8) | copy-start | bytes 2359300
  61.0 46.6 %copy-start.3 = (f32[768]{0:T(1024)S(1)}, f32[768]{0:T(1024)}, u32[]{:S(2)}) copy-start(f32[768]{0:T(1024)} %param.13) | copy-start | bytes 9220
  61.5 10.3 %collective-permute-start = (f32[256,288]{0,1:T(8,128)S(1)}, f32[256,288]{0,1:T(8,128)S(1)}, u32[]{:S(2)}, u32[]{:S(2)}) collective-permute-start(f32[256,288]{0,1:T(8,128)S(1)} %constant_dynamic-slice_fusion.1), channel_id=1, source_target_pairs={{0,2},{1,3},{2,0},{3,1},{4,6},{5,7},{6,4},{7,5},{8,10},{9,11},{10,... | collective-permute-start | bytes 884744 | tf_op jit(solution)/shard_map/ppermute | solution.py:181
  71.9 5.2 %collective-permute-start.1 = (f32[128,288]{0,1:T(8,128)S(1)}, f32[128,288]{0,1:T(8,128)S(1)}, u32[]{:S(2)}, u32[]{:S(2)}) collective-permute-start(f32[128,288]{0,1:T(8,128)S(1)} %constant_dynamic-slice_fusion), channel_id=1, source_target_pairs={{0,1},{1,0},{2,3},{3,2},{4,5},{5,4},{6,7},{7,6},{8,9},{9,8},{10,11... | collective-permute-start | bytes 442376 | tf_op jit(solution)/shard_map/ppermute | solution.py:181
  77.1 1.5 collective-permute-start.2
  78.6 6.0 %collective-permute-start.3 = (f32[128,288]{0,1:T(8,128)S(1)}, f32[128,288]{0,1:T(8,128)S(1)}, u32[]{:S(2)}, u32[]{:S(2)}) collective-permute-start(f32[128,288]{0,1:T(8,128)S(1)} %add.214), channel_id=1, source_target_pairs={{0,8},{4,12},{8,0},{12,4},{16,24},{20,28},{24,16},{28,20},{32,40},... | collective-permute-start | bytes 442376 | tf_op jit(solution)/shard_map/ppermute | solution.py:191
  84.6 6.7 %collective-permute-start.4 = (f32[128,288]{0,1:T(8,128)S(1)}, f32[128,288]{0,1:T(8,128)S(1)}, u32[]{:S(2)}, u32[]{:S(2)}) collective-permute-start(f32[128,288]{0,1:T(8,128)S(1)} %add.215), channel_id=1, source_target_pairs={{0,16},{4,20},{8,24},{12,28},{16,0},{20,4},{24,8},{28,12},{32,48},... | collective-permute-start | bytes 442376 | tf_op jit(solution)/shard_map/ppermute | solution.py:191
  91.4 6.2 %collective-permute-start.5 = (f32[128,288]{0,1:T(8,128)S(1)}, f32[128,288]{0,1:T(8,128)S(1)}, u32[]{:S(2)}, u32[]{:S(2)}) collective-permute-start(f32[128,288]{0,1:T(8,128)S(1)} %add.216), channel_id=1, source_target_pairs={{0,32},{4,36},{8,40},{12,44},{16,48},{20,52},{24,56},{28,60},{32,0... | collective-permute-start | bytes 442376 | tf_op jit(solution)/shard_map/ppermute | solution.py:191
  97.6 6.7 %collective-permute-start.6 = (f32[128,288]{0,1:T(8,128)S(1)}, f32[128,288]{0,1:T(8,128)S(1)}, u32[]{:S(2)}, u32[]{:S(2)}) collective-permute-start(f32[128,288]{0,1:T(8,128)S(1)} %add.217), channel_id=1, source_target_pairs={{0,64},{4,68},{8,72},{12,76},{16,80},{20,84},{24,88},{28,92},{32,9... | collective-permute-start | bytes 442376 | tf_op jit(solution)/shard_map/ppermute | solution.py:191

commit v4 on v3

--- a/solution.py
+++ b/solution.py
@@ -89,18 +89,7 @@
     return jnp.dot(onehot, flat, precision=lax.Precision.HIGHEST)
 
 
-def band_to_lower(band, group_cols):
-    group_knots = group_cols // KDOF
-    band4 = band.reshape(group_knots, WIN_KNOTS, KDOF, KDOF)
-    k = lax.broadcasted_iota(jnp.int32, (group_knots, WIN_KNOTS, group_knots), 0)
-    d = lax.broadcasted_iota(jnp.int32, (group_knots, WIN_KNOTS, group_knots), 1)
-    m = lax.broadcasted_iota(jnp.int32, (group_knots, WIN_KNOTS, group_knots), 2)
-    spread = (m == k + d).astype(jnp.float32)
-    lower = jnp.einsum("kdef,kdm->mfke", band4, spread, precision=lax.Precision.HIGHEST)
-    return lower.reshape(group_cols, group_cols)
-
-
-def band_chol_kernel(n, band_w, yt_ref, out_ref, w_ref, r_ref, u_ref):
+def band_chol_kernel(n, band_w, yt_ref, out_ref, w_ref, r_ref):
     w_ref[...] = jnp.zeros_like(w_ref)
     r_ref[...] = jnp.zeros_like(r_ref)
     lanes = lax.broadcasted_iota(jnp.int32, (band_w, WIDTH), 1)
@@ -122,14 +111,15 @@
             upper = (ci + 128 * b) // KDOF > (ri + 128 * a) // KDOF
             w_ref[128 * a:128 * a + 128, 128 * b:128 * b + 128] = jnp.where(upper, mirror, low)
 
-    lane = lax.broadcasted_iota(jnp.int32, (PANEL, WIDTH), 1)
-    row = lax.broadcasted_iota(jnp.int32, (PANEL, 1), 0)
+    rows = PANEL + band_w
+    lane = lax.broadcasted_iota(jnp.int32, (rows, WIDTH), 1)
+    row = lax.broadcasted_iota(jnp.int32, (rows, 1), 0)
 
     def panel(p, carry):
         j0 = pl.multiple_of(p * PANEL, PANEL)
         base = pl.multiple_of((p // (128 // PANEL)) * 128, 128)
         off = j0 - base
-        blk = w_ref[pl.ds(j0, PANEL), pl.ds(base, WIDTH)]
+        blk = w_ref[pl.ds(j0, rows), pl.ds(base, WIDTH)]
         out_rows = []
         for t in range(PANEL):
             jt = off + t
@@ -139,12 +129,9 @@
             out_rows.append(rrow)
             mult = jnp.where(row > t, col * inv, 0.0)
             blk = blk - mult * rrow
-        rp = jnp.concatenate(out_rows, axis=0)
-        r_ref[pl.ds(j0, PANEL), pl.ds(base, WIDTH)] = rp
-        u_ref[...] = jnp.dot(rp.T, rp, precision=lax.Precision.HIGHEST, preferred_element_type=jnp.float32)
+        r_ref[pl.ds(j0, PANEL), pl.ds(base, WIDTH)] = jnp.concatenate(out_rows, axis=0)
         start = pl.multiple_of(j0 + PANEL, PANEL)
-        trail = w_ref[pl.ds(start, band_w), pl.ds(base, WIDTH)]
-        w_ref[pl.ds(start, band_w), pl.ds(base, WIDTH)] = trail - u_ref[pl.ds(off + PANEL, band_w), :]
+        w_ref[pl.ds(start, band_w), pl.ds(base, WIDTH)] = blk[PANEL:, :]
         return carry
 
     lax.fori_loop(0, n // PANEL, panel, 0)
@@ -163,7 +150,6 @@
         scratch_shapes=[
             pltpu.VMEM((n + 64, padded), jnp.float32),
             pltpu.VMEM((n, padded), jnp.float32),
-            pltpu.VMEM((WIDTH, WIDTH), jnp.float32),
         ],
     )(yt)
 

time: 220 us -> 183 us (0.83)
  Pallas kernels: 111 us -> 74.4 us
    pallas_call x1, Pallas kernels: 111 us -> 74.4 us  [band_cholesky(): pl.pallas_call(functools.partial(band_chol_kernel, n, band_w), out_shape=...]
where the time goes in v4:
time: 183 us
  Pallas kernels  74.4 us (41%)
  waiting for transfers between devices  33 us (18%)
  local copies, waits for them, and re-layouts  27.1 us (15%)
  other arithmetic  23.7 us (13%)
  matrix products  14.3 us (8%)
  starting transfers between devices  9.64 us (5%)
    pallas_call x1, Pallas kernels, band_cholesky(): pl.pallas_call(functools.partial(band_chol_kernel, n, band_w), out_shape=...  74.4 us
    ppermute x5, waiting for transfers between devices, butterfly_sum(): band = band + lax.ppermute(band, axis, [(i, i ^ s) for i in range(n)])  22.4 us
    dot_general x1, matrix products, block_grams(): jnp.einsum('rcbl,rdbl->bcd', shaped, shaped, precision=lax.Precision.HIGH...  11.9 us
    ppermute x2, waiting for transfers between devices, halve_over(): band = keep + lax.ppermute(send, axis, [(i, i ^ s) for i in range(n)])  10.6 us
    reduce_sum x4, other arithmetic, reflect(): projection = jnp.sum(vector[:, None, :] * lower_rows, axis=0)  8.98 us
    mul x2, local copies, waits for them, and re-layouts, reduce_rows(): knot_weight[:, None, :, None, :] * pose_rows  8.9 us
    reshape x1, local copies, waits for them, and re-layouts, block_grams(): reduced.reshape(red_rows, win_width, num_blocks, landmarks // num_blocks)  6.97 us
    mul x1, other arithmetic, reduce_rows(): knot_weight[:, None, :, None, :] * pose_rows  6.76 us
  transfers between devices with their start and end apart: 7, of which 7 were waited for; matrix products, arithmetic and copies ran while one was open for 0% of the time, Pallas kernels for 0%

profile of v4, /device:TPU:38, one launch (start us, length us, event | category | flops | bytes accessed | tf_op | source)
XLA Modules:
  0.0 182.7 jit_solution(1794233387782490786)
XLA Ops:
  0.0 0.0 copy-start.4
  0.0 0.0 copy-start.1
  0.0 0.0 copy-start.2
  0.0 0.0 copy-start
  0.0 0.8 fusion.20
  0.9 0.1 mul.341
  1.0 1.0 broadcast_multiply_fusion.2
  2.2 1.1 multiply_reduce_fusion.4
  3.2 0.1 mul.357
  3.4 1.1 multiply_subtract_fusion.1
  4.7 0.1 multiply_reduce_fusion.3
  4.8 0.1 multiply_subtract_fusion
  5.0 0.0 copy-done.4
  5.0 0.1 iota_add_fusion
  5.1 0.0 copy-done.1
  5.1 0.0 copy-done.2
  5.4 0.0 copy-done
  5.4 0.1 broadcast_multiply_fusion.1
  5.4 0.5 mul.344
  5.9 0.2 select_add_fusion
  6.1 6.8 %broadcast_multiply_fusion = (f32[8,2,8,6,2048]{4,1,0,3,2:T(2,128)}, f32[8,6,2048]{2,1,0:T(8,128)S(1)}) fusion(f32[8,2,6,2048]{3,1,0,2:T(2,128)S(1)} %mul.344, f32[8,8,2048]{2,0,1:T(8,128)S(1)} %select_add_fusion, f32[8,2,2048]{2,1,0:T(2,128)S(1)} %mul.357), kind=kLoop, calls=%fused_computation.8 | loop fusion | flops 4620288 | bytes 8126464 | tf_op jit(solution)/shard_map/mul | solution.py:42
  12.9 8.4 %mul.347 = f32[16,48,2048]{2,0,1:T(8,128)} reshape(f32[8,2,8,6,2048]{4,1,0,3,2:T(2,128)} %get-tuple-element.15) | data formatting | bytes 12582912 | tf_op jit(solution)/shard_map/mul | solution.py:42
  21.3 0.1 mul.360
  21.4 5.1 %multiply_reduce_fusion.1 = (f32[48,2048]{1,0:T(8,128)S(1)}, f32[15,48,2048]{2,0,1:T(8,128)S(1)}) fusion(f32[15,2048]{1,0:T(8,128)S(1)} %get-tuple-element.10, f32[48,2048]{1,0:T(8,128)S(1)} %mul.360, f32[15,2048]{1,0:T(8,128)S(1)} %slice.79, f32[16,48,2048]{2,0,1:T(8,128)} %mul.347), kind=kLoop, calls=%fused_computation.4 | loop fusion | flops 5799936 | bytes 12828672 | tf_op jit(solution)/shard_map/reduce_sum | solution.py:55
  26.5 2.7 %multiply_reduce_fusion = (f32[48,2048]{1,0:T(8,128)S(1)}, f32[14,48,2048]{2,0,1:T(8,128)S(1)}) fusion(f32[14,2048]{1,0:T(8,128)S(1)} %get-tuple-element.6, f32[48,2048]{1,0:T(8,128)S(1)} %get-tuple-element.11, f32[14,2048]{1,0:T(8,128)S(1)} %slice.84, f32[15,48,2048]{2,0,1:T(8,128)S(1)} %get-tuple-element.12), kind=kLoop, calls=%fused_computation.3 | loop fusion | flops 5406720 | bytes 12025856 | tf_op jit(solution)/shard_map/reduce_sum | solution.py:55
  29.2 4.0 %slice_subtract_fusion = f32[13,48,2048]{2,0,1:T(8,128)} fusion(f32[14,48,2048]{2,0,1:T(8,128)S(1)} %get-tuple-element.8, f32[48,2048]{1,0:T(8,128)S(1)} %get-tuple-element.7, f32[13,2048]{1,0:T(8,128)S(1)} %slice.90), kind=kLoop, calls=%fused_computation | loop fusion | flops 2555904 | bytes 10723328 | tf_op jit(solution)/shard_map/sub | solution.py:56
  33.2 7.0 %reshape.338 = f32[13,48,16,128]{3,2,0,1:T(8,128)} reshape(f32[13,48,2048]{2,0,1:T(8,128)} %slice_subtract_fusion) | data formatting | bytes 10223616 | tf_op jit(solution)/shard_map/reshape | solution.py:66
  40.1 11.9 %fusion.2 = f32[16,48,48]{2,1,0:T(8,128)S(1)} fusion(f32[13,48,16,128]{3,2,0,1:T(8,128)} %reshape.338), kind=kOutput, calls=%fused_computation.10 | convolution fusion | flops 736100352 | bytes 5259264 | tf_op jit(solution)/shard_map/rcbl,rdbl->bcd/dot_general | solution.py:67
  52.1 0.9 reshape.339
  53.0 3.7 %copy.15 = f32[16,8,6,8,6]{0,3,4,2,1:T(8,128)} copy(f32[16,8,6,8,6]{4,3,2,1,0:T(8,128)S(1)} %reshape.339) | data formatting | bytes 294912 | tf_op jit(solution)/shard_map/reshape | solution.py:72
  56.7 1.9 %convolution_bitcast_fusion = f32[16,8,8,6,6]{0,2,4,3,1:T(8,128)S(1)} fusion(f32[16,8,6,8,6]{0,3,4,2,1:T(8,128)} %copy.15), kind=kOutput, calls=%fused_computation.9 | convolution fusion | flops 3539968 | bytes 294912 | tf_op jit(solution)/shard_map/bienf,ind->bidef/dot_general | solution.py:77
  58.6 1.2 copy.16
  59.8 1.2 reshape.333
  61.0 0.0 copy-start.3
  61.0 0.5 fusion.6
  61.5 3.3 %collective-permute-start = (f32[256,288]{0,1:T(8,128)S(1)}, f32[256,288]{0,1:T(8,128)S(1)}, u32[]{:S(2)}, u32[]{:S(2)}) collective-permute-start(f32[256,288]{0,1:T(8,128)S(1)} %constant_dynamic-slice_fusion.1), channel_id=1, source_target_pairs={{0,2},{1,3},{2,0},{3,1},{4,6},{5,7},{6,4},{7,5},{8,10},{9,11},{10,... | collective-permute-start | bytes 884744 | tf_op jit(solution)/shard_map/ppermute | solution.py:167
  64.8 7.1 %collective-permute-done = f32[256,288]{0,1:T(8,128)S(1)} collective-permute-done((f32[256,288]{0,1:T(8,128)S(1)}, f32[256,288]{0,1:T(8,128)S(1)}, u32[]{:S(2)}, u32[]{:S(2)}) %collective-permute-start) | collective-permute-done | bytes 294944 | tf_op jit(solution)/shard_map/ppermute | solution.py:167
  71.9 1.7 collective-permute-start.1
  73.6 3.6 %collective-permute-done.1 = f32[128,288]{0,1:T(8,128)S(1)} collective-permute-done((f32[128,288]{0,1:T(8,128)S(1)}, f32[128,288]{0,1:T(8,128)S(1)}, u32[]{:S(2)}, u32[]{:S(2)}) %collective-permute-start.1) | collective-permute-done | bytes 147488 | tf_op jit(solution)/shard_map/ppermute | solution.py:167
  77.1 0.1 collective-permute-start.2
  77.2 1.4 collective-permute-done.2
  78.6 0.2 collective-permute-start.3
  78.8 5.8 %collective-permute-done.3 = f32[128,288]{0,1:T(8,128)S(1)} collective-permute-done((f32[128,288]{0,1:T(8,128)S(1)}, f32[128,288]{0,1:T(8,128)S(1)}, u32[]{:S(2)}, u32[]{:S(2)}) %collective-permute-start.3) | collective-permute-done | bytes 147488 | tf_op jit(solution)/shard_map/ppermute | solution.py:177
  84.6 3.1 %collective-permute-start.4 = (f32[128,288]{0,1:T(8,128)S(1)}, f32[128,288]{0,1:T(8,128)S(1)}, u32[]{:S(2)}, u32[]{:S(2)}) collective-permute-start(f32[128,288]{0,1:T(8,128)S(1)} %add.215), channel_id=1, source_target_pairs={{0,16},{4,20},{8,24},{12,28},{16,0},{20,4},{24,8},{28,12},{32,48},... | collective-permute-start | bytes 442376 | tf_op jit(solution)/shard_map/ppermute | solution.py:177
  87.7 3.7 %collective-permute-done.4 = f32[128,288]{0,1:T(8,128)S(1)} collective-permute-done((f32[128,288]{0,1:T(8,128)S(1)}, f32[128,288]{0,1:T(8,128)S(1)}, u32[]{:S(2)}, u32[]{:S(2)}) %collective-permute-start.4) | collective-permute-done | bytes 147488 | tf_op jit(solution)/shard_map/ppermute | solution.py:177
  91.4 0.9 collective-permute-start.5
  92.3 5.3 %collective-permute-done.5 = f32[128,288]{0,1:T(8,128)S(1)} collective-permute-done((f32[128,288]{0,1:T(8,128)S(1)}, f32[128,288]{0,1:T(8,128)S(1)}, u32[]{:S(2)}, u32[]{:S(2)}) %collective-permute-start.5) | collective-permute-done | bytes 147488 | tf_op jit(solution)/shard_map/ppermute | solution.py:177
  97.6 0.5 collective-permute-start.6
  98.1 6.2 %collective-permute-done.6 = f32[128,288]{0,1:T(8,128)S(1)} collective-permute-done((f32[128,288]{0,1:T(8,128)S(1)}, f32[128,288]{0,1:T(8,128)S(1)}, u32[]{:S(2)}, u32[]{:S(2)}) %collective-permute-start.6) | collective-permute-done | bytes 147488 | tf_op jit(solution)/shard_map/ppermute | solution.py:177
  104.4 1.1 copy.17
  105.5 2.1 %reshape.335 = f32[48,768]{1,0:T(8,128)S(1)} reshape(f32[8,6,128,6]{3,2,1,0:T(8,128)S(1)} %copy.17) | data formatting | bytes 294912 | tf_op jit(solution)/shard_map/reshape | solution.py:192
  107.6 0.0 copy-done.3
  107.6 0.7 pad.4.yt_ref
  108.3 74.4 %shard_map.73 = f32[768,768]{1,0:T(8,128)} custom-call(f32[48,896]{1,0:T(8,128)} %pad.4.yt_ref), custom_call_target="tpu_custom_call" | custom-call | tf_op jit(solution)/shard_map/pallas_call | solution.py:145
  (44 shorter events, 0.9 us)
Async XLA Ops:
  0.0 5.0 %copy-start.4 = (s32[16]{0:T(128)S(1)}, s32[16]{0:T(128)}, u32[]{:S(2)}) copy-start(s32[16]{0:T(128)} %param.12) | copy-start | bytes 196
  0.0 5.1 %copy-start.1 = (s32[8,2048]{1,0:T(8,128)S(1)}, s32[8,2048]{1,0:T(8,128)}, u32[]{:S(2)}) copy-start(s32[8,2048]{1,0:T(8,128)} %param.9) | copy-start | bytes 196612
  0.0 5.1 %copy-start.2 = (f32[8,2048]{1,0:T(8,128)S(1)}, f32[8,2048]{1,0:T(8,128)}, u32[]{:S(2)}) copy-start(f32[8,2048]{1,0:T(8,128)} %param.10) | copy-start | bytes 196612
  0.0 5.4 %copy-start = (f32[16,6,2048]{2,0,1:T(8,128)S(1)}, f32[16,6,2048]{2,0,1:T(8,128)}, u32[]{:S(2)}) copy-start(f32[16,6,2048]{2,0,1:T(8,128)} %param.8) | copy-start | bytes 2359300
  61.0 46.6 %copy-start.3 = (f32[768]{0:T(1024)S(1)}, f32[768]{0:T(1024)}, u32[]{:S(2)}) copy-start(f32[768]{0:T(1024)} %param.13) | copy-start | bytes 9220
  61.5 10.3 %collective-permute-start = (f32[256,288]{0,1:T(8,128)S(1)}, f32[256,288]{0,1:T(8,128)S(1)}, u32[]{:S(2)}, u32[]{:S(2)}) collective-permute-start(f32[256,288]{0,1:T(8,128)S(1)} %constant_dynamic-slice_fusion.1), channel_id=1, source_target_pairs={{0,2},{1,3},{2,0},{3,1},{4,6},{5,7},{6,4},{7,5},{8,10},{9,11},{10,... | collective-permute-start | bytes 884744 | tf_op jit(solution)/shard_map/ppermute | solution.py:167
  71.9 5.2 %collective-permute-start.1 = (f32[128,288]{0,1:T(8,128)S(1)}, f32[128,288]{0,1:T(8,128)S(1)}, u32[]{:S(2)}, u32[]{:S(2)}) collective-permute-start(f32[128,288]{0,1:T(8,128)S(1)} %constant_dynamic-slice_fusion), channel_id=1, source_target_pairs={{0,1},{1,0},{2,3},{3,2},{4,5},{5,4},{6,7},{7,6},{8,9},{9,8},{10,11... | collective-permute-start | bytes 442376 | tf_op jit(solution)/shard_map/ppermute | solution.py:167
  77.1 1.5 collective-permute-start.2
  78.6 6.0 %collective-permute-start.3 = (f32[128,288]{0,1:T(8,128)S(1)}, f32[128,288]{0,1:T(8,128)S(1)}, u32[]{:S(2)}, u32[]{:S(2)}) collective-permute-start(f32[128,288]{0,1:T(8,128)S(1)} %add.214), channel_id=1, source_target_pairs={{0,8},{4,12},{8,0},{12,4},{16,24},{20,28},{24,16},{28,20},{32,40},... | collective-permute-start | bytes 442376 | tf_op jit(solution)/shard_map/ppermute | solution.py:177
  84.6 6.7 %collective-permute-start.4 = (f32[128,288]{0,1:T(8,128)S(1)}, f32[128,288]{0,1:T(8,128)S(1)}, u32[]{:S(2)}, u32[]{:S(2)}) collective-permute-start(f32[128,288]{0,1:T(8,128)S(1)} %add.215), channel_id=1, source_target_pairs={{0,16},{4,20},{8,24},{12,28},{16,0},{20,4},{24,8},{28,12},{32,48},... | collective-permute-start | bytes 442376 | tf_op jit(solution)/shard_map/ppermute | solution.py:177
  91.4 6.2 %collective-permute-start.5 = (f32[128,288]{0,1:T(8,128)S(1)}, f32[128,288]{0,1:T(8,128)S(1)}, u32[]{:S(2)}, u32[]{:S(2)}) collective-permute-start(f32[128,288]{0,1:T(8,128)S(1)} %add.216), channel_id=1, source_target_pairs={{0,32},{4,36},{8,40},{12,44},{16,48},{20,52},{24,56},{28,60},{32,0... | collective-permute-start | bytes 442376 | tf_op jit(solution)/shard_map/ppermute | solution.py:177
  97.6 6.7 %collective-permute-start.6 = (f32[128,288]{0,1:T(8,128)S(1)}, f32[128,288]{0,1:T(8,128)S(1)}, u32[]{:S(2)}, u32[]{:S(2)}) collective-permute-start(f32[128,288]{0,1:T(8,128)S(1)} %add.217), channel_id=1, source_target_pairs={{0,64},{4,68},{8,72},{12,76},{16,80},{20,84},{24,88},{28,92},{32,9... | collective-permute-start | bytes 442376 | tf_op jit(solution)/shard_map/ppermute | solution.py:177

commit v5 on v4

--- a/solution.py
+++ b/solution.py
@@ -12,64 +12,82 @@
 WIDTH = 256
 
 
-def basis_weights(knot_frac):
-    u_square = knot_frac * knot_frac
-    u_cubed = u_square * knot_frac
-    return (
-        (1.0 - knot_frac) ** 3 / 6.0,
+def gram_kernel(land_ref, pose_ref, seg_ref, frac_ref, len_ref, out_ref):
+    num_obs, lanes = seg_ref.shape
+    rows = 2 * num_obs
+    u = frac_ref[...]
+    u_square = u * u
+    u_cubed = u_square * u
+    basis = (
+        (1.0 - u) ** 3 / 6.0,
         (3.0 * u_cubed - 6.0 * u_square + 4.0) / 6.0,
-        (-3.0 * u_cubed + 3.0 * u_square + 3.0 * knot_frac + 1.0) / 6.0,
+        (-3.0 * u_cubed + 3.0 * u_square + 3.0 * u + 1.0) / 6.0,
         u_cubed / 6.0,
     )
-
-
-def reduce_rows(land_jac, pose_jac, segment, knot_frac, track_len):
+    seg = seg_ref[...]
+    obs = lax.broadcasted_iota(jnp.int32, (num_obs, lanes), 0)
+    observed = (obs < len_ref[...]).astype(jnp.float32)
+    knot = lax.broadcasted_iota(jnp.int32, (WIN_KNOTS, lanes), 0)
+    land = []
+    knots = []
+    for j in range(num_obs):
+        seg_j = seg[j:j + 1, :]
+        weight = jnp.zeros((WIN_KNOTS, lanes), jnp.float32)
+        for k in range(4):
+            weight = weight + basis[k][j:j + 1, :] * (seg_j + k == knot).astype(jnp.float32)
+        mask = observed[j:j + 1, :]
+        for i in range(2):
+            r = 2 * j + i
+            land.append(land_ref[r] * mask)
+            pose = pose_ref[r] * mask
+            knots.append(jnp.concatenate([pose[e:e + 1, :] * weight for e in range(KDOF)], axis=0))
+    for k in range(3):
+        column = [land[r][k:k + 1, :] for r in range(k, rows)]
+        total = column[0] * column[0]
+        for x in column[1:]:
+            total = total + x * x
+        length = jnp.sqrt(total)
+        signum = jnp.where(column[0] >= 0.0, 1.0, -1.0)
+        vector = [column[0] + signum * length] + column[1:]
+        vv = vector[0] * vector[0]
+        for x in vector[1:]:
+            vv = vv + x * x
+        scale = 2.0 / vv
+        for mats in (land, knots):
+            proj = vector[0] * mats[k]
+            for idx in range(1, rows - k):
+                proj = proj + vector[idx] * mats[k + idx]
+            for idx in range(rows - k):
+                mats[k + idx] = mats[k + idx] - (scale * vector[idx]) * proj
+    reduced = jnp.concatenate(knots[3:], axis=1)
+    out_ref[0] = lax.dot_general(reduced, reduced, (((1,), (1,)), ((), ())),
+                                 precision=lax.Precision.HIGHEST, preferred_element_type=jnp.float32)
+
+
+def block_grams_kernel(land_jac, pose_jac, segment, knot_frac, track_len, num_blocks):
+    rows, ldim, landmarks = land_jac.shape
+    pdim = pose_jac.shape[1]
     num_obs = segment.shape[0]
-    landmarks = segment.shape[1]
-    observed = (
-        lax.broadcasted_iota(jnp.int32, (num_obs, landmarks), 0) < track_len[None, :]
-    ).astype(jnp.float32)
-    row_mask = jnp.repeat(observed, 2, axis=0)
-    landmark = land_jac * row_mask[:, None, :]
-    pose_rows = (pose_jac * row_mask[:, None, :]).reshape(num_obs, 2, 1, KDOF, landmarks)
-    weights = basis_weights(knot_frac)
-    knot_index = lax.broadcasted_iota(jnp.int32, (1, WIN_KNOTS, 1), 1)
-    knot_weight = jnp.zeros((num_obs, WIN_KNOTS, landmarks), jnp.float32)
-    for k in range(4):
-        knot_weight = knot_weight + weights[k][:, None, :] * (
-            segment[:, None, :] + k == knot_index
-        ).astype(jnp.float32)
-    knot_jac = (knot_weight[:, None, :, None, :] * pose_rows).reshape(
-        2 * num_obs, WIN_KNOTS * KDOF, landmarks
-    )
-    for k in range(3):
-        column = landmark[k:, k, :]
-        length = jnp.sqrt(jnp.sum(column * column, axis=0))
-        signum = jnp.where(column[0] >= 0.0, 1.0, -1.0)
-        leading = column[0] + signum * length
-        vector = jnp.concatenate([leading[None, :], column[1:]], axis=0)
-        reflect_scale = 2.0 / jnp.sum(vector * vector, axis=0)
-
-        def reflect(matrix):
-            lower_rows = matrix[k:]
-            projection = jnp.sum(vector[:, None, :] * lower_rows, axis=0)
-            updated = lower_rows - (reflect_scale * vector)[:, None, :] * projection[None, :, :]
-            return jnp.concatenate([matrix[:k], updated], axis=0)
-
-        landmark = reflect(landmark)
-        knot_jac = reflect(knot_jac)
-    return knot_jac[3:]
-
-
-def block_grams(reduced, num_blocks):
-    red_rows, win_width, landmarks = reduced.shape
-    shaped = reduced.reshape(red_rows, win_width, num_blocks, landmarks // num_blocks)
-    return jnp.einsum("rcbl,rdbl->bcd", shaped, shaped, precision=lax.Precision.HIGHEST)
+    blk = landmarks // num_blocks
+    width = WIN_KNOTS * KDOF
+    return pl.pallas_call(
+        gram_kernel,
+        out_shape=jax.ShapeDtypeStruct((num_blocks, width, width), jnp.float32),
+        grid=(num_blocks,),
+        in_specs=[
+            pl.BlockSpec((rows, ldim, blk), lambda b: (0, 0, b)),
+            pl.BlockSpec((rows, pdim, blk), lambda b: (0, 0, b)),
+            pl.BlockSpec((num_obs, blk), lambda b: (0, b)),
+            pl.BlockSpec((num_obs, blk), lambda b: (0, b)),
+            pl.BlockSpec((1, blk), lambda b: (0, b)),
+        ],
+        out_specs=pl.BlockSpec((1, width, width), lambda b: (b, 0, 0)),
+    )(land_jac, pose_jac, segment, knot_frac, track_len.reshape(1, landmarks))
 
 
 def skew_blocks(grams):
     num_blocks = grams.shape[0]
-    g5 = grams.reshape(num_blocks, WIN_KNOTS, KDOF, WIN_KNOTS, KDOF)
+    g5 = grams.reshape(num_blocks, KDOF, WIN_KNOTS, KDOF, WIN_KNOTS).transpose(0, 2, 1, 4, 3)
     k1 = lax.broadcasted_iota(jnp.int32, (WIN_KNOTS, WIN_KNOTS, WIN_KNOTS), 0)
     k2 = lax.broadcasted_iota(jnp.int32, (WIN_KNOTS, WIN_KNOTS, WIN_KNOTS), 1)
     d = lax.broadcasted_iota(jnp.int32, (WIN_KNOTS, WIN_KNOTS, WIN_KNOTS), 2)
@@ -181,8 +199,7 @@
 
 def local(land_jac, pose_jac, segment, knot_frac, track_len, block_base, damping):
     num_blocks = block_base.shape[0]
-    reduced = reduce_rows(land_jac, pose_jac, segment, knot_frac, track_len)
-    grams = block_grams(reduced, num_blocks)
+    grams = block_grams_kernel(land_jac, pose_jac, segment, knot_frac, track_len, num_blocks)
     group_cols = damping.shape[0]
     num_groups = lax.axis_size("cols")
     band = place_band(skew_blocks(grams), block_base, group_cols, num_groups)

time: 183 us -> 144 us (0.79)
  other arithmetic: 23.7 us -> 0.27 us
  local copies, waits for them, and re-layouts: 27.1 us -> 11 us
  Pallas kernels: 74.4 us -> 88.1 us
  matrix products: 14.3 us -> 1.14 us
    pallas_call x0 -> x1, Pallas kernels: none -> 13.7 us  [block_grams_kernel(): pl.pallas_call(gram_kernel, out_shape=jax.ShapeDtypeStruct((num_blocks, w...]
    dot_general x1 -> x0, matrix products: 11.9 us -> none  [block_grams(): jnp.einsum('rcbl,rdbl->bcd', shaped, shaped, precision=lax.Precision.HIGH...]
    reshape x3 -> x0, local copies, waits for them, and re-layouts: 11.6 us -> none  [the longest x1 6.97 us: block_grams(): reduced.reshape(red_rows, win_width, num_blocks, landmarks // num_blocks)]
    reduce_sum x10 -> x0, other arithmetic: 9.22 us -> none  [the longest x4 8.98 us: reflect(): projection = jnp.sum(vector[:, None, :] * lower_rows, axis=0)]
    mul x5 -> x0, local copies, waits for them, and re-layouts: 9.12 us -> none  [the longest x2 8.9 us: reduce_rows(): knot_weight[:, None, :, None, :] * pose_rows]
    mul x6 -> x0, other arithmetic: 7.93 us -> none  [the longest x1 6.76 us: reduce_rows(): knot_weight[:, None, :, None, :] * pose_rows]
    sub x3 -> x0, other arithmetic: 5.12 us -> none  [reflect(): lower_rows - (reflect_scale * vector)[:, None, :] * projection[None, :, :]]
    unnamed x10 -> x8, local copies, waits for them, and re-layouts: 0.02 us -> 3.59 us
where the time goes in v5:
time: 144 us; the launch traced here: 143 us
  Pallas kernels  88.1 us (61%)
  waiting for transfers between devices  33 us (23%)
  local copies, waits for them, and re-layouts  11 us (8%)
  starting transfers between devices  9.65 us (7%)
    pallas_call x1, Pallas kernels, band_cholesky(): pl.pallas_call(functools.partial(band_chol_kernel, n, band_w), out_shape=...  74.4 us
    ppermute x5, waiting for transfers between devices, butterfly_sum(): band = band + lax.ppermute(band, axis, [(i, i ^ s) for i in range(n)])  22.4 us
    pallas_call x1, Pallas kernels, block_grams_kernel(): pl.pallas_call(gram_kernel, out_shape=jax.ShapeDtypeStruct((num_blocks, w...  13.7 us
    ppermute x2, waiting for transfers between devices, halve_over(): band = keep + lax.ppermute(send, axis, [(i, i ^ s) for i in range(n)])  10.6 us
    ppermute x2, starting transfers between devices, halve_over(): band = keep + lax.ppermute(send, axis, [(i, i ^ s) for i in range(n)])  4.93 us
    ppermute x5, starting transfers between devices, butterfly_sum(): band = band + lax.ppermute(band, axis, [(i, i ^ s) for i in range(n)])  4.72 us
    unnamed x8, local copies, waits for them, and re-layouts  3.59 us
  transfers between devices with their start and end apart: 7, of which 7 were waited for; matrix products, arithmetic and copies ran while one was open for 0% of the time, Pallas kernels for 0%

profile of v5, /device:TPU:38, one launch (start us, length us, event | category | flops | bytes accessed | tf_op | source)
XLA Modules:
  0.0 143.2 jit_solution(17697686996753965657)
XLA Ops:
  0.0 0.0 copy-start
  0.0 2.1 %copy.12.land_ref = f32[16,3,2048]{2,1,0:T(4,128)} copy(f32[16,3,2048]{2,0,1:T(8,128)} %param.7) | data formatting | bytes 786432 | tf_op args[0]
  2.1 0.0 copy-done
  2.1 1.4 %copy.13.pose_ref = f32[16,6,2048]{2,1,0:T(8,128)} copy(f32[16,6,2048]{2,0,1:T(8,128)S(1)} %copy-done) | data formatting | bytes 1572864 | tf_op args[1]
  3.6 13.7 %shard_map.73 = f32[16,48,48]{2,1,0:T(8,128)} custom-call(f32[16,3,2048]{2,1,0:T(4,128)} %copy.12.land_ref, f32[16,6,2048]{2,1,0:T(8,128)} %copy.13.pose_ref, s32[8,2048]{1,0:T(8,128)} %seg_ref.1, f32[8,2048]{1,0:T(8,128)} %frac_ref.1, s32[1,2048]{1,0:T(1,128)} %bitcast.26), custom_call_target="tpu_custom_call" | custom-call | tf_op jit(solution)/shard_map/pallas_call | solution.py:73
  17.3 1.4 copy.14
  18.7 0.7 convolution_bitcast_fusion
  19.3 0.9 copy.16
  20.3 0.0 copy-start.2
  20.3 1.2 reshape.70
  21.4 0.0 copy-done.2
  21.4 0.1 iota_add_fusion
  21.5 0.5 fusion.2
  22.0 3.3 %collective-permute-start = (f32[256,288]{0,1:T(8,128)S(1)}, f32[256,288]{0,1:T(8,128)S(1)}, u32[]{:S(2)}, u32[]{:S(2)}) collective-permute-start(f32[256,288]{0,1:T(8,128)S(1)} %constant_dynamic-slice_fusion.1), channel_id=1, source_target_pairs={{0,2},{1,3},{2,0},{3,1},{4,6},{5,7},{6,4},{7,5},{8,10},{9,11},{10,... | collective-permute-start | bytes 884744 | tf_op jit(solution)/shard_map/ppermute | solution.py:185
  25.3 7.0 %collective-permute-done = f32[256,288]{0,1:T(8,128)S(1)} collective-permute-done((f32[256,288]{0,1:T(8,128)S(1)}, f32[256,288]{0,1:T(8,128)S(1)}, u32[]{:S(2)}, u32[]{:S(2)}) %collective-permute-start) | collective-permute-done | bytes 294944 | tf_op jit(solution)/shard_map/ppermute | solution.py:185
  32.5 1.7 %collective-permute-start.1 = (f32[128,288]{0,1:T(8,128)S(1)}, f32[128,288]{0,1:T(8,128)S(1)}, u32[]{:S(2)}, u32[]{:S(2)}) collective-permute-start(f32[128,288]{0,1:T(8,128)S(1)} %constant_dynamic-slice_fusion), channel_id=1, source_target_pairs={{0,1},{1,0},{2,3},{3,2},{4,5},{5,4},{6,7},{7,6},{8,9},{9,8},{10,11... | collective-permute-start | bytes 442376 | tf_op jit(solution)/shard_map/ppermute | solution.py:185
  34.1 3.6 %collective-permute-done.1 = f32[128,288]{0,1:T(8,128)S(1)} collective-permute-done((f32[128,288]{0,1:T(8,128)S(1)}, f32[128,288]{0,1:T(8,128)S(1)}, u32[]{:S(2)}, u32[]{:S(2)}) %collective-permute-start.1) | collective-permute-done | bytes 147488 | tf_op jit(solution)/shard_map/ppermute | solution.py:185
  37.7 0.1 collective-permute-start.2
  37.8 1.4 collective-permute-done.2
  39.2 0.2 collective-permute-start.3
  39.4 5.8 %collective-permute-done.3 = f32[128,288]{0,1:T(8,128)S(1)} collective-permute-done((f32[128,288]{0,1:T(8,128)S(1)}, f32[128,288]{0,1:T(8,128)S(1)}, u32[]{:S(2)}, u32[]{:S(2)}) %collective-permute-start.3) | collective-permute-done | bytes 147488 | tf_op jit(solution)/shard_map/ppermute | solution.py:195
  45.2 3.1 %collective-permute-start.4 = (f32[128,288]{0,1:T(8,128)S(1)}, f32[128,288]{0,1:T(8,128)S(1)}, u32[]{:S(2)}, u32[]{:S(2)}) collective-permute-start(f32[128,288]{0,1:T(8,128)S(1)} %add.99), channel_id=1, source_target_pairs={{0,16},{4,20},{8,24},{12,28},{16,0},{20,4},{24,8},{28,12},{32,48},... | collective-permute-start | bytes 442376 | tf_op jit(solution)/shard_map/ppermute | solution.py:195
  48.2 3.7 %collective-permute-done.4 = f32[128,288]{0,1:T(8,128)S(1)} collective-permute-done((f32[128,288]{0,1:T(8,128)S(1)}, f32[128,288]{0,1:T(8,128)S(1)}, u32[]{:S(2)}, u32[]{:S(2)}) %collective-permute-start.4) | collective-permute-done | bytes 147488 | tf_op jit(solution)/shard_map/ppermute | solution.py:195
  51.9 0.9 collective-permute-start.5
  52.8 5.3 %collective-permute-done.5 = f32[128,288]{0,1:T(8,128)S(1)} collective-permute-done((f32[128,288]{0,1:T(8,128)S(1)}, f32[128,288]{0,1:T(8,128)S(1)}, u32[]{:S(2)}, u32[]{:S(2)}) %collective-permute-start.5) | collective-permute-done | bytes 147488 | tf_op jit(solution)/shard_map/ppermute | solution.py:195
  58.2 0.5 collective-permute-start.6
  58.7 6.2 %collective-permute-done.6 = f32[128,288]{0,1:T(8,128)S(1)} collective-permute-done((f32[128,288]{0,1:T(8,128)S(1)}, f32[128,288]{0,1:T(8,128)S(1)}, u32[]{:S(2)}, u32[]{:S(2)}) %collective-permute-start.6) | collective-permute-done | bytes 147488 | tf_op jit(solution)/shard_map/ppermute | solution.py:195
  64.9 1.1 copy.17
  66.0 0.0 copy-start.1
  66.0 2.1 %reshape.72 = f32[48,768]{1,0:T(8,128)S(1)} reshape(f32[8,6,128,6]{3,2,1,0:T(8,128)S(1)} %copy.17) | data formatting | bytes 294912 | tf_op jit(solution)/shard_map/reshape | solution.py:209
  68.1 0.0 copy-done.1
  68.2 0.7 pad.4.yt_ref
  68.9 74.4 %shard_map.74 = f32[768,768]{1,0:T(8,128)} custom-call(f32[48,896]{1,0:T(8,128)} %pad.4.yt_ref), custom_call_target="tpu_custom_call" | custom-call | tf_op jit(solution)/shard_map/pallas_call | solution.py:163
  (14 shorter events, 0.3 us)
Async XLA Ops:
  0.0 2.1 %copy-start = (f32[16,6,2048]{2,0,1:T(8,128)S(1)}, f32[16,6,2048]{2,0,1:T(8,128)}, u32[]{:S(2)}) copy-start(f32[16,6,2048]{2,0,1:T(8,128)} %param.8) | copy-start | bytes 2359300
  20.3 1.2 copy-start.2
  22.0 10.3 %collective-permute-start = (f32[256,288]{0,1:T(8,128)S(1)}, f32[256,288]{0,1:T(8,128)S(1)}, u32[]{:S(2)}, u32[]{:S(2)}) collective-permute-start(f32[256,288]{0,1:T(8,128)S(1)} %constant_dynamic-slice_fusion.1), channel_id=1, source_target_pairs={{0,2},{1,3},{2,0},{3,1},{4,6},{5,7},{6,4},{7,5},{8,10},{9,11},{10,... | collective-permute-start | bytes 884744 | tf_op jit(solution)/shard_map/ppermute | solution.py:185
  32.5 5.2 %collective-permute-start.1 = (f32[128,288]{0,1:T(8,128)S(1)}, f32[128,288]{0,1:T(8,128)S(1)}, u32[]{:S(2)}, u32[]{:S(2)}) collective-permute-start(f32[128,288]{0,1:T(8,128)S(1)} %constant_dynamic-slice_fusion), channel_id=1, source_target_pairs={{0,1},{1,0},{2,3},{3,2},{4,5},{5,4},{6,7},{7,6},{8,9},{9,8},{10,11... | collective-permute-start | bytes 442376 | tf_op jit(solution)/shard_map/ppermute | solution.py:185
  37.7 1.5 %collective-permute-start.2 = (f32[128,288]{0,1:T(8,128)S(1)}, f32[128,288]{0,1:T(8,128)S(1)}, u32[]{:S(2)}, u32[]{:S(2)}) collective-permute-start(f32[128,288]{0,1:T(8,128)S(1)} %dynamic-slice_add_fusion.1), channel_id=1, source_target_pairs={{0,4},{4,0},{8,12},{12,8},{16,20},{20,16},{24,28},{28,24},{32,36},... | collective-permute-start | bytes 442376 | tf_op jit(solution)/shard_map/ppermute | solution.py:195
  39.2 6.0 %collective-permute-start.3 = (f32[128,288]{0,1:T(8,128)S(1)}, f32[128,288]{0,1:T(8,128)S(1)}, u32[]{:S(2)}, u32[]{:S(2)}) collective-permute-start(f32[128,288]{0,1:T(8,128)S(1)} %add.98), channel_id=1, source_target_pairs={{0,8},{4,12},{8,0},{12,4},{16,24},{20,28},{24,16},{28,20},{32,40},... | collective-permute-start | bytes 442376 | tf_op jit(solution)/shard_map/ppermute | solution.py:195
  45.2 6.7 %collective-permute-start.4 = (f32[128,288]{0,1:T(8,128)S(1)}, f32[128,288]{0,1:T(8,128)S(1)}, u32[]{:S(2)}, u32[]{:S(2)}) collective-permute-start(f32[128,288]{0,1:T(8,128)S(1)} %add.99), channel_id=1, source_target_pairs={{0,16},{4,20},{8,24},{12,28},{16,0},{20,4},{24,8},{28,12},{32,48},... | collective-permute-start | bytes 442376 | tf_op jit(solution)/shard_map/ppermute | solution.py:195
  51.9 6.2 %collective-permute-start.5 = (f32[128,288]{0,1:T(8,128)S(1)}, f32[128,288]{0,1:T(8,128)S(1)}, u32[]{:S(2)}, u32[]{:S(2)}) collective-permute-start(f32[128,288]{0,1:T(8,128)S(1)} %add.100), channel_id=1, source_target_pairs={{0,32},{4,36},{8,40},{12,44},{16,48},{20,52},{24,56},{28,60},{32,0... | collective-permute-start | bytes 442376 | tf_op jit(solution)/shard_map/ppermute | solution.py:195
  58.2 6.7 %collective-permute-start.6 = (f32[128,288]{0,1:T(8,128)S(1)}, f32[128,288]{0,1:T(8,128)S(1)}, u32[]{:S(2)}, u32[]{:S(2)}) collective-permute-start(f32[128,288]{0,1:T(8,128)S(1)} %add.101), channel_id=1, source_target_pairs={{0,64},{4,68},{8,72},{12,76},{16,80},{20,84},{24,88},{28,92},{32,9... | collective-permute-start | bytes 442376 | tf_op jit(solution)/shard_map/ppermute | solution.py:195
  66.0 2.1 %copy-start.1 = (f32[768]{0:T(1024)S(1)}, f32[768]{0:T(1024)}, u32[]{:S(2)}) copy-start(f32[768]{0:T(1024)} %param.13) | copy-start | bytes 9220

commit v6 on v5

--- a/solution.py
+++ b/solution.py
@@ -138,18 +138,31 @@
         base = pl.multiple_of((p // (128 // PANEL)) * 128, 128)
         off = j0 - base
         blk = w_ref[pl.ds(j0, rows), pl.ds(base, WIDTH)]
-        out_rows = []
+        first = blk[:, :128]
+        lane_first = lane[:, :128]
+        cols = [jnp.sum(jnp.where(lane_first == off + t, first, 0.0), axis=1, keepdims=True)
+                for t in range(PANEL)]
+        lcols = []
+        invs = []
         for t in range(PANEL):
-            jt = off + t
-            col = jnp.sum(jnp.where(lane == jt, blk, 0.0), axis=1, keepdims=True)
-            inv = lax.rsqrt(col[t:t + 1, :])
-            rrow = jnp.where(lane[0:1, :] >= jt, blk[t:t + 1, :] * inv, 0.0)
-            out_rows.append(rrow)
-            mult = jnp.where(row > t, col * inv, 0.0)
-            blk = blk - mult * rrow
-        r_ref[pl.ds(j0, PANEL), pl.ds(base, WIDTH)] = jnp.concatenate(out_rows, axis=0)
+            inv = lax.rsqrt(cols[t][t:t + 1, :])
+            lcol = jnp.where(row >= t, cols[t] * inv, 0.0)
+            lcols.append(lcol)
+            invs.append(inv)
+            for t2 in range(t + 1, PANEL):
+                cols[t2] = cols[t2] - lcol * lcol[t2:t2 + 1, :]
+        rrows = []
+        for t in range(PANEL):
+            acc = blk[t:t + 1, :]
+            for t1 in range(t):
+                acc = acc - lcols[t1][t:t + 1, :] * rrows[t1]
+            rrows.append(jnp.where(lane[0:1, :] >= off + t, acc * invs[t], 0.0))
+        r_ref[pl.ds(j0, PANEL), pl.ds(base, WIDTH)] = jnp.concatenate(rrows, axis=0)
+        trail = blk[PANEL:, :]
+        for t in range(PANEL):
+            trail = trail - lcols[t][PANEL:, :] * rrows[t]
         start = pl.multiple_of(j0 + PANEL, PANEL)
-        w_ref[pl.ds(start, band_w), pl.ds(base, WIDTH)] = blk[PANEL:, :]
+        w_ref[pl.ds(start, band_w), pl.ds(base, WIDTH)] = trail
         return carry
 
     lax.fori_loop(0, n // PANEL, panel, 0)

time: 144 us -> 95.3 us (0.66)
  Pallas kernels: 88.1 us -> 39.1 us
    pallas_call x1, Pallas kernels: 74.4 us -> 25.4 us  [band_cholesky(): pl.pallas_call(functools.partial(band_chol_kernel, n, band_w), out_shape=...]
where the time goes in v6:
time: 95.3 us; the launch traced here: 94.3 us
  Pallas kernels  39.1 us (41%)
  waiting for transfers between devices  33 us (35%)
  local copies, waits for them, and re-layouts  11 us (12%)
  starting transfers between devices  9.65 us (10%)
  matrix products  1.14 us (1%)
    pallas_call x1, Pallas kernels, band_cholesky(): pl.pallas_call(functools.partial(band_chol_kernel, n, band_w), out_shape=...  25.4 us
    ppermute x5, waiting for transfers between devices, butterfly_sum(): band = band + lax.ppermute(band, axis, [(i, i ^ s) for i in range(n)])  22.4 us
    pallas_call x1, Pallas kernels, block_grams_kernel(): pl.pallas_call(gram_kernel, out_shape=jax.ShapeDtypeStruct((num_blocks, w...  13.7 us
    ppermute x2, waiting for transfers between devices, halve_over(): band = keep + lax.ppermute(send, axis, [(i, i ^ s) for i in range(n)])  10.6 us
    ppermute x2, starting transfers between devices, halve_over(): band = keep + lax.ppermute(send, axis, [(i, i ^ s) for i in range(n)])  4.93 us
    ppermute x5, starting transfers between devices, butterfly_sum(): band = band + lax.ppermute(band, axis, [(i, i ^ s) for i in range(n)])  4.72 us
    unnamed x8, local copies, waits for them, and re-layouts  3.59 us
    reshape x1, local copies, waits for them, and re-layouts, local(): yt = yt.reshape(WIN_KNOTS * KDOF, group_cols)  2.12 us
  transfers between devices with their start and end apart: 7, of which 7 were waited for; matrix products, arithmetic and copies ran while one was open for 0% of the time, Pallas kernels for 0%

profile of v6, /device:TPU:38, one launch (start us, length us, event | category | flops | bytes accessed | tf_op | source)
XLA Modules:
  0.0 94.3 jit_solution(17037721586670321932)
XLA Ops:
  0.0 0.0 copy-start
  0.0 2.1 %copy.12.land_ref = f32[16,3,2048]{2,1,0:T(4,128)} copy(f32[16,3,2048]{2,0,1:T(8,128)} %param.7) | data formatting | bytes 786432 | tf_op args[0]
  2.1 0.0 copy-done
  2.1 1.4 %copy.13.pose_ref = f32[16,6,2048]{2,1,0:T(8,128)} copy(f32[16,6,2048]{2,0,1:T(8,128)S(1)} %copy-done) | data formatting | bytes 1572864 | tf_op args[1]
  3.6 13.7 %shard_map.73 = f32[16,48,48]{2,1,0:T(8,128)} custom-call(f32[16,3,2048]{2,1,0:T(4,128)} %copy.12.land_ref, f32[16,6,2048]{2,1,0:T(8,128)} %copy.13.pose_ref, s32[8,2048]{1,0:T(8,128)} %seg_ref.1, f32[8,2048]{1,0:T(8,128)} %frac_ref.1, s32[1,2048]{1,0:T(1,128)} %bitcast.26), custom_call_target="tpu_custom_call" | custom-call | tf_op jit(solution)/shard_map/pallas_call | solution.py:73
  17.3 1.4 %copy.14 = f32[16,48,48]{0,2,1:T(8,128)S(1)} copy(f32[16,48,48]{2,1,0:T(8,128)} %shard_map.73) | data formatting | bytes 294912 | tf_op jit(solution)/shard_map/pallas_call | solution.py:73
  18.7 0.7 convolution_bitcast_fusion
  19.3 0.9 copy.16
  20.3 0.0 copy-start.2
  20.3 1.2 %reshape.70 = f32[128,288]{0,1:T(8,128)S(1)} reshape(f32[16,8,8,6,6]{1,0,4,3,2:T(8,128)S(1)} %copy.16) | data formatting | bytes 294912 | tf_op jit(solution)/shard_map/reshape | solution.py:106
  21.4 0.0 copy-done.2
  21.4 0.1 iota_add_fusion
  21.5 0.5 fusion.2
  22.0 3.3 %collective-permute-start = (f32[256,288]{0,1:T(8,128)S(1)}, f32[256,288]{0,1:T(8,128)S(1)}, u32[]{:S(2)}, u32[]{:S(2)}) collective-permute-start(f32[256,288]{0,1:T(8,128)S(1)} %constant_dynamic-slice_fusion.1), channel_id=1, source_target_pairs={{0,2},{1,3},{2,0},{3,1},{4,6},{5,7},{6,4},{7,5},{8,10},{9,11},{10,... | collective-permute-start | bytes 884744 | tf_op jit(solution)/shard_map/ppermute | solution.py:198
  25.3 7.0 %collective-permute-done = f32[256,288]{0,1:T(8,128)S(1)} collective-permute-done((f32[256,288]{0,1:T(8,128)S(1)}, f32[256,288]{0,1:T(8,128)S(1)}, u32[]{:S(2)}, u32[]{:S(2)}) %collective-permute-start) | collective-permute-done | bytes 294944 | tf_op jit(solution)/shard_map/ppermute | solution.py:198
  32.5 1.7 %collective-permute-start.1 = (f32[128,288]{0,1:T(8,128)S(1)}, f32[128,288]{0,1:T(8,128)S(1)}, u32[]{:S(2)}, u32[]{:S(2)}) collective-permute-start(f32[128,288]{0,1:T(8,128)S(1)} %constant_dynamic-slice_fusion), channel_id=1, source_target_pairs={{0,1},{1,0},{2,3},{3,2},{4,5},{5,4},{6,7},{7,6},{8,9},{9,8},{10,11... | collective-permute-start | bytes 442376 | tf_op jit(solution)/shard_map/ppermute | solution.py:198
  34.1 3.6 %collective-permute-done.1 = f32[128,288]{0,1:T(8,128)S(1)} collective-permute-done((f32[128,288]{0,1:T(8,128)S(1)}, f32[128,288]{0,1:T(8,128)S(1)}, u32[]{:S(2)}, u32[]{:S(2)}) %collective-permute-start.1) | collective-permute-done | bytes 147488 | tf_op jit(solution)/shard_map/ppermute | solution.py:198
  37.7 0.1 collective-permute-start.2
  37.8 1.4 %collective-permute-done.2 = f32[128,288]{0,1:T(8,128)S(1)} collective-permute-done((f32[128,288]{0,1:T(8,128)S(1)}, f32[128,288]{0,1:T(8,128)S(1)}, u32[]{:S(2)}, u32[]{:S(2)}) %collective-permute-start.2) | collective-permute-done | bytes 147488 | tf_op jit(solution)/shard_map/ppermute | solution.py:208
  39.2 0.2 collective-permute-start.3
  39.4 5.8 %collective-permute-done.3 = f32[128,288]{0,1:T(8,128)S(1)} collective-permute-done((f32[128,288]{0,1:T(8,128)S(1)}, f32[128,288]{0,1:T(8,128)S(1)}, u32[]{:S(2)}, u32[]{:S(2)}) %collective-permute-start.3) | collective-permute-done | bytes 147488 | tf_op jit(solution)/shard_map/ppermute | solution.py:208
  45.2 3.1 %collective-permute-start.4 = (f32[128,288]{0,1:T(8,128)S(1)}, f32[128,288]{0,1:T(8,128)S(1)}, u32[]{:S(2)}, u32[]{:S(2)}) collective-permute-start(f32[128,288]{0,1:T(8,128)S(1)} %add.99), channel_id=1, source_target_pairs={{0,16},{4,20},{8,24},{12,28},{16,0},{20,4},{24,8},{28,12},{32,48},... | collective-permute-start | bytes 442376 | tf_op jit(solution)/shard_map/ppermute | solution.py:208
  48.2 3.7 %collective-permute-done.4 = f32[128,288]{0,1:T(8,128)S(1)} collective-permute-done((f32[128,288]{0,1:T(8,128)S(1)}, f32[128,288]{0,1:T(8,128)S(1)}, u32[]{:S(2)}, u32[]{:S(2)}) %collective-permute-start.4) | collective-permute-done | bytes 147488 | tf_op jit(solution)/shard_map/ppermute | solution.py:208
  51.9 0.9 collective-permute-start.5
  52.8 5.3 %collective-permute-done.5 = f32[128,288]{0,1:T(8,128)S(1)} collective-permute-done((f32[128,288]{0,1:T(8,128)S(1)}, f32[128,288]{0,1:T(8,128)S(1)}, u32[]{:S(2)}, u32[]{:S(2)}) %collective-permute-start.5) | collective-permute-done | bytes 147488 | tf_op jit(solution)/shard_map/ppermute | solution.py:208
  58.2 0.5 collective-permute-start.6
  58.7 6.2 %collective-permute-done.6 = f32[128,288]{0,1:T(8,128)S(1)} collective-permute-done((f32[128,288]{0,1:T(8,128)S(1)}, f32[128,288]{0,1:T(8,128)S(1)}, u32[]{:S(2)}, u32[]{:S(2)}) %collective-permute-start.6) | collective-permute-done | bytes 147488 | tf_op jit(solution)/shard_map/ppermute | solution.py:208
  64.9 1.1 %copy.17 = f32[8,6,128,6]{3,2,1,0:T(8,128)S(1)} copy(f32[8,6,128,6]{2,1,3,0:T(8,128)S(1)} %bitcast.25) | data formatting | bytes 294912 | tf_op jit(solution)/shard_map/transpose | solution.py:221
  66.0 0.0 copy-start.1
  66.0 2.1 %reshape.72 = f32[48,768]{1,0:T(8,128)S(1)} reshape(f32[8,6,128,6]{3,2,1,0:T(8,128)S(1)} %copy.17) | data formatting | bytes 294912 | tf_op jit(solution)/shard_map/reshape | solution.py:222
  68.1 0.0 copy-done.1
  68.2 0.7 pad.4.yt_ref
  68.9 25.4 %shard_map.74 = f32[768,768]{1,0:T(8,128)} custom-call(f32[48,896]{1,0:T(8,128)} %pad.4.yt_ref), custom_call_target="tpu_custom_call" | custom-call | tf_op jit(solution)/shard_map/pallas_call | solution.py:176
  (14 shorter events, 0.3 us)
Async XLA Ops:
  0.0 2.1 %copy-start = (f32[16,6,2048]{2,0,1:T(8,128)S(1)}, f32[16,6,2048]{2,0,1:T(8,128)}, u32[]{:S(2)}) copy-start(f32[16,6,2048]{2,0,1:T(8,128)} %param.8) | copy-start | bytes 2359300
  20.3 1.2 %copy-start.2 = (s32[16]{0:T(128)S(1)}, s32[16]{0:T(128)}, u32[]{:S(2)}) copy-start(s32[16]{0:T(128)} %param.12) | copy-start | bytes 196
  22.0 10.3 %collective-permute-start = (f32[256,288]{0,1:T(8,128)S(1)}, f32[256,288]{0,1:T(8,128)S(1)}, u32[]{:S(2)}, u32[]{:S(2)}) collective-permute-start(f32[256,288]{0,1:T(8,128)S(1)} %constant_dynamic-slice_fusion.1), channel_id=1, source_target_pairs={{0,2},{1,3},{2,0},{3,1},{4,6},{5,7},{6,4},{7,5},{8,10},{9,11},{10,... | collective-permute-start | bytes 884744 | tf_op jit(solution)/shard_map/ppermute | solution.py:198
  32.5 5.2 %collective-permute-start.1 = (f32[128,288]{0,1:T(8,128)S(1)}, f32[128,288]{0,1:T(8,128)S(1)}, u32[]{:S(2)}, u32[]{:S(2)}) collective-permute-start(f32[128,288]{0,1:T(8,128)S(1)} %constant_dynamic-slice_fusion), channel_id=1, source_target_pairs={{0,1},{1,0},{2,3},{3,2},{4,5},{5,4},{6,7},{7,6},{8,9},{9,8},{10,11... | collective-permute-start | bytes 442376 | tf_op jit(solution)/shard_map/ppermute | solution.py:198
  37.7 1.5 %collective-permute-start.2 = (f32[128,288]{0,1:T(8,128)S(1)}, f32[128,288]{0,1:T(8,128)S(1)}, u32[]{:S(2)}, u32[]{:S(2)}) collective-permute-start(f32[128,288]{0,1:T(8,128)S(1)} %dynamic-slice_add_fusion.1), channel_id=1, source_target_pairs={{0,4},{4,0},{8,12},{12,8},{16,20},{20,16},{24,28},{28,24},{32,36},... | collective-permute-start | bytes 442376 | tf_op jit(solution)/shard_map/ppermute | solution.py:208
  39.2 6.0 %collective-permute-start.3 = (f32[128,288]{0,1:T(8,128)S(1)}, f32[128,288]{0,1:T(8,128)S(1)}, u32[]{:S(2)}, u32[]{:S(2)}) collective-permute-start(f32[128,288]{0,1:T(8,128)S(1)} %add.98), channel_id=1, source_target_pairs={{0,8},{4,12},{8,0},{12,4},{16,24},{20,28},{24,16},{28,20},{32,40},... | collective-permute-start | bytes 442376 | tf_op jit(solution)/shard_map/ppermute | solution.py:208
  45.2 6.7 %collective-permute-start.4 = (f32[128,288]{0,1:T(8,128)S(1)}, f32[128,288]{0,1:T(8,128)S(1)}, u32[]{:S(2)}, u32[]{:S(2)}) collective-permute-start(f32[128,288]{0,1:T(8,128)S(1)} %add.99), channel_id=1, source_target_pairs={{0,16},{4,20},{8,24},{12,28},{16,0},{20,4},{24,8},{28,12},{32,48},... | collective-permute-start | bytes 442376 | tf_op jit(solution)/shard_map/ppermute | solution.py:208
  51.9 6.2 %collective-permute-start.5 = (f32[128,288]{0,1:T(8,128)S(1)}, f32[128,288]{0,1:T(8,128)S(1)}, u32[]{:S(2)}, u32[]{:S(2)}) collective-permute-start(f32[128,288]{0,1:T(8,128)S(1)} %add.100), channel_id=1, source_target_pairs={{0,32},{4,36},{8,40},{12,44},{16,48},{20,52},{24,56},{28,60},{32,0... | collective-permute-start | bytes 442376 | tf_op jit(solution)/shard_map/ppermute | solution.py:208
  58.2 6.7 %collective-permute-start.6 = (f32[128,288]{0,1:T(8,128)S(1)}, f32[128,288]{0,1:T(8,128)S(1)}, u32[]{:S(2)}, u32[]{:S(2)}) collective-permute-start(f32[128,288]{0,1:T(8,128)S(1)} %add.101), channel_id=1, source_target_pairs={{0,64},{4,68},{8,72},{12,76},{16,80},{20,84},{24,88},{28,92},{32,9... | collective-permute-start | bytes 442376 | tf_op jit(solution)/shard_map/ppermute | solution.py:208
  66.0 2.1 %copy-start.1 = (f32[768]{0:T(1024)S(1)}, f32[768]{0:T(1024)}, u32[]{:S(2)}) copy-start(f32[768]{0:T(1024)} %param.13) | copy-start | bytes 9220

commit v7 on v6

--- a/solution.py
+++ b/solution.py
@@ -59,21 +59,23 @@
                 proj = proj + vector[idx] * mats[k + idx]
             for idx in range(rows - k):
                 mats[k + idx] = mats[k + idx] - (scale * vector[idx]) * proj
-    reduced = jnp.concatenate(knots[3:], axis=1)
-    out_ref[0] = lax.dot_general(reduced, reduced, (((1,), (1,)), ((), ())),
-                                 precision=lax.Precision.HIGHEST, preferred_element_type=jnp.float32)
-
-
-def block_grams_kernel(land_jac, pose_jac, segment, knot_frac, track_len, num_blocks):
+    for s in range(out_ref.shape[0]):
+        reduced = jnp.concatenate([m[:, 128 * s:128 * (s + 1)] for m in knots[3:]], axis=1)
+        out_ref[s] = lax.dot_general(reduced, reduced, (((1,), (1,)), ((), ())),
+                                     precision=lax.Precision.HIGHEST, preferred_element_type=jnp.float32)
+
+
+def block_grams_kernel(land_jac, pose_jac, segment, knot_frac, track_len, num_blocks, per_step=1):
     rows, ldim, landmarks = land_jac.shape
     pdim = pose_jac.shape[1]
     num_obs = segment.shape[0]
-    blk = landmarks // num_blocks
+    sub = landmarks // num_blocks
+    blk = sub * per_step
     width = WIN_KNOTS * KDOF
     return pl.pallas_call(
         gram_kernel,
         out_shape=jax.ShapeDtypeStruct((num_blocks, width, width), jnp.float32),
-        grid=(num_blocks,),
+        grid=(num_blocks // per_step,),
         in_specs=[
             pl.BlockSpec((rows, ldim, blk), lambda b: (0, 0, b)),
             pl.BlockSpec((rows, pdim, blk), lambda b: (0, 0, b)),
@@ -81,7 +83,7 @@
             pl.BlockSpec((num_obs, blk), lambda b: (0, b)),
             pl.BlockSpec((1, blk), lambda b: (0, b)),
         ],
-        out_specs=pl.BlockSpec((1, width, width), lambda b: (b, 0, 0)),
+        out_specs=pl.BlockSpec((per_step, width, width), lambda b: (b, 0, 0)),
     )(land_jac, pose_jac, segment, knot_frac, track_len.reshape(1, landmarks))
 
 
@@ -212,7 +214,7 @@
 
 def local(land_jac, pose_jac, segment, knot_frac, track_len, block_base, damping):
     num_blocks = block_base.shape[0]
-    grams = block_grams_kernel(land_jac, pose_jac, segment, knot_frac, track_len, num_blocks)
+    grams = block_grams_kernel(land_jac, pose_jac, segment, knot_frac, track_len, num_blocks, 4)
     group_cols = damping.shape[0]
     num_groups = lax.axis_size("cols")
     band = place_band(skew_blocks(grams), block_base, group_cols, num_groups)

time: 95.3 us -> 90.6 us (0.951)
  Pallas kernels: 39.1 us -> 35.2 us
    pallas_call x1, Pallas kernels: 13.7 us -> 9.77 us  [block_grams_kernel(): pl.pallas_call(gram_kernel, out_shape=jax.ShapeDtypeStruct((num_blocks, w...]
where the time goes in v7:
time: 90.6 us; the launch traced here: 90.4 us
  Pallas kernels  35.2 us (39%)
  waiting for transfers between devices  32.6 us (36%)
  local copies, waits for them, and re-layouts  11 us (12%)
  starting transfers between devices  10 us (11%)
  matrix products  1.13 us (1%)
    pallas_call x1, Pallas kernels, band_cholesky(): pl.pallas_call(functools.partial(band_chol_kernel, n, band_w), out_shape=...  25.4 us
    ppermute x5, waiting for transfers between devices, butterfly_sum(): band = band + lax.ppermute(band, axis, [(i, i ^ s) for i in range(n)])  22 us
    ppermute x2, waiting for transfers between devices, halve_over(): band = keep + lax.ppermute(send, axis, [(i, i ^ s) for i in range(n)])  10.6 us
    pallas_call x1, Pallas kernels, block_grams_kernel(): pl.pallas_call(gram_kernel, out_shape=jax.ShapeDtypeStruct((num_blocks, w...  9.77 us
    ppermute x5, starting transfers between devices, butterfly_sum(): band = band + lax.ppermute(band, axis, [(i, i ^ s) for i in range(n)])  5.09 us
    ppermute x2, starting transfers between devices, halve_over(): band = keep + lax.ppermute(send, axis, [(i, i ^ s) for i in range(n)])  4.94 us
    unnamed x8, local copies, waits for them, and re-layouts  3.59 us
    reshape x1, local copies, waits for them, and re-layouts, local(): yt = yt.reshape(WIN_KNOTS * KDOF, group_cols)  2.12 us
  transfers between devices with their start and end apart: 7, of which 7 were waited for; matrix products, arithmetic and copies ran while one was open for 0% of the time, Pallas kernels for 0%

profile of v7, /device:TPU:38, one launch (start us, length us, event | category | flops | bytes accessed | tf_op | source)
XLA Modules:
  0.0 90.4 jit_solution(16514612159177312618)
XLA Ops:
  0.0 0.0 copy-start
  0.0 2.1 %copy.12.land_ref = f32[16,3,2048]{2,1,0:T(4,128)} copy(f32[16,3,2048]{2,0,1:T(8,128)} %param.7) | data formatting | bytes 786432 | tf_op args[0]
  2.1 0.0 copy-done
  2.1 1.4 %copy.13.pose_ref = f32[16,6,2048]{2,1,0:T(8,128)} copy(f32[16,6,2048]{2,0,1:T(8,128)S(1)} %copy-done) | data formatting | bytes 1572864 | tf_op args[1]
  3.6 9.8 %shard_map.73 = f32[16,48,48]{2,1,0:T(8,128)} custom-call(f32[16,3,2048]{2,1,0:T(4,128)} %copy.12.land_ref, f32[16,6,2048]{2,1,0:T(8,128)} %copy.13.pose_ref, s32[8,2048]{1,0:T(8,128)} %seg_ref.1, f32[8,2048]{1,0:T(8,128)} %frac_ref.1, s32[1,2048]{1,0:T(1,128)} %bitcast.26), custom_call_target="tpu_custom_call" | custom-call | tf_op jit(solution)/shard_map/pallas_call | solution.py:75
  13.4 1.4 %copy.14 = f32[16,48,48]{0,2,1:T(8,128)S(1)} copy(f32[16,48,48]{2,1,0:T(8,128)} %shard_map.73) | data formatting | bytes 294912 | tf_op jit(solution)/shard_map/pallas_call | solution.py:75
  14.8 0.7 convolution_bitcast_fusion
  15.4 0.9 %copy.16 = f32[16,8,8,6,6]{1,0,4,3,2:T(8,128)S(1)} copy(f32[16,8,8,6,6]{0,2,4,3,1:T(8,128)S(1)} %convolution_bitcast_fusion) | data formatting | bytes 294912 | tf_op jit(solution)/shard_map/bienf,ind->bidef/transpose | solution.py:97
  16.4 0.0 copy-start.2
  16.4 1.2 %reshape.70 = f32[128,288]{0,1:T(8,128)S(1)} reshape(f32[16,8,8,6,6]{1,0,4,3,2:T(8,128)S(1)} %copy.16) | data formatting | bytes 294912 | tf_op jit(solution)/shard_map/reshape | solution.py:108
  17.5 0.0 copy-done.2
  17.5 0.1 iota_add_fusion
  17.6 0.5 fusion.2
  18.1 3.3 %collective-permute-start = (f32[256,288]{0,1:T(8,128)S(1)}, f32[256,288]{0,1:T(8,128)S(1)}, u32[]{:S(2)}, u32[]{:S(2)}) collective-permute-start(f32[256,288]{0,1:T(8,128)S(1)} %constant_dynamic-slice_fusion.1), channel_id=1, source_target_pairs={{0,2},{1,3},{2,0},{3,1},{4,6},{5,7},{6,4},{7,5},{8,10},{9,11},{10,... | collective-permute-start | bytes 884744 | tf_op jit(solution)/shard_map/ppermute | solution.py:200
  21.4 7.1 %collective-permute-done = f32[256,288]{0,1:T(8,128)S(1)} collective-permute-done((f32[256,288]{0,1:T(8,128)S(1)}, f32[256,288]{0,1:T(8,128)S(1)}, u32[]{:S(2)}, u32[]{:S(2)}) %collective-permute-start) | collective-permute-done | bytes 294944 | tf_op jit(solution)/shard_map/ppermute | solution.py:200
  28.5 1.7 %collective-permute-start.1 = (f32[128,288]{0,1:T(8,128)S(1)}, f32[128,288]{0,1:T(8,128)S(1)}, u32[]{:S(2)}, u32[]{:S(2)}) collective-permute-start(f32[128,288]{0,1:T(8,128)S(1)} %constant_dynamic-slice_fusion), channel_id=1, source_target_pairs={{0,1},{1,0},{2,3},{3,2},{4,5},{5,4},{6,7},{7,6},{8,9},{9,8},{10,11... | collective-permute-start | bytes 442376 | tf_op jit(solution)/shard_map/ppermute | solution.py:200
  30.2 3.6 %collective-permute-done.1 = f32[128,288]{0,1:T(8,128)S(1)} collective-permute-done((f32[128,288]{0,1:T(8,128)S(1)}, f32[128,288]{0,1:T(8,128)S(1)}, u32[]{:S(2)}, u32[]{:S(2)}) %collective-permute-start.1) | collective-permute-done | bytes 147488 | tf_op jit(solution)/shard_map/ppermute | solution.py:200
  33.8 0.1 collective-permute-start.2
  33.9 1.4 %collective-permute-done.2 = f32[128,288]{0,1:T(8,128)S(1)} collective-permute-done((f32[128,288]{0,1:T(8,128)S(1)}, f32[128,288]{0,1:T(8,128)S(1)}, u32[]{:S(2)}, u32[]{:S(2)}) %collective-permute-start.2) | collective-permute-done | bytes 147488 | tf_op jit(solution)/shard_map/ppermute | solution.py:210
  35.3 0.2 collective-permute-start.3
  35.5 5.8 %collective-permute-done.3 = f32[128,288]{0,1:T(8,128)S(1)} collective-permute-done((f32[128,288]{0,1:T(8,128)S(1)}, f32[128,288]{0,1:T(8,128)S(1)}, u32[]{:S(2)}, u32[]{:S(2)}) %collective-permute-start.3) | collective-permute-done | bytes 147488 | tf_op jit(solution)/shard_map/ppermute | solution.py:210
  41.3 3.1 %collective-permute-start.4 = (f32[128,288]{0,1:T(8,128)S(1)}, f32[128,288]{0,1:T(8,128)S(1)}, u32[]{:S(2)}, u32[]{:S(2)}) collective-permute-start(f32[128,288]{0,1:T(8,128)S(1)} %add.99), channel_id=1, source_target_pairs={{0,16},{4,20},{8,24},{12,28},{16,0},{20,4},{24,8},{28,12},{32,48},... | collective-permute-start | bytes 442376 | tf_op jit(solution)/shard_map/ppermute | solution.py:210
  44.3 3.7 %collective-permute-done.4 = f32[128,288]{0,1:T(8,128)S(1)} collective-permute-done((f32[128,288]{0,1:T(8,128)S(1)}, f32[128,288]{0,1:T(8,128)S(1)}, u32[]{:S(2)}, u32[]{:S(2)}) %collective-permute-start.4) | collective-permute-done | bytes 147488 | tf_op jit(solution)/shard_map/ppermute | solution.py:210
  48.0 0.9 %collective-permute-start.5 = (f32[128,288]{0,1:T(8,128)S(1)}, f32[128,288]{0,1:T(8,128)S(1)}, u32[]{:S(2)}, u32[]{:S(2)}) collective-permute-start(f32[128,288]{0,1:T(8,128)S(1)} %add.100), channel_id=1, source_target_pairs={{0,32},{4,36},{8,40},{12,44},{16,48},{20,52},{24,56},{28,60},{32,0... | collective-permute-start | bytes 442376 | tf_op jit(solution)/shard_map/ppermute | solution.py:210
  48.9 5.1 %collective-permute-done.5 = f32[128,288]{0,1:T(8,128)S(1)} collective-permute-done((f32[128,288]{0,1:T(8,128)S(1)}, f32[128,288]{0,1:T(8,128)S(1)}, u32[]{:S(2)}, u32[]{:S(2)}) %collective-permute-start.5) | collective-permute-done | bytes 147488 | tf_op jit(solution)/shard_map/ppermute | solution.py:210
  54.1 0.8 collective-permute-start.6
  54.9 6.0 %collective-permute-done.6 = f32[128,288]{0,1:T(8,128)S(1)} collective-permute-done((f32[128,288]{0,1:T(8,128)S(1)}, f32[128,288]{0,1:T(8,128)S(1)}, u32[]{:S(2)}, u32[]{:S(2)}) %collective-permute-start.6) | collective-permute-done | bytes 147488 | tf_op jit(solution)/shard_map/ppermute | solution.py:210
  61.0 1.1 %copy.17 = f32[8,6,128,6]{3,2,1,0:T(8,128)S(1)} copy(f32[8,6,128,6]{2,1,3,0:T(8,128)S(1)} %bitcast.25) | data formatting | bytes 294912 | tf_op jit(solution)/shard_map/transpose | solution.py:223
  62.1 0.0 copy-start.1
  62.1 2.1 %reshape.72 = f32[48,768]{1,0:T(8,128)S(1)} reshape(f32[8,6,128,6]{3,2,1,0:T(8,128)S(1)} %copy.17) | data formatting | bytes 294912 | tf_op jit(solution)/shard_map/reshape | solution.py:224
  64.2 0.0 copy-done.1
  64.3 0.7 pad.4.yt_ref
  64.9 25.4 %shard_map.74 = f32[768,768]{1,0:T(8,128)} custom-call(f32[48,896]{1,0:T(8,128)} %pad.4.yt_ref), custom_call_target="tpu_custom_call" | custom-call | tf_op jit(solution)/shard_map/pallas_call | solution.py:178
  (14 shorter events, 0.3 us)
Async XLA Ops:
  0.0 2.1 %copy-start = (f32[16,6,2048]{2,0,1:T(8,128)S(1)}, f32[16,6,2048]{2,0,1:T(8,128)}, u32[]{:S(2)}) copy-start(f32[16,6,2048]{2,0,1:T(8,128)} %param.8) | copy-start | bytes 2359300
  16.4 1.2 %copy-start.2 = (s32[16]{0:T(128)S(1)}, s32[16]{0:T(128)}, u32[]{:S(2)}) copy-start(s32[16]{0:T(128)} %param.12) | copy-start | bytes 196
  18.1 10.3 %collective-permute-start = (f32[256,288]{0,1:T(8,128)S(1)}, f32[256,288]{0,1:T(8,128)S(1)}, u32[]{:S(2)}, u32[]{:S(2)}) collective-permute-start(f32[256,288]{0,1:T(8,128)S(1)} %constant_dynamic-slice_fusion.1), channel_id=1, source_target_pairs={{0,2},{1,3},{2,0},{3,1},{4,6},{5,7},{6,4},{7,5},{8,10},{9,11},{10,... | collective-permute-start | bytes 884744 | tf_op jit(solution)/shard_map/ppermute | solution.py:200
  28.5 5.2 %collective-permute-start.1 = (f32[128,288]{0,1:T(8,128)S(1)}, f32[128,288]{0,1:T(8,128)S(1)}, u32[]{:S(2)}, u32[]{:S(2)}) collective-permute-start(f32[128,288]{0,1:T(8,128)S(1)} %constant_dynamic-slice_fusion), channel_id=1, source_target_pairs={{0,1},{1,0},{2,3},{3,2},{4,5},{5,4},{6,7},{7,6},{8,9},{9,8},{10,11... | collective-permute-start | bytes 442376 | tf_op jit(solution)/shard_map/ppermute | solution.py:200
  33.8 1.5 %collective-permute-start.2 = (f32[128,288]{0,1:T(8,128)S(1)}, f32[128,288]{0,1:T(8,128)S(1)}, u32[]{:S(2)}, u32[]{:S(2)}) collective-permute-start(f32[128,288]{0,1:T(8,128)S(1)} %dynamic-slice_add_fusion.1), channel_id=1, source_target_pairs={{0,4},{4,0},{8,12},{12,8},{16,20},{20,16},{24,28},{28,24},{32,36},... | collective-permute-start | bytes 442376 | tf_op jit(solution)/shard_map/ppermute | solution.py:210
  35.3 6.0 %collective-permute-start.3 = (f32[128,288]{0,1:T(8,128)S(1)}, f32[128,288]{0,1:T(8,128)S(1)}, u32[]{:S(2)}, u32[]{:S(2)}) collective-permute-start(f32[128,288]{0,1:T(8,128)S(1)} %add.98), channel_id=1, source_target_pairs={{0,8},{4,12},{8,0},{12,4},{16,24},{20,28},{24,16},{28,20},{32,40},... | collective-permute-start | bytes 442376 | tf_op jit(solution)/shard_map/ppermute | solution.py:210
  41.3 6.7 %collective-permute-start.4 = (f32[128,288]{0,1:T(8,128)S(1)}, f32[128,288]{0,1:T(8,128)S(1)}, u32[]{:S(2)}, u32[]{:S(2)}) collective-permute-start(f32[128,288]{0,1:T(8,128)S(1)} %add.99), channel_id=1, source_target_pairs={{0,16},{4,20},{8,24},{12,28},{16,0},{20,4},{24,8},{28,12},{32,48},... | collective-permute-start | bytes 442376 | tf_op jit(solution)/shard_map/ppermute | solution.py:210
  48.0 6.1 %collective-permute-start.5 = (f32[128,288]{0,1:T(8,128)S(1)}, f32[128,288]{0,1:T(8,128)S(1)}, u32[]{:S(2)}, u32[]{:S(2)}) collective-permute-start(f32[128,288]{0,1:T(8,128)S(1)} %add.100), channel_id=1, source_target_pairs={{0,32},{4,36},{8,40},{12,44},{16,48},{20,52},{24,56},{28,60},{32,0... | collective-permute-start | bytes 442376 | tf_op jit(solution)/shard_map/ppermute | solution.py:210
  54.1 6.9 %collective-permute-start.6 = (f32[128,288]{0,1:T(8,128)S(1)}, f32[128,288]{0,1:T(8,128)S(1)}, u32[]{:S(2)}, u32[]{:S(2)}) collective-permute-start(f32[128,288]{0,1:T(8,128)S(1)} %add.101), channel_id=1, source_target_pairs={{0,64},{4,68},{8,72},{12,76},{16,80},{20,84},{24,88},{28,92},{32,9... | collective-permute-start | bytes 442376 | tf_op jit(solution)/shard_map/ppermute | solution.py:210
  62.1 2.1 %copy-start.1 = (f32[768]{0:T(1024)S(1)}, f32[768]{0:T(1024)}, u32[]{:S(2)}) copy-start(f32[768]{0:T(1024)} %param.13) | copy-start | bytes 9220

commit v8 on v7

--- a/solution.py
+++ b/solution.py
@@ -135,11 +135,10 @@
     lane = lax.broadcasted_iota(jnp.int32, (rows, WIDTH), 1)
     row = lax.broadcasted_iota(jnp.int32, (rows, 1), 0)
 
-    def panel(p, carry):
+    def panel(p, blk):
         j0 = pl.multiple_of(p * PANEL, PANEL)
         base = pl.multiple_of((p // (128 // PANEL)) * 128, 128)
         off = j0 - base
-        blk = w_ref[pl.ds(j0, rows), pl.ds(base, WIDTH)]
         first = blk[:, :128]
         lane_first = lane[:, :128]
         cols = [jnp.sum(jnp.where(lane_first == off + t, first, 0.0), axis=1, keepdims=True)
@@ -163,11 +162,14 @@
         trail = blk[PANEL:, :]
         for t in range(PANEL):
             trail = trail - lcols[t][PANEL:, :] * rrows[t]
-        start = pl.multiple_of(j0 + PANEL, PANEL)
-        w_ref[pl.ds(start, band_w), pl.ds(base, WIDTH)] = trail
-        return carry
-
-    lax.fori_loop(0, n // PANEL, panel, 0)
+        nxt = jnp.minimum(((p + 1) // (128 // PANEL)) * 128, w_ref.shape[1] - WIDTH)
+        nxt = pl.multiple_of(nxt, 128)
+        moved = jnp.concatenate([trail[:, 128:], jnp.zeros((band_w, WIDTH - 128), jnp.float32)], axis=1)
+        trail = jnp.where(nxt != base, moved, trail)
+        fresh = w_ref[pl.ds(pl.multiple_of(j0 + rows, PANEL), PANEL), pl.ds(nxt, WIDTH)]
+        return jnp.concatenate([trail, fresh], axis=0)
+
+    lax.fori_loop(0, n // PANEL, panel, w_ref[0:rows, 0:WIDTH])
     out_ref[...] = r_ref[0:n, 0:n]
 
 
@@ -187,20 +189,14 @@
     )(yt)
 
 
-def halve_over(band, axis):
+def scatter_sum(band, axis):
     n = lax.axis_size(axis)
-    c = lax.axis_index(axis)
-    size = band.shape[0]
-    s = n // 2
-    while s >= 1:
-        half = size // 2
-        bit = (c // s) % 2
-        keep = lax.dynamic_slice_in_dim(band, bit * half, half, 0)
-        send = lax.dynamic_slice_in_dim(band, (1 - bit) * half, half, 0)
-        band = keep + lax.ppermute(send, axis, [(i, i ^ s) for i in range(n)])
-        size = half
-        s //= 2
-    return band
+    got = lax.all_to_all(band, axis, 0, 0, tiled=True)
+    got = got.reshape(n, band.shape[0] // n, band.shape[1])
+    total = got[0]
+    for j in range(1, n):
+        total = total + got[j]
+    return total
 
 
 def butterfly_sum(band, axis):
@@ -218,7 +214,7 @@
     group_cols = damping.shape[0]
     num_groups = lax.axis_size("cols")
     band = place_band(skew_blocks(grams), block_base, group_cols, num_groups)
-    band_whole = butterfly_sum(halve_over(band, "cols"), "rows")
+    band_whole = butterfly_sum(scatter_sum(band, "cols"), "rows")
     group_knots = group_cols // KDOF
     yt = band_whole.reshape(group_knots, WIN_KNOTS, KDOF, KDOF).transpose(1, 3, 0, 2)
     yt = yt.reshape(WIN_KNOTS * KDOF, group_cols)

time: 90.6 us -> 89.1 us (0.983)
  blocking collectives: 0 us -> 14.4 us
  waiting for transfers between devices: 32.6 us -> 22.4 us
  starting transfers between devices: 10 us -> 4.72 us
    all_to_all x0 -> x1, blocking collectives: none -> 14.4 us  [scatter_sum(): got = lax.all_to_all(band, axis, 0, 0, tiled=True)]
    ppermute x2 -> x0, waiting for transfers between devices: 10.6 us -> none  [halve_over(): band = keep + lax.ppermute(send, axis, [(i, i ^ s) for i in range(n)])]
    ppermute x2 -> x0, starting transfers between devices: 4.94 us -> none  [halve_over(): band = keep + lax.ppermute(send, axis, [(i, i ^ s) for i in range(n)])]
  transfers between devices with their start and end apart: 7 -> 5, of which waited for: 7 -> 5; matrix products, arithmetic and copies ran while one was open for 0% -> 0% of each run, Pallas kernels for 0% -> 0%
where the time goes in v8:
time: 89.1 us; the launch traced here: 88.8 us
  Pallas kernels  34.5 us (39%)
  waiting for transfers between devices  22.4 us (25%)
  blocking collectives  14.4 us (16%)
  local copies, waits for them, and re-layouts  11.3 us (13%)
  starting transfers between devices  4.72 us (5%)
  matrix products  1.16 us (1%)
    pallas_call x1, Pallas kernels, band_cholesky(): pl.pallas_call(functools.partial(band_chol_kernel, n, band_w), out_shape=...  24.7 us
    ppermute x5, waiting for transfers between devices, butterfly_sum(): band = band + lax.ppermute(band, axis, [(i, i ^ s) for i in range(n)])  22.4 us
    all_to_all x1, blocking collectives, scatter_sum(): got = lax.all_to_all(band, axis, 0, 0, tiled=True)  14.4 us
    pallas_call x1, Pallas kernels, block_grams_kernel(): pl.pallas_call(gram_kernel, out_shape=jax.ShapeDtypeStruct((num_blocks, w...  9.79 us
    ppermute x5, starting transfers between devices, butterfly_sum(): band = band + lax.ppermute(band, axis, [(i, i ^ s) for i in range(n)])  4.72 us
    unnamed x8, local copies, waits for them, and re-layouts  3.72 us
    reshape x1, local copies, waits for them, and re-layouts, local(): yt = yt.reshape(WIN_KNOTS * KDOF, group_cols)  2.12 us
  transfers between devices with their start and end apart: 5, of which 5 were waited for; matrix products, arithmetic and copies ran while one was open for 0% of the time, Pallas kernels for 0%

profile of v8, /device:TPU:38, one launch (start us, length us, event | category | flops | bytes accessed | tf_op | source)
XLA Modules:
  0.0 88.8 jit_solution(6658289922749911271)
XLA Ops:
  0.0 0.0 copy-start
  0.0 2.6 %copy.13.pose_ref = f32[16,6,2048]{2,1,0:T(8,128)} copy(f32[16,6,2048]{2,0,1:T(8,128)} %param.8) | data formatting | bytes 1572864 | tf_op args[1]
  2.6 0.0 copy-done
  2.6 1.1 %copy.12.land_ref = f32[16,3,2048]{2,1,0:T(4,128)} copy(f32[16,3,2048]{2,0,1:T(8,128)S(1)} %copy-done) | data formatting | bytes 786432 | tf_op args[0]
  3.7 9.8 %shard_map.73 = f32[16,48,48]{2,1,0:T(8,128)} custom-call(f32[16,3,2048]{2,1,0:T(4,128)} %copy.12.land_ref, f32[16,6,2048]{2,1,0:T(8,128)} %copy.13.pose_ref, s32[8,2048]{1,0:T(8,128)} %seg_ref.1, f32[8,2048]{1,0:T(8,128)} %frac_ref.1, s32[1,2048]{1,0:T(1,128)} %bitcast.29), custom_call_target="tpu_custom_call" | custom-call | tf_op jit(solution)/shard_map/pallas_call | solution.py:75
  13.5 1.4 %copy.14 = f32[16,48,48]{0,2,1:T(8,128)S(1)} copy(f32[16,48,48]{2,1,0:T(8,128)} %shard_map.73) | data formatting | bytes 294912 | tf_op jit(solution)/shard_map/pallas_call | solution.py:75
  14.9 0.7 convolution_bitcast_fusion
  15.6 0.9 %copy.16 = f32[16,8,8,6,6]{1,0,4,3,2:T(8,128)S(1)} copy(f32[16,8,8,6,6]{0,2,4,3,1:T(8,128)S(1)} %convolution_bitcast_fusion) | data formatting | bytes 294912 | tf_op jit(solution)/shard_map/bienf,ind->bidef/transpose | solution.py:97
  16.5 0.0 copy-start.2
  16.5 1.2 %reshape.71 = f32[128,288,1]{0,1,2:T(8,128)S(1)} reshape(f32[16,8,8,6,6]{1,0,4,3,2:T(8,128)S(1)} %copy.16) | data formatting | bytes 294912 | tf_op jit(solution)/shard_map/reshape | solution.py:108
  17.7 0.0 copy-done.2
  17.7 0.1 add.78
  17.8 0.1 add.79
  17.9 0.1 add.81
  18.0 0.5 fusion.1
  18.5 14.4 %all_to_all.6 = f32[4,128,288]{1,2,0:T(8,128)S(1)} all-to-all(f32[4,128,288]{1,2,0:T(8,128)S(1)} %fusion.1), channel_id=1, replica_groups=mesh['rows'=32,'cols'=4] {'cols'}, dimensions={0} | all-to-all | bytes 1179648 | tf_op jit(solution)/shard_map/all_to_all | solution.py:194
  33.0 0.1 collective-permute-start
  33.0 1.4 %collective-permute-done = f32[128,288]{0,1:T(8,128)S(1)} collective-permute-done((f32[128,288]{0,1:T(8,128)S(1)}, f32[128,288]{0,1:T(8,128)S(1)}, u32[]{:S(2)}, u32[]{:S(2)}) %collective-permute-start) | collective-permute-done | bytes 147488 | tf_op jit(solution)/shard_map/ppermute | solution.py:206
  34.4 0.2 collective-permute-start.1
  34.6 5.8 %collective-permute-done.1 = f32[128,288]{0,1:T(8,128)S(1)} collective-permute-done((f32[128,288]{0,1:T(8,128)S(1)}, f32[128,288]{0,1:T(8,128)S(1)}, u32[]{:S(2)}, u32[]{:S(2)}) %collective-permute-start.1) | collective-permute-done | bytes 147488 | tf_op jit(solution)/shard_map/ppermute | solution.py:206
  40.4 3.1 %collective-permute-start.2 = (f32[128,288]{0,1:T(8,128)S(1)}, f32[128,288]{0,1:T(8,128)S(1)}, u32[]{:S(2)}, u32[]{:S(2)}) collective-permute-start(f32[128,288]{0,1:T(8,128)S(1)} %add.89), channel_id=1, source_target_pairs={{0,16},{4,20},{8,24},{12,28},{16,0},{20,4},{24,8},{28,12},{32,48},... | collective-permute-start | bytes 442376 | tf_op jit(solution)/shard_map/ppermute | solution.py:206
  43.5 3.7 %collective-permute-done.2 = f32[128,288]{0,1:T(8,128)S(1)} collective-permute-done((f32[128,288]{0,1:T(8,128)S(1)}, f32[128,288]{0,1:T(8,128)S(1)}, u32[]{:S(2)}, u32[]{:S(2)}) %collective-permute-start.2) | collective-permute-done | bytes 147488 | tf_op jit(solution)/shard_map/ppermute | solution.py:206
  47.2 0.9 %collective-permute-start.3 = (f32[128,288]{0,1:T(8,128)S(1)}, f32[128,288]{0,1:T(8,128)S(1)}, u32[]{:S(2)}, u32[]{:S(2)}) collective-permute-start(f32[128,288]{0,1:T(8,128)S(1)} %add.90), channel_id=1, source_target_pairs={{0,32},{4,36},{8,40},{12,44},{16,48},{20,52},{24,56},{28,60},{32,0... | collective-permute-start | bytes 442376 | tf_op jit(solution)/shard_map/ppermute | solution.py:206
  48.1 5.3 %collective-permute-done.3 = f32[128,288]{0,1:T(8,128)S(1)} collective-permute-done((f32[128,288]{0,1:T(8,128)S(1)}, f32[128,288]{0,1:T(8,128)S(1)}, u32[]{:S(2)}, u32[]{:S(2)}) %collective-permute-start.3) | collective-permute-done | bytes 147488 | tf_op jit(solution)/shard_map/ppermute | solution.py:206
  53.4 0.5 collective-permute-start.4
  53.9 6.2 %collective-permute-done.4 = f32[128,288]{0,1:T(8,128)S(1)} collective-permute-done((f32[128,288]{0,1:T(8,128)S(1)}, f32[128,288]{0,1:T(8,128)S(1)}, u32[]{:S(2)}, u32[]{:S(2)}) %collective-permute-start.4) | collective-permute-done | bytes 147488 | tf_op jit(solution)/shard_map/ppermute | solution.py:206
  60.2 1.1 %copy.17 = f32[8,6,128,6]{3,2,1,0:T(8,128)S(1)} copy(f32[8,6,128,6]{2,1,3,0:T(8,128)S(1)} %bitcast.28) | data formatting | bytes 294912 | tf_op jit(solution)/shard_map/transpose | solution.py:219
  61.3 0.0 copy-start.1
  61.3 2.1 %reshape.69 = f32[48,768]{1,0:T(8,128)S(1)} reshape(f32[8,6,128,6]{3,2,1,0:T(8,128)S(1)} %copy.17) | data formatting | bytes 294912 | tf_op jit(solution)/shard_map/reshape | solution.py:220
  63.4 0.0 copy-done.1
  63.4 0.7 pad.4.yt_ref
  64.1 24.7 %shard_map.74 = f32[768,768]{1,0:T(8,128)} custom-call(f32[48,896]{1,0:T(8,128)} %pad.4.yt_ref), custom_call_target="tpu_custom_call" | custom-call | tf_op jit(solution)/shard_map/pallas_call | solution.py:180
  (14 shorter events, 0.2 us)
Async XLA Ops:
  0.0 2.6 %copy-start = (f32[16,3,2048]{2,0,1:T(8,128)S(1)}, f32[16,3,2048]{2,0,1:T(8,128)}, u32[]{:S(2)}) copy-start(f32[16,3,2048]{2,0,1:T(8,128)} %param.7) | copy-start | bytes 1179652
  16.5 1.2 %copy-start.2 = (s32[16]{0:T(128)S(1)}, s32[16]{0:T(128)}, u32[]{:S(2)}) copy-start(s32[16]{0:T(128)} %param.12) | copy-start | bytes 196
  33.0 1.5 %collective-permute-start = (f32[128,288]{0,1:T(8,128)S(1)}, f32[128,288]{0,1:T(8,128)S(1)}, u32[]{:S(2)}, u32[]{:S(2)}) collective-permute-start(f32[128,288]{0,1:T(8,128)S(1)} %fusion.3), channel_id=1, source_target_pairs={{0,4},{4,0},{8,12},{12,8},{16,20},{20,16},{24,28},{28,24},{32,36},... | collective-permute-start | bytes 442376 | tf_op jit(solution)/shard_map/ppermute | solution.py:206
  34.4 6.0 %collective-permute-start.1 = (f32[128,288]{0,1:T(8,128)S(1)}, f32[128,288]{0,1:T(8,128)S(1)}, u32[]{:S(2)}, u32[]{:S(2)}) collective-permute-start(f32[128,288]{0,1:T(8,128)S(1)} %fusion.14), channel_id=1, source_target_pairs={{0,8},{4,12},{8,0},{12,4},{16,24},{20,28},{24,16},{28,20},{32,40},... | collective-permute-start | bytes 442376 | tf_op jit(solution)/shard_map/ppermute | solution.py:206
  40.4 6.7 %collective-permute-start.2 = (f32[128,288]{0,1:T(8,128)S(1)}, f32[128,288]{0,1:T(8,128)S(1)}, u32[]{:S(2)}, u32[]{:S(2)}) collective-permute-start(f32[128,288]{0,1:T(8,128)S(1)} %add.89), channel_id=1, source_target_pairs={{0,16},{4,20},{8,24},{12,28},{16,0},{20,4},{24,8},{28,12},{32,48},... | collective-permute-start | bytes 442376 | tf_op jit(solution)/shard_map/ppermute | solution.py:206
  47.2 6.2 %collective-permute-start.3 = (f32[128,288]{0,1:T(8,128)S(1)}, f32[128,288]{0,1:T(8,128)S(1)}, u32[]{:S(2)}, u32[]{:S(2)}) collective-permute-start(f32[128,288]{0,1:T(8,128)S(1)} %add.90), channel_id=1, source_target_pairs={{0,32},{4,36},{8,40},{12,44},{16,48},{20,52},{24,56},{28,60},{32,0... | collective-permute-start | bytes 442376 | tf_op jit(solution)/shard_map/ppermute | solution.py:206
  53.4 6.7 %collective-permute-start.4 = (f32[128,288]{0,1:T(8,128)S(1)}, f32[128,288]{0,1:T(8,128)S(1)}, u32[]{:S(2)}, u32[]{:S(2)}) collective-permute-start(f32[128,288]{0,1:T(8,128)S(1)} %add.91), channel_id=1, source_target_pairs={{0,64},{4,68},{8,72},{12,76},{16,80},{20,84},{24,88},{28,92},{32,9... | collective-permute-start | bytes 442376 | tf_op jit(solution)/shard_map/ppermute | solution.py:206
  61.3 2.1 %copy-start.1 = (f32[768]{0:T(1024)S(1)}, f32[768]{0:T(1024)}, u32[]{:S(2)}) copy-start(f32[768]{0:T(1024)} %param.13) | copy-start | bytes 9220

commit v9 on v8

--- a/solution.py
+++ b/solution.py
@@ -12,7 +12,7 @@
 WIDTH = 256
 
 
-def gram_kernel(land_ref, pose_ref, seg_ref, frac_ref, len_ref, out_ref):
+def gram_kernel(ldim, pdim, land_ref, pose_ref, seg_ref, frac_ref, len_ref, out_ref):
     num_obs, lanes = seg_ref.shape
     rows = 2 * num_obs
     u = frac_ref[...]
@@ -38,9 +38,8 @@
         mask = observed[j:j + 1, :]
         for i in range(2):
             r = 2 * j + i
-            land.append(land_ref[r] * mask)
-            pose = pose_ref[r] * mask
-            knots.append(jnp.concatenate([pose[e:e + 1, :] * weight for e in range(KDOF)], axis=0))
+            land.append(jnp.concatenate([land_ref[c, r:r + 1, :] for c in range(ldim)], axis=0) * mask)
+            knots.append(jnp.concatenate([(pose_ref[e, r:r + 1, :] * mask) * weight for e in range(KDOF)], axis=0))
     for k in range(3):
         column = [land[r][k:k + 1, :] for r in range(k, rows)]
         total = column[0] * column[0]
@@ -73,18 +72,19 @@
     blk = sub * per_step
     width = WIN_KNOTS * KDOF
     return pl.pallas_call(
-        gram_kernel,
+        functools.partial(gram_kernel, ldim, pdim),
         out_shape=jax.ShapeDtypeStruct((num_blocks, width, width), jnp.float32),
         grid=(num_blocks // per_step,),
         in_specs=[
-            pl.BlockSpec((rows, ldim, blk), lambda b: (0, 0, b)),
-            pl.BlockSpec((rows, pdim, blk), lambda b: (0, 0, b)),
+            pl.BlockSpec((ldim, rows, blk), lambda b: (0, 0, b)),
+            pl.BlockSpec((pdim, rows, blk), lambda b: (0, 0, b)),
             pl.BlockSpec((num_obs, blk), lambda b: (0, b)),
             pl.BlockSpec((num_obs, blk), lambda b: (0, b)),
             pl.BlockSpec((1, blk), lambda b: (0, b)),
         ],
         out_specs=pl.BlockSpec((per_step, width, width), lambda b: (b, 0, 0)),
-    )(land_jac, pose_jac, segment, knot_frac, track_len.reshape(1, landmarks))
+    )(jnp.transpose(land_jac, (1, 0, 2)), jnp.transpose(pose_jac, (1, 0, 2)),
+      segment, knot_frac, track_len.reshape(1, landmarks))
 
 
 def skew_blocks(grams):
@@ -112,13 +112,14 @@
 def band_chol_kernel(n, band_w, yt_ref, out_ref, w_ref, r_ref):
     w_ref[...] = jnp.zeros_like(w_ref)
     r_ref[...] = jnp.zeros_like(r_ref)
-    lanes = lax.broadcasted_iota(jnp.int32, (band_w, WIDTH), 1)
     for k in range(n // KDOF):
         lo = KDOF * k
         tile = (lo // 128) * 128
-        blk = yt_ref[:, tile:tile + WIDTH]
+        span = 128 if lo - tile + KDOF <= 128 else WIDTH
+        lanes = lax.broadcasted_iota(jnp.int32, (band_w, span), 1)
+        blk = yt_ref[:, tile:tile + span]
         keep = (lanes >= lo - tile) & (lanes < lo - tile + KDOF)
-        w_ref[lo:lo + band_w, tile:tile + WIDTH] += jnp.where(keep, blk, 0.0)
+        w_ref[lo:lo + band_w, tile:tile + span] += jnp.where(keep, blk, 0.0)
     tiles = n // 128
     ri = lax.broadcasted_iota(jnp.int32, (128, 128), 0)
     ci = lax.broadcasted_iota(jnp.int32, (128, 128), 1)

time: 89.1 us -> 85.7 us (0.962)
  local copies, waits for them, and re-layouts: 11.3 us -> 7.59 us
    unnamed x8 -> x4, local copies, waits for them, and re-layouts: 3.72 us -> 0.01 us
where the time goes in v9:
time: 85.7 us; the launch traced here: 85.5 us
  Pallas kernels  34.9 us (41%)
  waiting for transfers between devices  22.4 us (26%)
  blocking collectives  14.4 us (17%)
  local copies, waits for them, and re-layouts  7.59 us (9%)
  starting transfers between devices  4.66 us (5%)
  matrix products  1.16 us (1%)
    pallas_call x1, Pallas kernels, band_cholesky(): pl.pallas_call(functools.partial(band_chol_kernel, n, band_w), out_shape=...  24.5 us
    ppermute x5, waiting for transfers between devices, butterfly_sum(): band = band + lax.ppermute(band, axis, [(i, i ^ s) for i in range(n)])  22.4 us
    all_to_all x1, blocking collectives, scatter_sum(): got = lax.all_to_all(band, axis, 0, 0, tiled=True)  14.4 us
    pallas_call x1, Pallas kernels, block_grams_kernel(): pl.pallas_call(functools.partial(gram_kernel, ldim, pdim), out_shape=jax....  10.3 us
    ppermute x5, starting transfers between devices, butterfly_sum(): band = band + lax.ppermute(band, axis, [(i, i ^ s) for i in range(n)])  4.66 us
    reshape x1, local copies, waits for them, and re-layouts, local(): yt = yt.reshape(WIN_KNOTS * KDOF, group_cols)  2.12 us
  transfers between devices with their start and end apart: 5, of which 5 were waited for; matrix products, arithmetic and copies ran while one was open for 0% of the time, Pallas kernels for 0%

profile of v9, /device:TPU:38, one launch (start us, length us, event | category | flops | bytes accessed | tf_op | source)
XLA Modules:
  0.0 85.5 jit_solution(2489906734625319454)
XLA Ops:
  0.0 10.3 %shard_map.73 = f32[16,48,48]{2,1,0:T(8,128)} custom-call(f32[3,16,2048]{2,1,0:T(8,128)} %bitcast.32, f32[6,16,2048]{2,1,0:T(8,128)} %bitcast.31, s32[8,2048]{1,0:T(8,128)} %seg_ref.1, f32[8,2048]{1,0:T(8,128)} %frac_ref.1, s32[1,2048]{1,0:T(1,128)} %bitcast.33), custom_call_target="tpu_custom_call" | custom-call | tf_op jit(solution)/shard_map/pallas_call | solution.py:74
  10.3 1.4 %copy.10 = f32[16,48,48]{0,2,1:T(8,128)S(1)} copy(f32[16,48,48]{2,1,0:T(8,128)} %shard_map.73) | data formatting | bytes 294912 | tf_op jit(solution)/shard_map/pallas_call | solution.py:74
  11.7 0.7 convolution_bitcast_fusion
  12.4 0.9 %copy.12 = f32[16,8,8,6,6]{1,0,4,3,2:T(8,128)S(1)} copy(f32[16,8,8,6,6]{0,2,4,3,1:T(8,128)S(1)} %convolution_bitcast_fusion) | data formatting | bytes 294912 | tf_op jit(solution)/shard_map/bienf,ind->bidef/transpose | solution.py:97
  13.3 0.0 copy-start.1
  13.3 1.2 %reshape.71 = f32[128,288,1]{0,1,2:T(8,128)S(1)} reshape(f32[16,8,8,6,6]{1,0,4,3,2:T(8,128)S(1)} %copy.12) | data formatting | bytes 294912 | tf_op jit(solution)/shard_map/reshape | solution.py:108
  14.5 0.0 copy-done.1
  14.5 0.1 add.78
  14.6 0.1 add.79
  14.7 0.1 add.81
  14.8 0.5 fusion.1
  15.3 14.4 %all_to_all.6 = f32[4,128,288]{1,2,0:T(8,128)S(1)} all-to-all(f32[4,128,288]{1,2,0:T(8,128)S(1)} %fusion.1), channel_id=1, replica_groups=mesh['rows'=32,'cols'=4] {'cols'}, dimensions={0} | all-to-all | bytes 1179648 | tf_op jit(solution)/shard_map/all_to_all | solution.py:195
  29.8 0.1 collective-permute-start
  29.9 1.4 %collective-permute-done = f32[128,288]{0,1:T(8,128)S(1)} collective-permute-done((f32[128,288]{0,1:T(8,128)S(1)}, f32[128,288]{0,1:T(8,128)S(1)}, u32[]{:S(2)}, u32[]{:S(2)}) %collective-permute-start) | collective-permute-done | bytes 147488 | tf_op jit(solution)/shard_map/ppermute | solution.py:207
  31.3 0.2 collective-permute-start.1
  31.5 5.8 %collective-permute-done.1 = f32[128,288]{0,1:T(8,128)S(1)} collective-permute-done((f32[128,288]{0,1:T(8,128)S(1)}, f32[128,288]{0,1:T(8,128)S(1)}, u32[]{:S(2)}, u32[]{:S(2)}) %collective-permute-start.1) | collective-permute-done | bytes 147488 | tf_op jit(solution)/shard_map/ppermute | solution.py:207
  37.3 3.0 %collective-permute-start.2 = (f32[128,288]{0,1:T(8,128)S(1)}, f32[128,288]{0,1:T(8,128)S(1)}, u32[]{:S(2)}, u32[]{:S(2)}) collective-permute-start(f32[128,288]{0,1:T(8,128)S(1)} %add.89), channel_id=1, source_target_pairs={{0,16},{4,20},{8,24},{12,28},{16,0},{20,4},{24,8},{28,12},{32,48},... | collective-permute-start | bytes 442376 | tf_op jit(solution)/shard_map/ppermute | solution.py:207
  40.3 3.7 %collective-permute-done.2 = f32[128,288]{0,1:T(8,128)S(1)} collective-permute-done((f32[128,288]{0,1:T(8,128)S(1)}, f32[128,288]{0,1:T(8,128)S(1)}, u32[]{:S(2)}, u32[]{:S(2)}) %collective-permute-start.2) | collective-permute-done | bytes 147488 | tf_op jit(solution)/shard_map/ppermute | solution.py:207
  44.0 0.9 %collective-permute-start.3 = (f32[128,288]{0,1:T(8,128)S(1)}, f32[128,288]{0,1:T(8,128)S(1)}, u32[]{:S(2)}, u32[]{:S(2)}) collective-permute-start(f32[128,288]{0,1:T(8,128)S(1)} %add.90), channel_id=1, source_target_pairs={{0,32},{4,36},{8,40},{12,44},{16,48},{20,52},{24,56},{28,60},{32,0... | collective-permute-start | bytes 442376 | tf_op jit(solution)/shard_map/ppermute | solution.py:207
  44.9 5.3 %collective-permute-done.3 = f32[128,288]{0,1:T(8,128)S(1)} collective-permute-done((f32[128,288]{0,1:T(8,128)S(1)}, f32[128,288]{0,1:T(8,128)S(1)}, u32[]{:S(2)}, u32[]{:S(2)}) %collective-permute-start.3) | collective-permute-done | bytes 147488 | tf_op jit(solution)/shard_map/ppermute | solution.py:207
  50.3 0.5 collective-permute-start.4
  50.8 6.3 %collective-permute-done.4 = f32[128,288]{0,1:T(8,128)S(1)} collective-permute-done((f32[128,288]{0,1:T(8,128)S(1)}, f32[128,288]{0,1:T(8,128)S(1)}, u32[]{:S(2)}, u32[]{:S(2)}) %collective-permute-start.4) | collective-permute-done | bytes 147488 | tf_op jit(solution)/shard_map/ppermute | solution.py:207
  57.1 1.1 %copy.13 = f32[8,6,128,6]{3,2,1,0:T(8,128)S(1)} copy(f32[8,6,128,6]{2,1,3,0:T(8,128)S(1)} %bitcast.30) | data formatting | bytes 294912 | tf_op jit(solution)/shard_map/transpose | solution.py:220
  58.1 0.0 copy-start
  58.1 2.1 %reshape.69 = f32[48,768]{1,0:T(8,128)S(1)} reshape(f32[8,6,128,6]{3,2,1,0:T(8,128)S(1)} %copy.13) | data formatting | bytes 294912 | tf_op jit(solution)/shard_map/reshape | solution.py:221
  60.3 0.0 copy-done
  60.3 0.7 pad.4.yt_ref
  61.0 24.5 %shard_map.74 = f32[768,768]{1,0:T(8,128)} custom-call(f32[48,896]{1,0:T(8,128)} %pad.4.yt_ref), custom_call_target="tpu_custom_call" | custom-call | tf_op jit(solution)/shard_map/pallas_call | solution.py:181
  (14 shorter events, 0.2 us)
Async XLA Ops:
  13.3 1.2 %copy-start.1 = (s32[16]{0:T(128)S(1)}, s32[16]{0:T(128)}, u32[]{:S(2)}) copy-start(s32[16]{0:T(128)} %param.12) | copy-start | bytes 196
  29.8 1.5 %collective-permute-start = (f32[128,288]{0,1:T(8,128)S(1)}, f32[128,288]{0,1:T(8,128)S(1)}, u32[]{:S(2)}, u32[]{:S(2)}) collective-permute-start(f32[128,288]{0,1:T(8,128)S(1)} %fusion.3), channel_id=1, source_target_pairs={{0,4},{4,0},{8,12},{12,8},{16,20},{20,16},{24,28},{28,24},{32,36},... | collective-permute-start | bytes 442376 | tf_op jit(solution)/shard_map/ppermute | solution.py:207
  31.3 6.0 %collective-permute-start.1 = (f32[128,288]{0,1:T(8,128)S(1)}, f32[128,288]{0,1:T(8,128)S(1)}, u32[]{:S(2)}, u32[]{:S(2)}) collective-permute-start(f32[128,288]{0,1:T(8,128)S(1)} %fusion.14), channel_id=1, source_target_pairs={{0,8},{4,12},{8,0},{12,4},{16,24},{20,28},{24,16},{28,20},{32,40},... | collective-permute-start | bytes 442376 | tf_op jit(solution)/shard_map/ppermute | solution.py:207
  37.3 6.7 %collective-permute-start.2 = (f32[128,288]{0,1:T(8,128)S(1)}, f32[128,288]{0,1:T(8,128)S(1)}, u32[]{:S(2)}, u32[]{:S(2)}) collective-permute-start(f32[128,288]{0,1:T(8,128)S(1)} %add.89), channel_id=1, source_target_pairs={{0,16},{4,20},{8,24},{12,28},{16,0},{20,4},{24,8},{28,12},{32,48},... | collective-permute-start | bytes 442376 | tf_op jit(solution)/shard_map/ppermute | solution.py:207
  44.0 6.2 %collective-permute-start.3 = (f32[128,288]{0,1:T(8,128)S(1)}, f32[128,288]{0,1:T(8,128)S(1)}, u32[]{:S(2)}, u32[]{:S(2)}) collective-permute-start(f32[128,288]{0,1:T(8,128)S(1)} %add.90), channel_id=1, source_target_pairs={{0,32},{4,36},{8,40},{12,44},{16,48},{20,52},{24,56},{28,60},{32,0... | collective-permute-start | bytes 442376 | tf_op jit(solution)/shard_map/ppermute | solution.py:207
  50.3 6.7 %collective-permute-start.4 = (f32[128,288]{0,1:T(8,128)S(1)}, f32[128,288]{0,1:T(8,128)S(1)}, u32[]{:S(2)}, u32[]{:S(2)}) collective-permute-start(f32[128,288]{0,1:T(8,128)S(1)} %add.91), channel_id=1, source_target_pairs={{0,64},{4,68},{8,72},{12,76},{16,80},{20,84},{24,88},{28,92},{32,9... | collective-permute-start | bytes 442376 | tf_op jit(solution)/shard_map/ppermute | solution.py:207
  58.1 2.1 %copy-start = (f32[768]{0:T(1024)S(1)}, f32[768]{0:T(1024)}, u32[]{:S(2)}) copy-start(f32[768]{0:T(1024)} %param.13) | copy-start | bytes 9220

commit v10 on v9

--- a/solution.py
+++ b/solution.py
@@ -109,7 +109,7 @@
     return jnp.dot(onehot, flat, precision=lax.Precision.HIGHEST)
 
 
-def band_chol_kernel(n, band_w, yt_ref, out_ref, w_ref, r_ref):
+def band_chol_kernel(n, band_w, yt_ref, damp_ref, out_ref, w_ref, r_ref):
     w_ref[...] = jnp.zeros_like(w_ref)
     r_ref[...] = jnp.zeros_like(r_ref)
     for k in range(n // KDOF):
@@ -130,7 +130,10 @@
             low = w_ref[128 * a:128 * a + 128, 128 * b:128 * b + 128]
             mirror = w_ref[128 * b:128 * b + 128, 128 * a:128 * a + 128].T
             upper = (ci + 128 * b) // KDOF > (ri + 128 * a) // KDOF
-            w_ref[128 * a:128 * a + 128, 128 * b:128 * b + 128] = jnp.where(upper, mirror, low)
+            tile_val = jnp.where(upper, mirror, low)
+            if a == b:
+                tile_val = tile_val + jnp.where(ri == ci, damp_ref[:, 128 * a:128 * a + 128], 0.0)
+            w_ref[128 * a:128 * a + 128, 128 * b:128 * b + 128] = tile_val
 
     rows = PANEL + band_w
     lane = lax.broadcasted_iota(jnp.int32, (rows, WIDTH), 1)
@@ -174,20 +177,19 @@
     out_ref[...] = r_ref[0:n, 0:n]
 
 
-def band_cholesky(yt, n):
+def band_cholesky(yt, damping, n):
     band_w = yt.shape[0]
     padded = n + 128
-    yt = jnp.pad(yt, ((0, 0), (0, padded - n)))
     return pl.pallas_call(
         functools.partial(band_chol_kernel, n, band_w),
         out_shape=jax.ShapeDtypeStruct((n, n), jnp.float32),
-        in_specs=[pl.BlockSpec(memory_space=pltpu.VMEM)],
+        in_specs=[pl.BlockSpec(memory_space=pltpu.VMEM)] * 2,
         out_specs=pl.BlockSpec(memory_space=pltpu.VMEM),
         scratch_shapes=[
             pltpu.VMEM((n + 64, padded), jnp.float32),
             pltpu.VMEM((n, padded), jnp.float32),
         ],
-    )(yt)
+    )(yt, damping.reshape(1, n))
 
 
 def scatter_sum(band, axis):
@@ -211,7 +213,7 @@
 
 def local(land_jac, pose_jac, segment, knot_frac, track_len, block_base, damping):
     num_blocks = block_base.shape[0]
-    grams = block_grams_kernel(land_jac, pose_jac, segment, knot_frac, track_len, num_blocks, 4)
+    grams = block_grams_kernel(land_jac, pose_jac, segment, knot_frac, track_len, num_blocks, 8)
     group_cols = damping.shape[0]
     num_groups = lax.axis_size("cols")
     band = place_band(skew_blocks(grams), block_base, group_cols, num_groups)
@@ -219,10 +221,7 @@
     group_knots = group_cols // KDOF
     yt = band_whole.reshape(group_knots, WIN_KNOTS, KDOF, KDOF).transpose(1, 3, 0, 2)
     yt = yt.reshape(WIN_KNOTS * KDOF, group_cols)
-    t = lax.broadcasted_iota(jnp.int32, yt.shape, 0)
-    i = lax.broadcasted_iota(jnp.int32, yt.shape, 1)
-    yt = yt + jnp.where(t == i % KDOF, damping[None, :], 0.0)
-    return band_cholesky(yt, group_cols)
+    return band_cholesky(yt, damping, group_cols)
 
 
 def solution(mesh):

time: 85.7 us -> 85.4 us (level)
  waiting for transfers between devices: 22.4 us -> 21.4 us
    ppermute x5, waiting for transfers between devices: 22.4 us -> 21.4 us  [butterfly_sum(): band = band + lax.ppermute(band, axis, [(i, i ^ s) for i in range(n)])]
  transfers between devices with their start and end apart: 5 -> 5, of which waited for: 5 -> 5; matrix products, arithmetic and copies ran while one was open for 0% -> 1% of each run, Pallas kernels for 0% -> 0%
where the time goes in v10:
time: 85.4 us; the launch traced here: 85.2 us
  Pallas kernels  34.6 us (41%)
  waiting for transfers between devices  21.4 us (25%)
  blocking collectives  14.4 us (17%)
  local copies, waits for them, and re-layouts  8.16 us (10%)
  starting transfers between devices  5.08 us (6%)
  matrix products  1.16 us (1%)
    pallas_call x1, Pallas kernels, band_cholesky(): pl.pallas_call(functools.partial(band_chol_kernel, n, band_w), out_shape=...  24.6 us
    ppermute x5, waiting for transfers between devices, butterfly_sum(): band = band + lax.ppermute(band, axis, [(i, i ^ s) for i in range(n)])  21.4 us
    all_to_all x1, blocking collectives, scatter_sum(): got = lax.all_to_all(band, axis, 0, 0, tiled=True)  14.4 us
    pallas_call x1, Pallas kernels, block_grams_kernel(): pl.pallas_call(functools.partial(gram_kernel, ldim, pdim), out_shape=jax....  10 us
    ppermute x5, starting transfers between devices, butterfly_sum(): band = band + lax.ppermute(band, axis, [(i, i ^ s) for i in range(n)])  5.08 us
    reshape x1, local copies, waits for them, and re-layouts, local(): yt = yt.reshape(WIN_KNOTS * KDOF, group_cols)  2.77 us
  transfers between devices with their start and end apart: 5, of which 5 were waited for; matrix products, arithmetic and copies ran while one was open for 1% of the time, Pallas kernels for 0%

profile of v10, /device:TPU:38, one launch (start us, length us, event | category | flops | bytes accessed | tf_op | source)
XLA Modules:
  0.0 85.2 jit_solution(11206743358865662302)
XLA Ops:
  0.0 10.0 %shard_map.73 = f32[16,48,48]{2,1,0:T(8,128)} custom-call(f32[3,16,2048]{2,1,0:T(8,128)} %bitcast.32, f32[6,16,2048]{2,1,0:T(8,128)} %bitcast.31, s32[8,2048]{1,0:T(8,128)} %seg_ref.1, f32[8,2048]{1,0:T(8,128)} %frac_ref.1, s32[1,2048]{1,0:T(1,128)} %bitcast.33), custom_call_target="tpu_custom_call" | custom-call | tf_op jit(solution)/shard_map/pallas_call | solution.py:74
  10.0 1.4 %copy.10 = f32[16,48,48]{0,2,1:T(8,128)S(1)} copy(f32[16,48,48]{2,1,0:T(8,128)} %shard_map.73) | data formatting | bytes 294912 | tf_op jit(solution)/shard_map/pallas_call | solution.py:74
  11.4 0.7 convolution_bitcast_fusion
  12.1 0.9 %copy.12 = f32[16,8,8,6,6]{1,0,4,3,2:T(8,128)S(1)} copy(f32[16,8,8,6,6]{0,2,4,3,1:T(8,128)S(1)} %convolution_bitcast_fusion) | data formatting | bytes 294912 | tf_op jit(solution)/shard_map/bienf,ind->bidef/transpose | solution.py:97
  13.0 0.0 copy-start.1
  13.0 1.2 %reshape.74 = f32[128,288,1]{0,1,2:T(8,128)S(1)} reshape(f32[16,8,8,6,6]{1,0,4,3,2:T(8,128)S(1)} %copy.12) | data formatting | bytes 294912 | tf_op jit(solution)/shard_map/reshape | solution.py:108
  14.2 0.0 copy-done.1
  14.2 0.1 add.66
  14.3 0.1 add.67
  14.4 0.1 add.69
  14.5 0.5 fusion.1
  15.0 14.4 %all_to_all.6 = f32[4,128,288]{1,2,0:T(8,128)S(1)} all-to-all(f32[4,128,288]{1,2,0:T(8,128)S(1)} %fusion.1), channel_id=1, replica_groups=mesh['rows'=32,'cols'=4] {'cols'}, dimensions={0} | all-to-all | bytes 1179648 | tf_op jit(solution)/shard_map/all_to_all | solution.py:197
  29.5 0.0 copy-start
  29.5 0.1 collective-permute-start
  29.6 1.4 %collective-permute-done = f32[128,288]{0,1:T(8,128)S(1)} collective-permute-done((f32[128,288]{0,1:T(8,128)S(1)}, f32[128,288]{0,1:T(8,128)S(1)}, u32[]{:S(2)}, u32[]{:S(2)}) %collective-permute-start) | collective-permute-done | bytes 147488 | tf_op jit(solution)/shard_map/ppermute | solution.py:209
  31.0 0.2 collective-permute-start.1
  31.2 5.8 %collective-permute-done.1 = f32[128,288]{0,1:T(8,128)S(1)} collective-permute-done((f32[128,288]{0,1:T(8,128)S(1)}, f32[128,288]{0,1:T(8,128)S(1)}, u32[]{:S(2)}, u32[]{:S(2)}) %collective-permute-start.1) | collective-permute-done | bytes 147488 | tf_op jit(solution)/shard_map/ppermute | solution.py:209
  37.0 3.1 %collective-permute-start.2 = (f32[128,288]{0,1:T(8,128)S(1)}, f32[128,288]{0,1:T(8,128)S(1)}, u32[]{:S(2)}, u32[]{:S(2)}) collective-permute-start(f32[128,288]{0,1:T(8,128)S(1)} %add.77), channel_id=1, source_target_pairs={{0,16},{4,20},{8,24},{12,28},{16,0},{20,4},{24,8},{28,12},{32,48},... | collective-permute-start | bytes 442376 | tf_op jit(solution)/shard_map/ppermute | solution.py:209
  40.0 3.7 %collective-permute-done.2 = f32[128,288]{0,1:T(8,128)S(1)} collective-permute-done((f32[128,288]{0,1:T(8,128)S(1)}, f32[128,288]{0,1:T(8,128)S(1)}, u32[]{:S(2)}, u32[]{:S(2)}) %collective-permute-start.2) | collective-permute-done | bytes 147488 | tf_op jit(solution)/shard_map/ppermute | solution.py:209
  43.7 0.9 %collective-permute-start.3 = (f32[128,288]{0,1:T(8,128)S(1)}, f32[128,288]{0,1:T(8,128)S(1)}, u32[]{:S(2)}, u32[]{:S(2)}) collective-permute-start(f32[128,288]{0,1:T(8,128)S(1)} %add.78), channel_id=1, source_target_pairs={{0,32},{4,36},{8,40},{12,44},{16,48},{20,52},{24,56},{28,60},{32,0... | collective-permute-start | bytes 442376 | tf_op jit(solution)/shard_map/ppermute | solution.py:209
  44.6 5.1 %collective-permute-done.3 = f32[128,288]{0,1:T(8,128)S(1)} collective-permute-done((f32[128,288]{0,1:T(8,128)S(1)}, f32[128,288]{0,1:T(8,128)S(1)}, u32[]{:S(2)}, u32[]{:S(2)}) %collective-permute-start.3) | collective-permute-done | bytes 147488 | tf_op jit(solution)/shard_map/ppermute | solution.py:209
  49.8 0.8 collective-permute-start.4
  50.6 0.0 copy-done
  50.6 0.6 reshape.72.damp_ref
  51.2 5.5 %collective-permute-done.4 = f32[128,288]{0,1:T(8,128)S(1)} collective-permute-done((f32[128,288]{0,1:T(8,128)S(1)}, f32[128,288]{0,1:T(8,128)S(1)}, u32[]{:S(2)}, u32[]{:S(2)}) %collective-permute-start.4) | collective-permute-done | bytes 147488 | tf_op jit(solution)/shard_map/ppermute | solution.py:209
  56.8 1.1 %copy.13 = f32[8,6,128,6]{3,2,1,0:T(8,128)S(1)} copy(f32[8,6,128,6]{2,1,3,0:T(8,128)S(1)} %bitcast.30) | data formatting | bytes 294912 | tf_op jit(solution)/shard_map/transpose | solution.py:222
  57.8 2.8 %reshape.71.yt_ref = f32[48,768]{1,0:T(8,128)} reshape(f32[8,6,128,6]{3,2,1,0:T(8,128)S(1)} %copy.13) | data formatting | bytes 294912 | tf_op jit(solution)/shard_map/reshape | solution.py:223
  60.6 24.6 %shard_map.74 = f32[768,768]{1,0:T(8,128)} custom-call(f32[48,768]{1,0:T(8,128)} %reshape.71.yt_ref, f32[1,768]{1,0:T(1,128)} %reshape.72.damp_ref), custom_call_target="tpu_custom_call" | custom-call | tf_op jit(solution)/shard_map/pallas_call | solution.py:183
  (11 shorter events, 0.2 us)
Async XLA Ops:
  13.0 1.2 %copy-start.1 = (s32[16]{0:T(128)S(1)}, s32[16]{0:T(128)}, u32[]{:S(2)}) copy-start(s32[16]{0:T(128)} %param.12) | copy-start | bytes 196
  29.5 21.2 %copy-start = (f32[768]{0:T(1024)S(1)}, f32[768]{0:T(1024)}, u32[]{:S(2)}) copy-start(f32[768]{0:T(1024)} %param.13) | copy-start | bytes 9220
  29.5 1.5 %collective-permute-start = (f32[128,288]{0,1:T(8,128)S(1)}, f32[128,288]{0,1:T(8,128)S(1)}, u32[]{:S(2)}, u32[]{:S(2)}) collective-permute-start(f32[128,288]{0,1:T(8,128)S(1)} %fusion.3), channel_id=1, source_target_pairs={{0,4},{4,0},{8,12},{12,8},{16,20},{20,16},{24,28},{28,24},{32,36},... | collective-permute-start | bytes 442376 | tf_op jit(solution)/shard_map/ppermute | solution.py:209
  31.0 6.0 %collective-permute-start.1 = (f32[128,288]{0,1:T(8,128)S(1)}, f32[128,288]{0,1:T(8,128)S(1)}, u32[]{:S(2)}, u32[]{:S(2)}) collective-permute-start(f32[128,288]{0,1:T(8,128)S(1)} %fusion.10), channel_id=1, source_target_pairs={{0,8},{4,12},{8,0},{12,4},{16,24},{20,28},{24,16},{28,20},{32,40},... | collective-permute-start | bytes 442376 | tf_op jit(solution)/shard_map/ppermute | solution.py:209
  37.0 6.7 %collective-permute-start.2 = (f32[128,288]{0,1:T(8,128)S(1)}, f32[128,288]{0,1:T(8,128)S(1)}, u32[]{:S(2)}, u32[]{:S(2)}) collective-permute-start(f32[128,288]{0,1:T(8,128)S(1)} %add.77), channel_id=1, source_target_pairs={{0,16},{4,20},{8,24},{12,28},{16,0},{20,4},{24,8},{28,12},{32,48},... | collective-permute-start | bytes 442376 | tf_op jit(solution)/shard_map/ppermute | solution.py:209
  43.7 6.1 %collective-permute-start.3 = (f32[128,288]{0,1:T(8,128)S(1)}, f32[128,288]{0,1:T(8,128)S(1)}, u32[]{:S(2)}, u32[]{:S(2)}) collective-permute-start(f32[128,288]{0,1:T(8,128)S(1)} %add.78), channel_id=1, source_target_pairs={{0,32},{4,36},{8,40},{12,44},{16,48},{20,52},{24,56},{28,60},{32,0... | collective-permute-start | bytes 442376 | tf_op jit(solution)/shard_map/ppermute | solution.py:209
  49.8 6.9 %collective-permute-start.4 = (f32[128,288]{0,1:T(8,128)S(1)}, f32[128,288]{0,1:T(8,128)S(1)}, u32[]{:S(2)}, u32[]{:S(2)}) collective-permute-start(f32[128,288]{0,1:T(8,128)S(1)} %add.79), channel_id=1, source_target_pairs={{0,64},{4,68},{8,72},{12,76},{16,80},{20,84},{24,88},{28,92},{32,9... | collective-permute-start | bytes 442376 | tf_op jit(solution)/shard_map/ppermute | solution.py:209

commit v11 on v10

--- a/solution.py
+++ b/solution.py
@@ -61,7 +61,7 @@
     for s in range(out_ref.shape[0]):
         reduced = jnp.concatenate([m[:, 128 * s:128 * (s + 1)] for m in knots[3:]], axis=1)
         out_ref[s] = lax.dot_general(reduced, reduced, (((1,), (1,)), ((), ())),
-                                     precision=lax.Precision.HIGHEST, preferred_element_type=jnp.float32)
+                                     precision=lax.Precision.HIGH, preferred_element_type=jnp.float32)
 
 
 def block_grams_kernel(land_jac, pose_jac, segment, knot_frac, track_len, num_blocks, per_step=1):

time: 85.4 us -> 83.4 us (0.977)
  Pallas kernels: 34.6 us -> 32.6 us
    pallas_call x1, Pallas kernels: 10 us -> 7.97 us  [block_grams_kernel(): pl.pallas_call(functools.partial(gram_kernel, ldim, pdim), out_shape=jax....]
where the time goes in v11:
time: 83.4 us; the launch traced here: 83.2 us
  Pallas kernels  32.6 us (39%)
  waiting for transfers between devices  21.8 us (26%)
  blocking collectives  14.4 us (17%)
  local copies, waits for them, and re-layouts  8.16 us (10%)
  starting transfers between devices  4.71 us (6%)
  matrix products  1.16 us (1%)
    pallas_call x1, Pallas kernels, band_cholesky(): pl.pallas_call(functools.partial(band_chol_kernel, n, band_w), out_shape=...  24.6 us
    ppermute x5, waiting for transfers between devices, butterfly_sum(): band = band + lax.ppermute(band, axis, [(i, i ^ s) for i in range(n)])  21.8 us
    all_to_all x1, blocking collectives, scatter_sum(): got = lax.all_to_all(band, axis, 0, 0, tiled=True)  14.4 us
    pallas_call x1, Pallas kernels, block_grams_kernel(): pl.pallas_call(functools.partial(gram_kernel, ldim, pdim), out_shape=jax....  7.97 us
    ppermute x5, starting transfers between devices, butterfly_sum(): band = band + lax.ppermute(band, axis, [(i, i ^ s) for i in range(n)])  4.71 us
    reshape x1, local copies, waits for them, and re-layouts, local(): yt = yt.reshape(WIN_KNOTS * KDOF, group_cols)  2.77 us
  transfers between devices with their start and end apart: 5, of which 5 were waited for; matrix products, arithmetic and copies ran while one was open for 1% of the time, Pallas kernels for 0%

profile of v11, /device:TPU:38, one launch (start us, length us, event | category | flops | bytes accessed | tf_op | source)
XLA Modules:
  0.0 83.2 jit_solution(6716184810027099280)
XLA Ops:
  0.0 8.0 %shard_map.73 = f32[16,48,48]{2,1,0:T(8,128)} custom-call(f32[3,16,2048]{2,1,0:T(8,128)} %bitcast.32, f32[6,16,2048]{2,1,0:T(8,128)} %bitcast.31, s32[8,2048]{1,0:T(8,128)} %seg_ref.1, f32[8,2048]{1,0:T(8,128)} %frac_ref.1, s32[1,2048]{1,0:T(1,128)} %bitcast.33), custom_call_target="tpu_custom_call" | custom-call | tf_op jit(solution)/shard_map/pallas_call | solution.py:74
  8.0 1.4 %copy.10 = f32[16,48,48]{0,2,1:T(8,128)S(1)} copy(f32[16,48,48]{2,1,0:T(8,128)} %shard_map.73) | data formatting | bytes 294912 | tf_op jit(solution)/shard_map/pallas_call | solution.py:74
  9.4 0.7 convolution_bitcast_fusion
  10.0 0.9 %copy.12 = f32[16,8,8,6,6]{1,0,4,3,2:T(8,128)S(1)} copy(f32[16,8,8,6,6]{0,2,4,3,1:T(8,128)S(1)} %convolution_bitcast_fusion) | data formatting | bytes 294912 | tf_op jit(solution)/shard_map/bienf,ind->bidef/transpose | solution.py:97
  11.0 0.0 copy-start.1
  11.0 1.2 %reshape.74 = f32[128,288,1]{0,1,2:T(8,128)S(1)} reshape(f32[16,8,8,6,6]{1,0,4,3,2:T(8,128)S(1)} %copy.12) | data formatting | bytes 294912 | tf_op jit(solution)/shard_map/reshape | solution.py:108
  12.1 0.0 copy-done.1
  12.2 0.1 add.66
  12.2 0.1 add.67
  12.3 0.1 add.69
  12.4 0.5 fusion.1
  13.0 14.4 %all_to_all.6 = f32[4,128,288]{1,2,0:T(8,128)S(1)} all-to-all(f32[4,128,288]{1,2,0:T(8,128)S(1)} %fusion.1), channel_id=1, replica_groups=mesh['rows'=32,'cols'=4] {'cols'}, dimensions={0} | all-to-all | bytes 1179648 | tf_op jit(solution)/shard_map/all_to_all | solution.py:197
  27.4 0.0 copy-start
  27.4 0.1 collective-permute-start
  27.5 1.4 %collective-permute-done = f32[128,288]{0,1:T(8,128)S(1)} collective-permute-done((f32[128,288]{0,1:T(8,128)S(1)}, f32[128,288]{0,1:T(8,128)S(1)}, u32[]{:S(2)}, u32[]{:S(2)}) %collective-permute-start) | collective-permute-done | bytes 147488 | tf_op jit(solution)/shard_map/ppermute | solution.py:209
  28.9 0.2 collective-permute-start.1
  29.1 5.8 %collective-permute-done.1 = f32[128,288]{0,1:T(8,128)S(1)} collective-permute-done((f32[128,288]{0,1:T(8,128)S(1)}, f32[128,288]{0,1:T(8,128)S(1)}, u32[]{:S(2)}, u32[]{:S(2)}) %collective-permute-start.1) | collective-permute-done | bytes 147488 | tf_op jit(solution)/shard_map/ppermute | solution.py:209
  34.9 3.1 %collective-permute-start.2 = (f32[128,288]{0,1:T(8,128)S(1)}, f32[128,288]{0,1:T(8,128)S(1)}, u32[]{:S(2)}, u32[]{:S(2)}) collective-permute-start(f32[128,288]{0,1:T(8,128)S(1)} %add.77), channel_id=1, source_target_pairs={{0,16},{4,20},{8,24},{12,28},{16,0},{20,4},{24,8},{28,12},{32,48},... | collective-permute-start | bytes 442376 | tf_op jit(solution)/shard_map/ppermute | solution.py:209
  38.0 3.7 %collective-permute-done.2 = f32[128,288]{0,1:T(8,128)S(1)} collective-permute-done((f32[128,288]{0,1:T(8,128)S(1)}, f32[128,288]{0,1:T(8,128)S(1)}, u32[]{:S(2)}, u32[]{:S(2)}) %collective-permute-start.2) | collective-permute-done | bytes 147488 | tf_op jit(solution)/shard_map/ppermute | solution.py:209
  41.7 0.9 %collective-permute-start.3 = (f32[128,288]{0,1:T(8,128)S(1)}, f32[128,288]{0,1:T(8,128)S(1)}, u32[]{:S(2)}, u32[]{:S(2)}) collective-permute-start(f32[128,288]{0,1:T(8,128)S(1)} %add.78), channel_id=1, source_target_pairs={{0,32},{4,36},{8,40},{12,44},{16,48},{20,52},{24,56},{28,60},{32,0... | collective-permute-start | bytes 442376 | tf_op jit(solution)/shard_map/ppermute | solution.py:209
  42.6 5.3 %collective-permute-done.3 = f32[128,288]{0,1:T(8,128)S(1)} collective-permute-done((f32[128,288]{0,1:T(8,128)S(1)}, f32[128,288]{0,1:T(8,128)S(1)}, u32[]{:S(2)}, u32[]{:S(2)}) %collective-permute-start.3) | collective-permute-done | bytes 147488 | tf_op jit(solution)/shard_map/ppermute | solution.py:209
  47.9 0.5 collective-permute-start.4
  48.4 0.0 copy-done
  48.4 0.6 reshape.72.damp_ref
  49.0 5.7 %collective-permute-done.4 = f32[128,288]{0,1:T(8,128)S(1)} collective-permute-done((f32[128,288]{0,1:T(8,128)S(1)}, f32[128,288]{0,1:T(8,128)S(1)}, u32[]{:S(2)}, u32[]{:S(2)}) %collective-permute-start.4) | collective-permute-done | bytes 147488 | tf_op jit(solution)/shard_map/ppermute | solution.py:209
  54.7 1.1 %copy.13 = f32[8,6,128,6]{3,2,1,0:T(8,128)S(1)} copy(f32[8,6,128,6]{2,1,3,0:T(8,128)S(1)} %bitcast.30) | data formatting | bytes 294912 | tf_op jit(solution)/shard_map/transpose | solution.py:222
  55.8 2.8 %reshape.71.yt_ref = f32[48,768]{1,0:T(8,128)} reshape(f32[8,6,128,6]{3,2,1,0:T(8,128)S(1)} %copy.13) | data formatting | bytes 294912 | tf_op jit(solution)/shard_map/reshape | solution.py:223
  58.6 24.6 %shard_map.74 = f32[768,768]{1,0:T(8,128)} custom-call(f32[48,768]{1,0:T(8,128)} %reshape.71.yt_ref, f32[1,768]{1,0:T(1,128)} %reshape.72.damp_ref), custom_call_target="tpu_custom_call" | custom-call | tf_op jit(solution)/shard_map/pallas_call | solution.py:183
  (11 shorter events, 0.2 us)
Async XLA Ops:
  11.0 1.2 %copy-start.1 = (s32[16]{0:T(128)S(1)}, s32[16]{0:T(128)}, u32[]{:S(2)}) copy-start(s32[16]{0:T(128)} %param.12) | copy-start | bytes 196
  27.4 21.0 %copy-start = (f32[768]{0:T(1024)S(1)}, f32[768]{0:T(1024)}, u32[]{:S(2)}) copy-start(f32[768]{0:T(1024)} %param.13) | copy-start | bytes 9220
  27.4 1.5 %collective-permute-start = (f32[128,288]{0,1:T(8,128)S(1)}, f32[128,288]{0,1:T(8,128)S(1)}, u32[]{:S(2)}, u32[]{:S(2)}) collective-permute-start(f32[128,288]{0,1:T(8,128)S(1)} %fusion.3), channel_id=1, source_target_pairs={{0,4},{4,0},{8,12},{12,8},{16,20},{20,16},{24,28},{28,24},{32,36},... | collective-permute-start | bytes 442376 | tf_op jit(solution)/shard_map/ppermute | solution.py:209
  28.9 6.0 %collective-permute-start.1 = (f32[128,288]{0,1:T(8,128)S(1)}, f32[128,288]{0,1:T(8,128)S(1)}, u32[]{:S(2)}, u32[]{:S(2)}) collective-permute-start(f32[128,288]{0,1:T(8,128)S(1)} %fusion.10), channel_id=1, source_target_pairs={{0,8},{4,12},{8,0},{12,4},{16,24},{20,28},{24,16},{28,20},{32,40},... | collective-permute-start | bytes 442376 | tf_op jit(solution)/shard_map/ppermute | solution.py:209
  34.9 6.7 %collective-permute-start.2 = (f32[128,288]{0,1:T(8,128)S(1)}, f32[128,288]{0,1:T(8,128)S(1)}, u32[]{:S(2)}, u32[]{:S(2)}) collective-permute-start(f32[128,288]{0,1:T(8,128)S(1)} %add.77), channel_id=1, source_target_pairs={{0,16},{4,20},{8,24},{12,28},{16,0},{20,4},{24,8},{28,12},{32,48},... | collective-permute-start | bytes 442376 | tf_op jit(solution)/shard_map/ppermute | solution.py:209
  41.7 6.2 %collective-permute-start.3 = (f32[128,288]{0,1:T(8,128)S(1)}, f32[128,288]{0,1:T(8,128)S(1)}, u32[]{:S(2)}, u32[]{:S(2)}) collective-permute-start(f32[128,288]{0,1:T(8,128)S(1)} %add.78), channel_id=1, source_target_pairs={{0,32},{4,36},{8,40},{12,44},{16,48},{20,52},{24,56},{28,60},{32,0... | collective-permute-start | bytes 442376 | tf_op jit(solution)/shard_map/ppermute | solution.py:209
  47.9 6.7 %collective-permute-start.4 = (f32[128,288]{0,1:T(8,128)S(1)}, f32[128,288]{0,1:T(8,128)S(1)}, u32[]{:S(2)}, u32[]{:S(2)}) collective-permute-start(f32[128,288]{0,1:T(8,128)S(1)} %add.79), channel_id=1, source_target_pairs={{0,64},{4,68},{8,72},{12,76},{16,80},{20,84},{24,88},{28,92},{32,9... | collective-permute-start | bytes 442376 | tf_op jit(solution)/shard_map/ppermute | solution.py:209

commit v12 on v11

--- a/solution.py
+++ b/solution.py
@@ -94,7 +94,7 @@
     k2 = lax.broadcasted_iota(jnp.int32, (WIN_KNOTS, WIN_KNOTS, WIN_KNOTS), 1)
     d = lax.broadcasted_iota(jnp.int32, (WIN_KNOTS, WIN_KNOTS, WIN_KNOTS), 2)
     pick = (k2 == k1 + d).astype(jnp.float32)
-    return jnp.einsum("bienf,ind->bidef", g5, pick, precision=lax.Precision.HIGHEST)
+    return jnp.einsum("bienf,ind->bidef", g5, pick, precision=lax.Precision.HIGH)
 
 
 def place_band(skewed, block_start, group_cols, num_groups):
@@ -106,7 +106,7 @@
     row_id = lax.broadcasted_iota(jnp.int32, (rows, num_blocks, WIN_KNOTS), 0)
     onehot = (row_id == target[None]).astype(jnp.float32).reshape(rows, num_blocks * WIN_KNOTS)
     flat = skewed.reshape(num_blocks * WIN_KNOTS, WIN_KNOTS * KDOF * KDOF)
-    return jnp.dot(onehot, flat, precision=lax.Precision.HIGHEST)
+    return jnp.dot(onehot, flat, precision=lax.Precision.HIGH)
 
 
 def band_chol_kernel(n, band_w, yt_ref, damp_ref, out_ref, w_ref, r_ref):

time: 83.4 us -> 83.1 us (level)
  no operation moved by 1% of the time
where the time goes in v12:
time: 83.1 us; the launch traced here: 82.9 us
  Pallas kernels  32.6 us (39%)
  waiting for transfers between devices  21.8 us (26%)
  blocking collectives  14.4 us (17%)
  local copies, waits for them, and re-layouts  8.16 us (10%)
  starting transfers between devices  4.71 us (6%)
  matrix products  0.88 us (1%)
    pallas_call x1, Pallas kernels, band_cholesky(): pl.pallas_call(functools.partial(band_chol_kernel, n, band_w), out_shape=...  24.6 us
    ppermute x5, waiting for transfers between devices, butterfly_sum(): band = band + lax.ppermute(band, axis, [(i, i ^ s) for i in range(n)])  21.8 us
    all_to_all x1, blocking collectives, scatter_sum(): got = lax.all_to_all(band, axis, 0, 0, tiled=True)  14.4 us
    pallas_call x1, Pallas kernels, block_grams_kernel(): pl.pallas_call(functools.partial(gram_kernel, ldim, pdim), out_shape=jax....  7.97 us
    ppermute x5, starting transfers between devices, butterfly_sum(): band = band + lax.ppermute(band, axis, [(i, i ^ s) for i in range(n)])  4.71 us
    reshape x1, local copies, waits for them, and re-layouts, local(): yt = yt.reshape(WIN_KNOTS * KDOF, group_cols)  2.77 us
  transfers between devices with their start and end apart: 5, of which 5 were waited for; matrix products, arithmetic and copies ran while one was open for 1% of the time, Pallas kernels for 0%

profile of v12, /device:TPU:38, one launch (start us, length us, event | category | flops | bytes accessed | tf_op | source)
XLA Modules:
  0.0 82.9 jit_solution(10370759224946516803)
XLA Ops:
  0.0 8.0 %shard_map.73 = f32[16,48,48]{2,1,0:T(8,128)} custom-call(f32[3,16,2048]{2,1,0:T(8,128)} %bitcast.32, f32[6,16,2048]{2,1,0:T(8,128)} %bitcast.31, s32[8,2048]{1,0:T(8,128)} %seg_ref.1, f32[8,2048]{1,0:T(8,128)} %frac_ref.1, s32[1,2048]{1,0:T(1,128)} %bitcast.33), custom_call_target="tpu_custom_call" | custom-call | tf_op jit(solution)/shard_map/pallas_call | solution.py:74
  8.0 1.4 %copy.10 = f32[16,48,48]{0,2,1:T(8,128)S(1)} copy(f32[16,48,48]{2,1,0:T(8,128)} %shard_map.73) | data formatting | bytes 294912 | tf_op jit(solution)/shard_map/pallas_call | solution.py:74
  9.4 0.5 convolution_bitcast_fusion
  9.8 0.9 %copy.12 = f32[16,8,8,6,6]{1,0,4,3,2:T(8,128)S(1)} copy(f32[16,8,8,6,6]{0,2,4,3,1:T(8,128)S(1)} %convolution_bitcast_fusion) | data formatting | bytes 294912 | tf_op jit(solution)/shard_map/bienf,ind->bidef/transpose | solution.py:97
  10.8 0.0 copy-start.1
  10.8 1.2 %reshape.74 = f32[128,288,1]{0,1,2:T(8,128)S(1)} reshape(f32[16,8,8,6,6]{1,0,4,3,2:T(8,128)S(1)} %copy.12) | data formatting | bytes 294912 | tf_op jit(solution)/shard_map/reshape | solution.py:108
  11.9 0.0 copy-done.1
  12.0 0.1 add.66
  12.0 0.1 add.67
  12.1 0.1 add.69
  12.2 0.4 fusion.1
  12.7 14.4 %all_to_all.6 = f32[4,128,288]{1,2,0:T(8,128)S(1)} all-to-all(f32[4,128,288]{1,2,0:T(8,128)S(1)} %fusion.1), channel_id=1, replica_groups=mesh['rows'=32,'cols'=4] {'cols'}, dimensions={0} | all-to-all | bytes 1179648 | tf_op jit(solution)/shard_map/all_to_all | solution.py:197
  27.1 0.0 copy-start
  27.2 0.1 collective-permute-start
  27.2 1.4 %collective-permute-done = f32[128,288]{0,1:T(8,128)S(1)} collective-permute-done((f32[128,288]{0,1:T(8,128)S(1)}, f32[128,288]{0,1:T(8,128)S(1)}, u32[]{:S(2)}, u32[]{:S(2)}) %collective-permute-start) | collective-permute-done | bytes 147488 | tf_op jit(solution)/shard_map/ppermute | solution.py:209
  28.6 0.2 collective-permute-start.1
  28.8 5.8 %collective-permute-done.1 = f32[128,288]{0,1:T(8,128)S(1)} collective-permute-done((f32[128,288]{0,1:T(8,128)S(1)}, f32[128,288]{0,1:T(8,128)S(1)}, u32[]{:S(2)}, u32[]{:S(2)}) %collective-permute-start.1) | collective-permute-done | bytes 147488 | tf_op jit(solution)/shard_map/ppermute | solution.py:209
  34.6 3.1 %collective-permute-start.2 = (f32[128,288]{0,1:T(8,128)S(1)}, f32[128,288]{0,1:T(8,128)S(1)}, u32[]{:S(2)}, u32[]{:S(2)}) collective-permute-start(f32[128,288]{0,1:T(8,128)S(1)} %add.77), channel_id=1, source_target_pairs={{0,16},{4,20},{8,24},{12,28},{16,0},{20,4},{24,8},{28,12},{32,48},... | collective-permute-start | bytes 442376 | tf_op jit(solution)/shard_map/ppermute | solution.py:209
  37.7 3.7 %collective-permute-done.2 = f32[128,288]{0,1:T(8,128)S(1)} collective-permute-done((f32[128,288]{0,1:T(8,128)S(1)}, f32[128,288]{0,1:T(8,128)S(1)}, u32[]{:S(2)}, u32[]{:S(2)}) %collective-permute-start.2) | collective-permute-done | bytes 147488 | tf_op jit(solution)/shard_map/ppermute | solution.py:209
  41.4 0.9 %collective-permute-start.3 = (f32[128,288]{0,1:T(8,128)S(1)}, f32[128,288]{0,1:T(8,128)S(1)}, u32[]{:S(2)}, u32[]{:S(2)}) collective-permute-start(f32[128,288]{0,1:T(8,128)S(1)} %add.78), channel_id=1, source_target_pairs={{0,32},{4,36},{8,40},{12,44},{16,48},{20,52},{24,56},{28,60},{32,0... | collective-permute-start | bytes 442376 | tf_op jit(solution)/shard_map/ppermute | solution.py:209
  42.3 5.3 %collective-permute-done.3 = f32[128,288]{0,1:T(8,128)S(1)} collective-permute-done((f32[128,288]{0,1:T(8,128)S(1)}, f32[128,288]{0,1:T(8,128)S(1)}, u32[]{:S(2)}, u32[]{:S(2)}) %collective-permute-start.3) | collective-permute-done | bytes 147488 | tf_op jit(solution)/shard_map/ppermute | solution.py:209
  47.7 0.5 collective-permute-start.4
  48.1 0.0 copy-done
  48.1 0.6 reshape.72.damp_ref
  48.7 5.7 %collective-permute-done.4 = f32[128,288]{0,1:T(8,128)S(1)} collective-permute-done((f32[128,288]{0,1:T(8,128)S(1)}, f32[128,288]{0,1:T(8,128)S(1)}, u32[]{:S(2)}, u32[]{:S(2)}) %collective-permute-start.4) | collective-permute-done | bytes 147488 | tf_op jit(solution)/shard_map/ppermute | solution.py:209
  54.4 1.1 %copy.13 = f32[8,6,128,6]{3,2,1,0:T(8,128)S(1)} copy(f32[8,6,128,6]{2,1,3,0:T(8,128)S(1)} %bitcast.30) | data formatting | bytes 294912 | tf_op jit(solution)/shard_map/transpose | solution.py:222
  55.5 2.8 %reshape.71.yt_ref = f32[48,768]{1,0:T(8,128)} reshape(f32[8,6,128,6]{3,2,1,0:T(8,128)S(1)} %copy.13) | data formatting | bytes 294912 | tf_op jit(solution)/shard_map/reshape | solution.py:223
  58.3 24.6 %shard_map.74 = f32[768,768]{1,0:T(8,128)} custom-call(f32[48,768]{1,0:T(8,128)} %reshape.71.yt_ref, f32[1,768]{1,0:T(1,128)} %reshape.72.damp_ref), custom_call_target="tpu_custom_call" | custom-call | tf_op jit(solution)/shard_map/pallas_call | solution.py:183
  (11 shorter events, 0.2 us)
Async XLA Ops:
  10.8 1.2 %copy-start.1 = (s32[16]{0:T(128)S(1)}, s32[16]{0:T(128)}, u32[]{:S(2)}) copy-start(s32[16]{0:T(128)} %param.12) | copy-start | bytes 196
  27.1 21.0 %copy-start = (f32[768]{0:T(1024)S(1)}, f32[768]{0:T(1024)}, u32[]{:S(2)}) copy-start(f32[768]{0:T(1024)} %param.13) | copy-start | bytes 9220
  27.2 1.5 %collective-permute-start = (f32[128,288]{0,1:T(8,128)S(1)}, f32[128,288]{0,1:T(8,128)S(1)}, u32[]{:S(2)}, u32[]{:S(2)}) collective-permute-start(f32[128,288]{0,1:T(8,128)S(1)} %fusion.3), channel_id=1, source_target_pairs={{0,4},{4,0},{8,12},{12,8},{16,20},{20,16},{24,28},{28,24},{32,36},... | collective-permute-start | bytes 442376 | tf_op jit(solution)/shard_map/ppermute | solution.py:209
  28.6 6.0 %collective-permute-start.1 = (f32[128,288]{0,1:T(8,128)S(1)}, f32[128,288]{0,1:T(8,128)S(1)}, u32[]{:S(2)}, u32[]{:S(2)}) collective-permute-start(f32[128,288]{0,1:T(8,128)S(1)} %fusion.10), channel_id=1, source_target_pairs={{0,8},{4,12},{8,0},{12,4},{16,24},{20,28},{24,16},{28,20},{32,40},... | collective-permute-start | bytes 442376 | tf_op jit(solution)/shard_map/ppermute | solution.py:209
  34.6 6.7 %collective-permute-start.2 = (f32[128,288]{0,1:T(8,128)S(1)}, f32[128,288]{0,1:T(8,128)S(1)}, u32[]{:S(2)}, u32[]{:S(2)}) collective-permute-start(f32[128,288]{0,1:T(8,128)S(1)} %add.77), channel_id=1, source_target_pairs={{0,16},{4,20},{8,24},{12,28},{16,0},{20,4},{24,8},{28,12},{32,48},... | collective-permute-start | bytes 442376 | tf_op jit(solution)/shard_map/ppermute | solution.py:209
  41.4 6.2 %collective-permute-start.3 = (f32[128,288]{0,1:T(8,128)S(1)}, f32[128,288]{0,1:T(8,128)S(1)}, u32[]{:S(2)}, u32[]{:S(2)}) collective-permute-start(f32[128,288]{0,1:T(8,128)S(1)} %add.78), channel_id=1, source_target_pairs={{0,32},{4,36},{8,40},{12,44},{16,48},{20,52},{24,56},{28,60},{32,0... | collective-permute-start | bytes 442376 | tf_op jit(solution)/shard_map/ppermute | solution.py:209
  47.7 6.7 %collective-permute-start.4 = (f32[128,288]{0,1:T(8,128)S(1)}, f32[128,288]{0,1:T(8,128)S(1)}, u32[]{:S(2)}, u32[]{:S(2)}) collective-permute-start(f32[128,288]{0,1:T(8,128)S(1)} %add.79), channel_id=1, source_target_pairs={{0,64},{4,68},{8,72},{12,76},{16,80},{20,84},{24,88},{28,92},{32,9... | collective-permute-start | bytes 442376 | tf_op jit(solution)/shard_map/ppermute | solution.py:209

commit v13 on v12

--- a/solution.py
+++ b/solution.py
@@ -109,9 +109,9 @@
     return jnp.dot(onehot, flat, precision=lax.Precision.HIGH)
 
 
-def band_chol_kernel(n, band_w, yt_ref, damp_ref, out_ref, w_ref, r_ref):
+def band_chol_kernel(n, band_w, yt_ref, damp_ref, out_ref, w_ref):
     w_ref[...] = jnp.zeros_like(w_ref)
-    r_ref[...] = jnp.zeros_like(r_ref)
+    out_ref[...] = jnp.zeros_like(out_ref)
     for k in range(n // KDOF):
         lo = KDOF * k
         tile = (lo // 128) * 128
@@ -162,7 +162,16 @@
             for t1 in range(t):
                 acc = acc - lcols[t1][t:t + 1, :] * rrows[t1]
             rrows.append(jnp.where(lane[0:1, :] >= off + t, acc * invs[t], 0.0))
-        r_ref[pl.ds(j0, PANEL), pl.ds(base, WIDTH)] = jnp.concatenate(rrows, axis=0)
+        rp = jnp.concatenate(rrows, axis=0)
+        last = n - 128
+
+        @pl.when(base < last)
+        def _():
+            out_ref[pl.ds(j0, PANEL), pl.ds(base, WIDTH)] = rp
+
+        @pl.when(base >= last)
+        def _():
+            out_ref[pl.ds(j0, PANEL), pl.ds(last, 128)] = rp[:, :128]
         trail = blk[PANEL:, :]
         for t in range(PANEL):
             trail = trail - lcols[t][PANEL:, :] * rrows[t]
@@ -174,7 +183,6 @@
         return jnp.concatenate([trail, fresh], axis=0)
 
     lax.fori_loop(0, n // PANEL, panel, w_ref[0:rows, 0:WIDTH])
-    out_ref[...] = r_ref[0:n, 0:n]
 
 
 def band_cholesky(yt, damping, n):
@@ -187,7 +195,6 @@
         out_specs=pl.BlockSpec(memory_space=pltpu.VMEM),
         scratch_shapes=[
             pltpu.VMEM((n + 64, padded), jnp.float32),
-            pltpu.VMEM((n, padded), jnp.float32),
         ],
     )(yt, damping.reshape(1, n))
 

time: 83.1 us -> 83.6 us (level)
  no operation moved by 1% of the time
where the time goes in v13:
time: 83.6 us; the launch traced here: 83.4 us
  Pallas kernels  33.1 us (40%)
  waiting for transfers between devices  21.8 us (26%)
  blocking collectives  14.4 us (17%)
  local copies, waits for them, and re-layouts  8.16 us (10%)
  starting transfers between devices  4.71 us (6%)
  matrix products  0.88 us (1%)
    pallas_call x1, Pallas kernels, band_cholesky(): pl.pallas_call(functools.partial(band_chol_kernel, n, band_w), out_shape=...  25.1 us
    ppermute x5, waiting for transfers between devices, butterfly_sum(): band = band + lax.ppermute(band, axis, [(i, i ^ s) for i in range(n)])  21.8 us
    all_to_all x1, blocking collectives, scatter_sum(): got = lax.all_to_all(band, axis, 0, 0, tiled=True)  14.4 us
    pallas_call x1, Pallas kernels, block_grams_kernel(): pl.pallas_call(functools.partial(gram_kernel, ldim, pdim), out_shape=jax....  7.97 us
    ppermute x5, starting transfers between devices, butterfly_sum(): band = band + lax.ppermute(band, axis, [(i, i ^ s) for i in range(n)])  4.71 us
    reshape x1, local copies, waits for them, and re-layouts, local(): yt = yt.reshape(WIN_KNOTS * KDOF, group_cols)  2.77 us
  transfers between devices with their start and end apart: 5, of which 5 were waited for; matrix products, arithmetic and copies ran while one was open for 1% of the time, Pallas kernels for 0%

profile of v13, /device:TPU:38, one launch (start us, length us, event | category | flops | bytes accessed | tf_op | source)
XLA Modules:
  0.0 83.4 jit_solution(15920847968060543415)
XLA Ops:
  0.0 8.0 %shard_map.73 = f32[16,48,48]{2,1,0:T(8,128)} custom-call(f32[3,16,2048]{2,1,0:T(8,128)} %bitcast.32, f32[6,16,2048]{2,1,0:T(8,128)} %bitcast.31, s32[8,2048]{1,0:T(8,128)} %seg_ref.1, f32[8,2048]{1,0:T(8,128)} %frac_ref.1, s32[1,2048]{1,0:T(1,128)} %bitcast.33), custom_call_target="tpu_custom_call" | custom-call | tf_op jit(solution)/shard_map/pallas_call | solution.py:74
  8.0 1.4 %copy.10 = f32[16,48,48]{0,2,1:T(8,128)S(1)} copy(f32[16,48,48]{2,1,0:T(8,128)} %shard_map.73) | data formatting | bytes 294912 | tf_op jit(solution)/shard_map/pallas_call | solution.py:74
  9.4 0.5 convolution_bitcast_fusion
  9.8 0.9 %copy.12 = f32[16,8,8,6,6]{1,0,4,3,2:T(8,128)S(1)} copy(f32[16,8,8,6,6]{0,2,4,3,1:T(8,128)S(1)} %convolution_bitcast_fusion) | data formatting | bytes 294912 | tf_op jit(solution)/shard_map/bienf,ind->bidef/transpose | solution.py:97
  10.8 0.0 copy-start.1
  10.8 1.2 %reshape.74 = f32[128,288,1]{0,1,2:T(8,128)S(1)} reshape(f32[16,8,8,6,6]{1,0,4,3,2:T(8,128)S(1)} %copy.12) | data formatting | bytes 294912 | tf_op jit(solution)/shard_map/reshape | solution.py:108
  11.9 0.0 copy-done.1
  12.0 0.1 add.66
  12.0 0.1 add.67
  12.1 0.1 add.69
  12.2 0.4 fusion.1
  12.7 14.4 %all_to_all.6 = f32[4,128,288]{1,2,0:T(8,128)S(1)} all-to-all(f32[4,128,288]{1,2,0:T(8,128)S(1)} %fusion.1), channel_id=1, replica_groups=mesh['rows'=32,'cols'=4] {'cols'}, dimensions={0} | all-to-all | bytes 1179648 | tf_op jit(solution)/shard_map/all_to_all | solution.py:204
  27.1 0.0 copy-start
  27.2 0.1 collective-permute-start
  27.2 1.4 %collective-permute-done = f32[128,288]{0,1:T(8,128)S(1)} collective-permute-done((f32[128,288]{0,1:T(8,128)S(1)}, f32[128,288]{0,1:T(8,128)S(1)}, u32[]{:S(2)}, u32[]{:S(2)}) %collective-permute-start) | collective-permute-done | bytes 147488 | tf_op jit(solution)/shard_map/ppermute | solution.py:216
  28.6 0.2 collective-permute-start.1
  28.8 5.8 %collective-permute-done.1 = f32[128,288]{0,1:T(8,128)S(1)} collective-permute-done((f32[128,288]{0,1:T(8,128)S(1)}, f32[128,288]{0,1:T(8,128)S(1)}, u32[]{:S(2)}, u32[]{:S(2)}) %collective-permute-start.1) | collective-permute-done | bytes 147488 | tf_op jit(solution)/shard_map/ppermute | solution.py:216
  34.6 3.1 %collective-permute-start.2 = (f32[128,288]{0,1:T(8,128)S(1)}, f32[128,288]{0,1:T(8,128)S(1)}, u32[]{:S(2)}, u32[]{:S(2)}) collective-permute-start(f32[128,288]{0,1:T(8,128)S(1)} %add.77), channel_id=1, source_target_pairs={{0,16},{4,20},{8,24},{12,28},{16,0},{20,4},{24,8},{28,12},{32,48},... | collective-permute-start | bytes 442376 | tf_op jit(solution)/shard_map/ppermute | solution.py:216
  37.7 3.7 %collective-permute-done.2 = f32[128,288]{0,1:T(8,128)S(1)} collective-permute-done((f32[128,288]{0,1:T(8,128)S(1)}, f32[128,288]{0,1:T(8,128)S(1)}, u32[]{:S(2)}, u32[]{:S(2)}) %collective-permute-start.2) | collective-permute-done | bytes 147488 | tf_op jit(solution)/shard_map/ppermute | solution.py:216
  41.4 0.9 %collective-permute-start.3 = (f32[128,288]{0,1:T(8,128)S(1)}, f32[128,288]{0,1:T(8,128)S(1)}, u32[]{:S(2)}, u32[]{:S(2)}) collective-permute-start(f32[128,288]{0,1:T(8,128)S(1)} %add.78), channel_id=1, source_target_pairs={{0,32},{4,36},{8,40},{12,44},{16,48},{20,52},{24,56},{28,60},{32,0... | collective-permute-start | bytes 442376 | tf_op jit(solution)/shard_map/ppermute | solution.py:216
  42.3 5.3 %collective-permute-done.3 = f32[128,288]{0,1:T(8,128)S(1)} collective-permute-done((f32[128,288]{0,1:T(8,128)S(1)}, f32[128,288]{0,1:T(8,128)S(1)}, u32[]{:S(2)}, u32[]{:S(2)}) %collective-permute-start.3) | collective-permute-done | bytes 147488 | tf_op jit(solution)/shard_map/ppermute | solution.py:216
  47.7 0.5 collective-permute-start.4
  48.1 0.0 copy-done
  48.1 0.6 reshape.72.damp_ref
  48.7 5.7 %collective-permute-done.4 = f32[128,288]{0,1:T(8,128)S(1)} collective-permute-done((f32[128,288]{0,1:T(8,128)S(1)}, f32[128,288]{0,1:T(8,128)S(1)}, u32[]{:S(2)}, u32[]{:S(2)}) %collective-permute-start.4) | collective-permute-done | bytes 147488 | tf_op jit(solution)/shard_map/ppermute | solution.py:216
  54.4 1.1 %copy.13 = f32[8,6,128,6]{3,2,1,0:T(8,128)S(1)} copy(f32[8,6,128,6]{2,1,3,0:T(8,128)S(1)} %bitcast.30) | data formatting | bytes 294912 | tf_op jit(solution)/shard_map/transpose | solution.py:229
  55.5 2.8 %reshape.71.yt_ref = f32[48,768]{1,0:T(8,128)} reshape(f32[8,6,128,6]{3,2,1,0:T(8,128)S(1)} %copy.13) | data formatting | bytes 294912 | tf_op jit(solution)/shard_map/reshape | solution.py:230
  58.3 25.1 %shard_map.74 = f32[768,768]{1,0:T(8,128)} custom-call(f32[48,768]{1,0:T(8,128)} %reshape.71.yt_ref, f32[1,768]{1,0:T(1,128)} %reshape.72.damp_ref), custom_call_target="tpu_custom_call" | custom-call | tf_op jit(solution)/shard_map/pallas_call | solution.py:191
  (11 shorter events, 0.2 us)
Async XLA Ops:
  10.8 1.2 %copy-start.1 = (s32[16]{0:T(128)S(1)}, s32[16]{0:T(128)}, u32[]{:S(2)}) copy-start(s32[16]{0:T(128)} %param.12) | copy-start | bytes 196
  27.1 21.0 %copy-start = (f32[768]{0:T(1024)S(1)}, f32[768]{0:T(1024)}, u32[]{:S(2)}) copy-start(f32[768]{0:T(1024)} %param.13) | copy-start | bytes 9220
  27.2 1.5 %collective-permute-start = (f32[128,288]{0,1:T(8,128)S(1)}, f32[128,288]{0,1:T(8,128)S(1)}, u32[]{:S(2)}, u32[]{:S(2)}) collective-permute-start(f32[128,288]{0,1:T(8,128)S(1)} %fusion.3), channel_id=1, source_target_pairs={{0,4},{4,0},{8,12},{12,8},{16,20},{20,16},{24,28},{28,24},{32,36},... | collective-permute-start | bytes 442376 | tf_op jit(solution)/shard_map/ppermute | solution.py:216
  28.6 6.0 %collective-permute-start.1 = (f32[128,288]{0,1:T(8,128)S(1)}, f32[128,288]{0,1:T(8,128)S(1)}, u32[]{:S(2)}, u32[]{:S(2)}) collective-permute-start(f32[128,288]{0,1:T(8,128)S(1)} %fusion.10), channel_id=1, source_target_pairs={{0,8},{4,12},{8,0},{12,4},{16,24},{20,28},{24,16},{28,20},{32,40},... | collective-permute-start | bytes 442376 | tf_op jit(solution)/shard_map/ppermute | solution.py:216
  34.6 6.7 %collective-permute-start.2 = (f32[128,288]{0,1:T(8,128)S(1)}, f32[128,288]{0,1:T(8,128)S(1)}, u32[]{:S(2)}, u32[]{:S(2)}) collective-permute-start(f32[128,288]{0,1:T(8,128)S(1)} %add.77), channel_id=1, source_target_pairs={{0,16},{4,20},{8,24},{12,28},{16,0},{20,4},{24,8},{28,12},{32,48},... | collective-permute-start | bytes 442376 | tf_op jit(solution)/shard_map/ppermute | solution.py:216
  41.4 6.2 %collective-permute-start.3 = (f32[128,288]{0,1:T(8,128)S(1)}, f32[128,288]{0,1:T(8,128)S(1)}, u32[]{:S(2)}, u32[]{:S(2)}) collective-permute-start(f32[128,288]{0,1:T(8,128)S(1)} %add.78), channel_id=1, source_target_pairs={{0,32},{4,36},{8,40},{12,44},{16,48},{20,52},{24,56},{28,60},{32,0... | collective-permute-start | bytes 442376 | tf_op jit(solution)/shard_map/ppermute | solution.py:216
  47.7 6.7 %collective-permute-start.4 = (f32[128,288]{0,1:T(8,128)S(1)}, f32[128,288]{0,1:T(8,128)S(1)}, u32[]{:S(2)}, u32[]{:S(2)}) collective-permute-start(f32[128,288]{0,1:T(8,128)S(1)} %add.79), channel_id=1, source_target_pairs={{0,64},{4,68},{8,72},{12,76},{16,80},{20,84},{24,88},{28,92},{32,9... | collective-permute-start | bytes 442376 | tf_op jit(solution)/shard_map/ppermute | solution.py:216

commit v14 on v12

--- a/solution.py
+++ b/solution.py
@@ -213,7 +213,7 @@
 
 def local(land_jac, pose_jac, segment, knot_frac, track_len, block_base, damping):
     num_blocks = block_base.shape[0]
-    grams = block_grams_kernel(land_jac, pose_jac, segment, knot_frac, track_len, num_blocks, 8)
+    grams = block_grams_kernel(land_jac, pose_jac, segment, knot_frac, track_len, num_blocks, 16)
     group_cols = damping.shape[0]
     num_groups = lax.axis_size("cols")
     band = place_band(skew_blocks(grams), block_base, group_cols, num_groups)

time: 83.1 us -> 83.1 us (level)
  no operation moved by 1% of the time
where the time goes in v14:
time: 83.1 us; the launch traced here: 82.8 us
  Pallas kernels  32.6 us (39%)
  waiting for transfers between devices  21.4 us (26%)
  blocking collectives  14.4 us (17%)
  local copies, waits for them, and re-layouts  8.16 us (10%)
  starting transfers between devices  5.1 us (6%)
  matrix products  0.88 us (1%)
    pallas_call x1, Pallas kernels, band_cholesky(): pl.pallas_call(functools.partial(band_chol_kernel, n, band_w), out_shape=...  24.6 us
    ppermute x5, waiting for transfers between devices, butterfly_sum(): band = band + lax.ppermute(band, axis, [(i, i ^ s) for i in range(n)])  21.4 us
    all_to_all x1, blocking collectives, scatter_sum(): got = lax.all_to_all(band, axis, 0, 0, tiled=True)  14.4 us
    pallas_call x1, Pallas kernels, block_grams_kernel(): pl.pallas_call(functools.partial(gram_kernel, ldim, pdim), out_shape=jax....  7.96 us
    ppermute x5, starting transfers between devices, butterfly_sum(): band = band + lax.ppermute(band, axis, [(i, i ^ s) for i in range(n)])  5.1 us
    reshape x1, local copies, waits for them, and re-layouts, local(): yt = yt.reshape(WIN_KNOTS * KDOF, group_cols)  2.77 us
  transfers between devices with their start and end apart: 5, of which 5 were waited for; matrix products, arithmetic and copies ran while one was open for 1% of the time, Pallas kernels for 0%

profile of v14, /device:TPU:38, one launch (start us, length us, event | category | flops | bytes accessed | tf_op | source)
XLA Modules:
  0.0 82.8 jit_solution(11100187036409018337)
XLA Ops:
  0.0 8.0 %shard_map.73 = f32[16,48,48]{2,1,0:T(8,128)} custom-call(f32[3,16,2048]{2,1,0:T(8,128)} %bitcast.32, f32[6,16,2048]{2,1,0:T(8,128)} %bitcast.31, s32[8,2048]{1,0:T(8,128)} %seg_ref.1, f32[8,2048]{1,0:T(8,128)} %frac_ref.1, s32[1,2048]{1,0:T(1,128)} %bitcast.33), custom_call_target="tpu_custom_call" | custom-call | tf_op jit(solution)/shard_map/pallas_call | solution.py:74
  8.0 1.4 %copy.10 = f32[16,48,48]{0,2,1:T(8,128)S(1)} copy(f32[16,48,48]{2,1,0:T(8,128)} %shard_map.73) | data formatting | bytes 294912 | tf_op jit(solution)/shard_map/pallas_call | solution.py:74
  9.4 0.5 convolution_bitcast_fusion
  9.8 0.9 %copy.12 = f32[16,8,8,6,6]{1,0,4,3,2:T(8,128)S(1)} copy(f32[16,8,8,6,6]{0,2,4,3,1:T(8,128)S(1)} %convolution_bitcast_fusion) | data formatting | bytes 294912 | tf_op jit(solution)/shard_map/bienf,ind->bidef/transpose | solution.py:97
  10.8 0.0 copy-start.1
  10.8 1.2 %reshape.74 = f32[128,288,1]{0,1,2:T(8,128)S(1)} reshape(f32[16,8,8,6,6]{1,0,4,3,2:T(8,128)S(1)} %copy.12) | data formatting | bytes 294912 | tf_op jit(solution)/shard_map/reshape | solution.py:108
  11.9 0.0 copy-done.1
  12.0 0.1 add.66
  12.0 0.1 add.67
  12.1 0.1 add.69
  12.2 0.4 fusion.1
  12.7 14.4 %all_to_all.6 = f32[4,128,288]{1,2,0:T(8,128)S(1)} all-to-all(f32[4,128,288]{1,2,0:T(8,128)S(1)} %fusion.1), channel_id=1, replica_groups=mesh['rows'=32,'cols'=4] {'cols'}, dimensions={0} | all-to-all | bytes 1179648 | tf_op jit(solution)/shard_map/all_to_all | solution.py:197
  27.1 0.0 copy-start
  27.2 0.1 collective-permute-start
  27.2 1.4 %collective-permute-done = f32[128,288]{0,1:T(8,128)S(1)} collective-permute-done((f32[128,288]{0,1:T(8,128)S(1)}, f32[128,288]{0,1:T(8,128)S(1)}, u32[]{:S(2)}, u32[]{:S(2)}) %collective-permute-start) | collective-permute-done | bytes 147488 | tf_op jit(solution)/shard_map/ppermute | solution.py:209
  28.6 0.2 collective-permute-start.1
  28.8 5.8 %collective-permute-done.1 = f32[128,288]{0,1:T(8,128)S(1)} collective-permute-done((f32[128,288]{0,1:T(8,128)S(1)}, f32[128,288]{0,1:T(8,128)S(1)}, u32[]{:S(2)}, u32[]{:S(2)}) %collective-permute-start.1) | collective-permute-done | bytes 147488 | tf_op jit(solution)/shard_map/ppermute | solution.py:209
  34.6 3.1 %collective-permute-start.2 = (f32[128,288]{0,1:T(8,128)S(1)}, f32[128,288]{0,1:T(8,128)S(1)}, u32[]{:S(2)}, u32[]{:S(2)}) collective-permute-start(f32[128,288]{0,1:T(8,128)S(1)} %add.77), channel_id=1, source_target_pairs={{0,16},{4,20},{8,24},{12,28},{16,0},{20,4},{24,8},{28,12},{32,48},... | collective-permute-start | bytes 442376 | tf_op jit(solution)/shard_map/ppermute | solution.py:209
  37.7 3.7 %collective-permute-done.2 = f32[128,288]{0,1:T(8,128)S(1)} collective-permute-done((f32[128,288]{0,1:T(8,128)S(1)}, f32[128,288]{0,1:T(8,128)S(1)}, u32[]{:S(2)}, u32[]{:S(2)}) %collective-permute-start.2) | collective-permute-done | bytes 147488 | tf_op jit(solution)/shard_map/ppermute | solution.py:209
  41.4 0.9 %collective-permute-start.3 = (f32[128,288]{0,1:T(8,128)S(1)}, f32[128,288]{0,1:T(8,128)S(1)}, u32[]{:S(2)}, u32[]{:S(2)}) collective-permute-start(f32[128,288]{0,1:T(8,128)S(1)} %add.78), channel_id=1, source_target_pairs={{0,32},{4,36},{8,40},{12,44},{16,48},{20,52},{24,56},{28,60},{32,0... | collective-permute-start | bytes 442376 | tf_op jit(solution)/shard_map/ppermute | solution.py:209
  42.3 5.1 %collective-permute-done.3 = f32[128,288]{0,1:T(8,128)S(1)} collective-permute-done((f32[128,288]{0,1:T(8,128)S(1)}, f32[128,288]{0,1:T(8,128)S(1)}, u32[]{:S(2)}, u32[]{:S(2)}) %collective-permute-start.3) | collective-permute-done | bytes 147488 | tf_op jit(solution)/shard_map/ppermute | solution.py:209
  47.5 0.8 %collective-permute-start.4 = (f32[128,288]{0,1:T(8,128)S(1)}, f32[128,288]{0,1:T(8,128)S(1)}, u32[]{:S(2)}, u32[]{:S(2)}) collective-permute-start(f32[128,288]{0,1:T(8,128)S(1)} %add.79), channel_id=1, source_target_pairs={{0,64},{4,68},{8,72},{12,76},{16,80},{20,84},{24,88},{28,92},{32,9... | collective-permute-start | bytes 442376 | tf_op jit(solution)/shard_map/ppermute | solution.py:209
  48.3 0.0 copy-done
  48.3 0.6 reshape.72.damp_ref
  48.9 5.5 %collective-permute-done.4 = f32[128,288]{0,1:T(8,128)S(1)} collective-permute-done((f32[128,288]{0,1:T(8,128)S(1)}, f32[128,288]{0,1:T(8,128)S(1)}, u32[]{:S(2)}, u32[]{:S(2)}) %collective-permute-start.4) | collective-permute-done | bytes 147488 | tf_op jit(solution)/shard_map/ppermute | solution.py:209
  54.4 1.1 %copy.13 = f32[8,6,128,6]{3,2,1,0:T(8,128)S(1)} copy(f32[8,6,128,6]{2,1,3,0:T(8,128)S(1)} %bitcast.30) | data formatting | bytes 294912 | tf_op jit(solution)/shard_map/transpose | solution.py:222
  55.5 2.8 %reshape.71.yt_ref = f32[48,768]{1,0:T(8,128)} reshape(f32[8,6,128,6]{3,2,1,0:T(8,128)S(1)} %copy.13) | data formatting | bytes 294912 | tf_op jit(solution)/shard_map/reshape | solution.py:223
  58.2 24.6 %shard_map.74 = f32[768,768]{1,0:T(8,128)} custom-call(f32[48,768]{1,0:T(8,128)} %reshape.71.yt_ref, f32[1,768]{1,0:T(1,128)} %reshape.72.damp_ref), custom_call_target="tpu_custom_call" | custom-call | tf_op jit(solution)/shard_map/pallas_call | solution.py:183
  (11 shorter events, 0.2 us)
Async XLA Ops:
  10.8 1.2 %copy-start.1 = (s32[16]{0:T(128)S(1)}, s32[16]{0:T(128)}, u32[]{:S(2)}) copy-start(s32[16]{0:T(128)} %param.12) | copy-start | bytes 196
  27.1 21.2 %copy-start = (f32[768]{0:T(1024)S(1)}, f32[768]{0:T(1024)}, u32[]{:S(2)}) copy-start(f32[768]{0:T(1024)} %param.13) | copy-start | bytes 9220
  27.2 1.5 %collective-permute-start = (f32[128,288]{0,1:T(8,128)S(1)}, f32[128,288]{0,1:T(8,128)S(1)}, u32[]{:S(2)}, u32[]{:S(2)}) collective-permute-start(f32[128,288]{0,1:T(8,128)S(1)} %fusion.3), channel_id=1, source_target_pairs={{0,4},{4,0},{8,12},{12,8},{16,20},{20,16},{24,28},{28,24},{32,36},... | collective-permute-start | bytes 442376 | tf_op jit(solution)/shard_map/ppermute | solution.py:209
  28.6 6.0 %collective-permute-start.1 = (f32[128,288]{0,1:T(8,128)S(1)}, f32[128,288]{0,1:T(8,128)S(1)}, u32[]{:S(2)}, u32[]{:S(2)}) collective-permute-start(f32[128,288]{0,1:T(8,128)S(1)} %fusion.10), channel_id=1, source_target_pairs={{0,8},{4,12},{8,0},{12,4},{16,24},{20,28},{24,16},{28,20},{32,40},... | collective-permute-start | bytes 442376 | tf_op jit(solution)/shard_map/ppermute | solution.py:209
  34.6 6.7 %collective-permute-start.2 = (f32[128,288]{0,1:T(8,128)S(1)}, f32[128,288]{0,1:T(8,128)S(1)}, u32[]{:S(2)}, u32[]{:S(2)}) collective-permute-start(f32[128,288]{0,1:T(8,128)S(1)} %add.77), channel_id=1, source_target_pairs={{0,16},{4,20},{8,24},{12,28},{16,0},{20,4},{24,8},{28,12},{32,48},... | collective-permute-start | bytes 442376 | tf_op jit(solution)/shard_map/ppermute | solution.py:209
  41.4 6.0 %collective-permute-start.3 = (f32[128,288]{0,1:T(8,128)S(1)}, f32[128,288]{0,1:T(8,128)S(1)}, u32[]{:S(2)}, u32[]{:S(2)}) collective-permute-start(f32[128,288]{0,1:T(8,128)S(1)} %add.78), channel_id=1, source_target_pairs={{0,32},{4,36},{8,40},{12,44},{16,48},{20,52},{24,56},{28,60},{32,0... | collective-permute-start | bytes 442376 | tf_op jit(solution)/shard_map/ppermute | solution.py:209
  47.5 6.9 %collective-permute-start.4 = (f32[128,288]{0,1:T(8,128)S(1)}, f32[128,288]{0,1:T(8,128)S(1)}, u32[]{:S(2)}, u32[]{:S(2)}) collective-permute-start(f32[128,288]{0,1:T(8,128)S(1)} %add.79), channel_id=1, source_target_pairs={{0,64},{4,68},{8,72},{12,76},{16,80},{20,84},{24,88},{28,92},{32,9... | collective-permute-start | bytes 442376 | tf_op jit(solution)/shard_map/ppermute | solution.py:209

commit v15 on v12

--- a/solution.py
+++ b/solution.py
@@ -94,7 +94,7 @@
     k2 = lax.broadcasted_iota(jnp.int32, (WIN_KNOTS, WIN_KNOTS, WIN_KNOTS), 1)
     d = lax.broadcasted_iota(jnp.int32, (WIN_KNOTS, WIN_KNOTS, WIN_KNOTS), 2)
     pick = (k2 == k1 + d).astype(jnp.float32)
-    return jnp.einsum("bienf,ind->bidef", g5, pick, precision=lax.Precision.HIGH)
+    return jnp.einsum("bienf,ind->bidfe", g5, pick, precision=lax.Precision.HIGH)
 
 
 def place_band(skewed, block_start, group_cols, num_groups):
@@ -219,7 +219,7 @@
     band = place_band(skew_blocks(grams), block_base, group_cols, num_groups)
     band_whole = butterfly_sum(scatter_sum(band, "cols"), "rows")
     group_knots = group_cols // KDOF
-    yt = band_whole.reshape(group_knots, WIN_KNOTS, KDOF, KDOF).transpose(1, 3, 0, 2)
+    yt = band_whole.reshape(group_knots, WIN_KNOTS * KDOF, KDOF).transpose(1, 0, 2)
     yt = yt.reshape(WIN_KNOTS * KDOF, group_cols)
     return band_cholesky(yt, damping, group_cols)
 

time: 83.1 us -> 80.4 us (0.968)
  local copies, waits for them, and re-layouts: 8.16 us -> 5.44 us
    reshape x1 -> x2, local copies, waits for them, and re-layouts: 2.77 us -> 0.85 us  [local(): yt = yt.reshape(WIN_KNOTS * KDOF, group_cols)]
where the time goes in v15:
time: 80.4 us; the launch traced here: 80.1 us
  Pallas kernels  32.6 us (41%)
  waiting for transfers between devices  21.8 us (27%)
  blocking collectives  14.4 us (18%)
  local copies, waits for them, and re-layouts  5.44 us (7%)
  starting transfers between devices  4.71 us (6%)
  matrix products  0.88 us (1%)
    pallas_call x1, Pallas kernels, band_cholesky(): pl.pallas_call(functools.partial(band_chol_kernel, n, band_w), out_shape=...  24.6 us
    ppermute x5, waiting for transfers between devices, butterfly_sum(): band = band + lax.ppermute(band, axis, [(i, i ^ s) for i in range(n)])  21.8 us
    all_to_all x1, blocking collectives, scatter_sum(): got = lax.all_to_all(band, axis, 0, 0, tiled=True)  14.4 us
    pallas_call x1, Pallas kernels, block_grams_kernel(): pl.pallas_call(functools.partial(gram_kernel, ldim, pdim), out_shape=jax....  7.97 us
    ppermute x5, starting transfers between devices, butterfly_sum(): band = band + lax.ppermute(band, axis, [(i, i ^ s) for i in range(n)])  4.71 us
  transfers between devices with their start and end apart: 5, of which 5 were waited for; matrix products, arithmetic and copies ran while one was open for 1% of the time, Pallas kernels for 0%

profile of v15, /device:TPU:38, one launch (start us, length us, event | category | flops | bytes accessed | tf_op | source)
XLA Modules:
  0.0 80.1 jit_solution(1945887321092970477)
XLA Ops:
  0.0 8.0 %shard_map.73 = f32[16,48,48]{2,1,0:T(8,128)} custom-call(f32[3,16,2048]{2,1,0:T(8,128)} %bitcast.32, f32[6,16,2048]{2,1,0:T(8,128)} %bitcast.30, s32[8,2048]{1,0:T(8,128)} %seg_ref.1, f32[8,2048]{1,0:T(8,128)} %frac_ref.1, s32[1,2048]{1,0:T(1,128)} %bitcast.33), custom_call_target="tpu_custom_call" | custom-call | tf_op jit(solution)/shard_map/pallas_call | solution.py:74
  8.0 1.4 %copy.10 = f32[16,48,48]{0,2,1:T(8,128)S(1)} copy(f32[16,48,48]{2,1,0:T(8,128)} %shard_map.73) | data formatting | bytes 294912 | tf_op jit(solution)/shard_map/pallas_call | solution.py:74
  9.4 0.5 convolution_bitcast_fusion
  9.8 0.9 %copy.12 = f32[16,8,8,6,6]{1,0,4,3,2:T(8,128)S(1)} copy(f32[16,8,8,6,6]{0,2,3,4,1:T(8,128)S(1)} %convolution_bitcast_fusion) | data formatting | bytes 294912 | tf_op jit(solution)/shard_map/bienf,ind->bidfe/transpose | solution.py:97
  10.8 0.0 copy-start.1
  10.8 1.2 %reshape.74 = f32[128,288,1]{0,1,2:T(8,128)S(1)} reshape(f32[16,8,8,6,6]{1,0,4,3,2:T(8,128)S(1)} %copy.12) | data formatting | bytes 294912 | tf_op jit(solution)/shard_map/reshape | solution.py:108
  11.9 0.0 copy-done.1
  12.0 0.1 add.66
  12.0 0.1 add.67
  12.1 0.1 add.69
  12.2 0.4 fusion.1
  12.7 14.4 %all_to_all.6 = f32[4,128,288]{1,2,0:T(8,128)S(1)} all-to-all(f32[4,128,288]{1,2,0:T(8,128)S(1)} %fusion.1), channel_id=1, replica_groups=mesh['rows'=32,'cols'=4] {'cols'}, dimensions={0} | all-to-all | bytes 1179648 | tf_op jit(solution)/shard_map/all_to_all | solution.py:197
  27.1 0.0 copy-start
  27.2 0.1 collective-permute-start
  27.2 1.4 %collective-permute-done = f32[128,288]{0,1:T(8,128)S(1)} collective-permute-done((f32[128,288]{0,1:T(8,128)S(1)}, f32[128,288]{0,1:T(8,128)S(1)}, u32[]{:S(2)}, u32[]{:S(2)}) %collective-permute-start) | collective-permute-done | bytes 147488 | tf_op jit(solution)/shard_map/ppermute | solution.py:209
  28.6 0.2 collective-permute-start.1
  28.8 5.8 %collective-permute-done.1 = f32[128,288]{0,1:T(8,128)S(1)} collective-permute-done((f32[128,288]{0,1:T(8,128)S(1)}, f32[128,288]{0,1:T(8,128)S(1)}, u32[]{:S(2)}, u32[]{:S(2)}) %collective-permute-start.1) | collective-permute-done | bytes 147488 | tf_op jit(solution)/shard_map/ppermute | solution.py:209
  34.6 3.1 %collective-permute-start.2 = (f32[128,288]{0,1:T(8,128)S(1)}, f32[128,288]{0,1:T(8,128)S(1)}, u32[]{:S(2)}, u32[]{:S(2)}) collective-permute-start(f32[128,288]{0,1:T(8,128)S(1)} %add.77), channel_id=1, source_target_pairs={{0,16},{4,20},{8,24},{12,28},{16,0},{20,4},{24,8},{28,12},{32,48},... | collective-permute-start | bytes 442376 | tf_op jit(solution)/shard_map/ppermute | solution.py:209
  37.7 3.7 %collective-permute-done.2 = f32[128,288]{0,1:T(8,128)S(1)} collective-permute-done((f32[128,288]{0,1:T(8,128)S(1)}, f32[128,288]{0,1:T(8,128)S(1)}, u32[]{:S(2)}, u32[]{:S(2)}) %collective-permute-start.2) | collective-permute-done | bytes 147488 | tf_op jit(solution)/shard_map/ppermute | solution.py:209
  41.4 0.9 %collective-permute-start.3 = (f32[128,288]{0,1:T(8,128)S(1)}, f32[128,288]{0,1:T(8,128)S(1)}, u32[]{:S(2)}, u32[]{:S(2)}) collective-permute-start(f32[128,288]{0,1:T(8,128)S(1)} %add.78), channel_id=1, source_target_pairs={{0,32},{4,36},{8,40},{12,44},{16,48},{20,52},{24,56},{28,60},{32,0... | collective-permute-start | bytes 442376 | tf_op jit(solution)/shard_map/ppermute | solution.py:209
  42.3 5.3 %collective-permute-done.3 = f32[128,288]{0,1:T(8,128)S(1)} collective-permute-done((f32[128,288]{0,1:T(8,128)S(1)}, f32[128,288]{0,1:T(8,128)S(1)}, u32[]{:S(2)}, u32[]{:S(2)}) %collective-permute-start.3) | collective-permute-done | bytes 147488 | tf_op jit(solution)/shard_map/ppermute | solution.py:209
  47.7 0.5 collective-permute-start.4
  48.1 0.0 copy-done
  48.1 0.6 reshape.72.damp_ref
  48.7 5.7 %collective-permute-done.4 = f32[128,288]{0,1:T(8,128)S(1)} collective-permute-done((f32[128,288]{0,1:T(8,128)S(1)}, f32[128,288]{0,1:T(8,128)S(1)}, u32[]{:S(2)}, u32[]{:S(2)}) %collective-permute-start.4) | collective-permute-done | bytes 147488 | tf_op jit(solution)/shard_map/ppermute | solution.py:209
  54.4 0.3 copy.13
  54.7 0.8 %copy.14.yt_ref = f32[48,768]{1,0:T(8,128)} copy(f32[48,768]{0,1:T(8,128)S(1)} %reshape.71) | data formatting | bytes 294912 | tf_op jit(solution)/shard_map/reshape | solution.py:223
  55.5 24.6 %shard_map.74 = f32[768,768]{1,0:T(8,128)} custom-call(f32[48,768]{1,0:T(8,128)} %copy.14.yt_ref, f32[1,768]{1,0:T(1,128)} %reshape.72.damp_ref), custom_call_target="tpu_custom_call" | custom-call | tf_op jit(solution)/shard_map/pallas_call | solution.py:183
  (12 shorter events, 0.2 us)
Async XLA Ops:
  10.8 1.2 %copy-start.1 = (s32[16]{0:T(128)S(1)}, s32[16]{0:T(128)}, u32[]{:S(2)}) copy-start(s32[16]{0:T(128)} %param.12) | copy-start | bytes 196
  27.1 21.0 %copy-start = (f32[768]{0:T(1024)S(1)}, f32[768]{0:T(1024)}, u32[]{:S(2)}) copy-start(f32[768]{0:T(1024)} %param.13) | copy-start | bytes 9220
  27.2 1.5 %collective-permute-start = (f32[128,288]{0,1:T(8,128)S(1)}, f32[128,288]{0,1:T(8,128)S(1)}, u32[]{:S(2)}, u32[]{:S(2)}) collective-permute-start(f32[128,288]{0,1:T(8,128)S(1)} %fusion.3), channel_id=1, source_target_pairs={{0,4},{4,0},{8,12},{12,8},{16,20},{20,16},{24,28},{28,24},{32,36},... | collective-permute-start | bytes 442376 | tf_op jit(solution)/shard_map/ppermute | solution.py:209
  28.6 6.0 %collective-permute-start.1 = (f32[128,288]{0,1:T(8,128)S(1)}, f32[128,288]{0,1:T(8,128)S(1)}, u32[]{:S(2)}, u32[]{:S(2)}) collective-permute-start(f32[128,288]{0,1:T(8,128)S(1)} %fusion.10), channel_id=1, source_target_pairs={{0,8},{4,12},{8,0},{12,4},{16,24},{20,28},{24,16},{28,20},{32,40},... | collective-permute-start | bytes 442376 | tf_op jit(solution)/shard_map/ppermute | solution.py:209
  34.6 6.7 %collective-permute-start.2 = (f32[128,288]{0,1:T(8,128)S(1)}, f32[128,288]{0,1:T(8,128)S(1)}, u32[]{:S(2)}, u32[]{:S(2)}) collective-permute-start(f32[128,288]{0,1:T(8,128)S(1)} %add.77), channel_id=1, source_target_pairs={{0,16},{4,20},{8,24},{12,28},{16,0},{20,4},{24,8},{28,12},{32,48},... | collective-permute-start | bytes 442376 | tf_op jit(solution)/shard_map/ppermute | solution.py:209
  41.4 6.2 %collective-permute-start.3 = (f32[128,288]{0,1:T(8,128)S(1)}, f32[128,288]{0,1:T(8,128)S(1)}, u32[]{:S(2)}, u32[]{:S(2)}) collective-permute-start(f32[128,288]{0,1:T(8,128)S(1)} %add.78), channel_id=1, source_target_pairs={{0,32},{4,36},{8,40},{12,44},{16,48},{20,52},{24,56},{28,60},{32,0... | collective-permute-start | bytes 442376 | tf_op jit(solution)/shard_map/ppermute | solution.py:209
  47.7 6.7 %collective-permute-start.4 = (f32[128,288]{0,1:T(8,128)S(1)}, f32[128,288]{0,1:T(8,128)S(1)}, u32[]{:S(2)}, u32[]{:S(2)}) collective-permute-start(f32[128,288]{0,1:T(8,128)S(1)} %add.79), channel_id=1, source_target_pairs={{0,64},{4,68},{8,72},{12,76},{16,80},{20,84},{24,88},{28,92},{32,9... | collective-permute-start | bytes 442376 | tf_op jit(solution)/shard_map/ppermute | solution.py:209
